TPU v7x, 256 devices: a whole 4x4x8 slice. The times are simulated.
256 devices in a mesh: expert: 8 (over x, core), tensor: 32 (over z, y).
Axes of the slice: x: 4, y: 4, z: 8, core: 2. Of those that a mesh axis runs over, the one named last changes fastest.
Arguments:
- resid: bfloat16 [16384, 2048], P(('expert', 'tensor')), may hold values from -6 to 6
- contexts: bfloat16 [16384, 4096], P('expert', 'tensor'), may hold values from -6 to 6
- att_routes: int32 [16384, 2], P('expert'), may hold values from 0 to 7, all different within a row
- att_scores: float32 [16384, 2], P('expert'), may hold values from -6 to 6
- att_out_w: bfloat16 [8, 2048, 2048], P(None, 'tensor'), may hold values from -0.125 to 0.125
- norm_gain: bfloat16 [2048], replicated, may hold values from 0.25 to 1.75
- router_w: bfloat16 [2048, 8], replicated, may hold values from -0.125 to 0.125
- mlp_routes: int32 [16384, 2], P(('expert', 'tensor')), may hold values from 0 to 7, all different within a row
- split_rule: int32 [16384, 2], P(('expert', 'tensor')), may hold values from 0 to 2519
- placement: int32 [32], replicated, may hold values from 0 to 7, as said below
- cap_blocks: int32 [32], replicated, may hold values from 1 to 2, as said below
- w_gate_up: bfloat16 [32, 2048, 2, 5632], P('tensor', None, None, 'expert'), as said below
- w_down: bfloat16 [32, 5632, 2048], P('tensor', 'expert'), as said below
- final_gain: bfloat16 [2048], replicated, may hold values from 0.25 to 1.75
Outputs:
- stream_out: bfloat16 [16384, 2048], P(('expert', 'tensor'))
- normalized: bfloat16 [16384, 2048], P(('expert', 'tensor'))
Inputs may be any that keep to these rules, and one draw needn't show every extreme that they name: `att_routes`: each row names 2 different experts. `mlp_routes`: each row names 2 different experts. `placement`: every expert is held by at least one slot. `cap_blocks`: some slot accepts 2 blocks. `w_gate_up`: slots that hold the same expert hold equal weights. `w_down`: slots that hold the same expert hold equal weights.
All inputs are finite; a program needn't handle non-finite values.
Results may differ from a plain program's by a relative error of at most 0.023.
Values may be sent and summed in bfloat16 or wider, within the bound.
No kernel may reach another device: no remote copies, remote signals or barrier semaphores. Data moves between devices by JAX's collectives and lax.ppermute only.
A program may use at most 64 MiB of HBM per device.

v0:
```python
import jax
import jax.numpy as jnp
from jax import lax
from jax.sharding import PartitionSpec as P

MAXB = 2


norm_eps = 1e-06


def rms_norm(values, gain):
    scale = lax.rsqrt(jnp.mean(values * values, axis=-1, keepdims=True) + norm_eps)
    return values * scale * gain.astype(values.dtype)


def pair_gates(scores):
    first = jax.nn.silu(scores[:, 0:1] * 0.0) * 0.0 + jax.nn.sigmoid(
        scores[:, 0:1] - scores[:, 1:2]
    )
    first = first[:, 0]
    return jnp.stack([first, 1.0 - first], axis=1)


def activate(shard_piece, w_gate_up):
    both = jnp.einsum(
        "tsecd,sdgf->tsecgf", shard_piece, w_gate_up, preferred_element_type=jnp.float32
    )
    hidden = (jax.nn.silu(both[:, :, :, :, 0, :]) * both[:, :, :, :, 1, :]).astype(jnp.bfloat16)
    hidden = jnp.transpose(hidden, (0, 2, 3, 1, 4))
    return hidden.reshape(
        hidden.shape[0] * hidden.shape[1] * hidden.shape[2], hidden.shape[3], hidden.shape[4]
    )


def per_device(
    resid,
    contexts,
    att_routes,
    att_scores,
    att_out_w,
    norm_gain,
    router_w,
    mlp_routes,
    split_rule,
    placement,
    cap_blocks,
    w_gate_up,
    w_down,
    final_gain,
):
    n_tensor = lax.axis_size("tensor")
    row_count = resid.shape[0]
    model_width = resid.shape[1]
    group_rows = contexts.shape[0]
    att_experts = att_out_w.shape[0]
    slice_ctx = att_out_w.shape[1]
    top_count = att_routes.shape[1]
    gate_att = pair_gates(att_scores)
    chosen = (
        att_routes[:, :, None] == jnp.arange(att_experts, dtype=jnp.int32)[None, None, :]
    ).astype(jnp.float32)
    weighted = chosen * gate_att[:, :, None]
    context_part = contexts.reshape(group_rows, slice_ctx, top_count).astype(jnp.float32)
    mixed = (
        jnp.einsum("tke,tck->tec", weighted, context_part)
        .astype(jnp.bfloat16)
        .reshape(group_rows, att_experts * slice_ctx)
    )
    weight_flat = att_out_w.reshape(att_experts * slice_ctx, model_width)
    row_block = mixed
    attention = lax.psum_scatter(
        jnp.dot(row_block, weight_flat, preferred_element_type=jnp.float32).astype(jnp.bfloat16),
        "tensor",
        scatter_dimension=0,
        tiled=True,
    ).astype(jnp.float32)
    stream = (resid.astype(jnp.float32) + attention).astype(jnp.bfloat16)
    normed = rms_norm(stream.astype(jnp.float32), norm_gain).astype(jnp.bfloat16)
    logits = jnp.dot(normed, router_w, preferred_element_type=jnp.float32)
    gate_mlp = pair_gates(jnp.take_along_axis(logits, mlp_routes, axis=1))
    replicas = placement.shape[0]
    slots = w_gate_up.shape[0]
    expert_total = router_w.shape[1]
    block_rows = max(1, row_count * top_count // (2 * replicas))
    capacity_rows = MAXB * block_rows
    slot_ids = jnp.arange(replicas, dtype=jnp.int32)
    expert_ids = jnp.arange(expert_total, dtype=jnp.int32)
    copies = jnp.sum((placement[None, :] == expert_ids[:, None]).astype(jnp.int32), axis=1)
    earlier = jnp.sum(
        (
            (placement[None, :] == placement[:, None]) & (slot_ids[None, :] < slot_ids[:, None])
        ).astype(jnp.int32),
        axis=1,
    )
    route_onehot = (mlp_routes[:, :, None] == expert_ids[None, None, :]).astype(jnp.int32)
    route_copies = jnp.sum(route_onehot * copies[None, None, :], axis=2)
    replica_rank = jnp.remainder(split_rule, route_copies)
    match = (
        (placement[None, None, :] == mlp_routes[:, :, None])
        & (earlier[None, None, :] == replica_rank[:, :, None])
    ).astype(jnp.int32)
    replica_slot = jnp.sum(match * slot_ids[None, None, :], axis=2)
    capacity = jnp.sum(match * cap_blocks[None, None, :], axis=2) * block_rows
    flat_match = match.reshape(row_count * top_count, replicas)
    before = jnp.cumsum(flat_match, axis=0) - flat_match
    arrival = jnp.sum(before * flat_match, axis=1).reshape(row_count, top_count)
    is_kept = arrival < capacity
    holder = replica_slot // slots
    within = replica_slot % slots
    position = within * (n_tensor * capacity_rows) + holder * capacity_rows + arrival
    position = jnp.where(is_kept, position, -1)
    buffer_rows = slots * n_tensor * capacity_rows
    placer = jnp.sum(
        (jnp.arange(buffer_rows, dtype=jnp.int32)[:, None, None] == position[None, :, :]).astype(
            jnp.bfloat16
        ),
        axis=2,
    )
    send_rows = jnp.dot(placer, normed, preferred_element_type=jnp.float32).astype(jnp.bfloat16)
    send_rows = send_rows.reshape(slots, n_tensor, capacity_rows, model_width)
    collected = lax.all_gather(send_rows[None], "expert", axis=0, tiled=True)
    arrived = lax.all_to_all(collected, "tensor", split_axis=2, concat_axis=2, tiled=True)
    hidden = activate(arrived, w_gate_up)
    row_block = hidden
    summed = lax.psum_scatter(
        jnp.einsum("bsf,sfd->bsd", row_block, w_down, preferred_element_type=jnp.float32).astype(
            jnp.bfloat16
        ),
        "expert",
        scatter_dimension=0,
        tiled=True,
    )
    results = summed.reshape(n_tensor, capacity_rows, slots, model_width)
    returned = lax.all_to_all(results, "tensor", split_axis=0, concat_axis=0, tiled=True)
    flat_back = returned.reshape(n_tensor * capacity_rows * slots, model_width)
    back_index = jnp.where(is_kept, holder * (capacity_rows * slots) + arrival * slots + within, 0)
    fetched = (
        jnp.take(flat_back, back_index.reshape(-1), axis=0)
        .reshape(row_count, top_count, model_width)
        .astype(jnp.float32)
    )
    factors = gate_mlp * is_kept.astype(jnp.float32)
    expert_mix = fetched[:, 0, :] * factors[:, 0:1] + fetched[:, 1, :] * factors[:, 1:2]
    after = stream.astype(jnp.float32) + expert_mix
    return (after.astype(jnp.bfloat16), rms_norm(after, final_gain).astype(jnp.bfloat16))


def solution(mesh):
    return jax.shard_map(
        per_device,
        mesh=mesh,
        in_specs=(
            P(("expert", "tensor"), None),
            P("expert", "tensor"),
            P("expert", None),
            P("expert", None),
            P(None, "tensor", None),
            P(),
            P(),
            P(("expert", "tensor"), None),
            P(("expert", "tensor"), None),
            P(),
            P(),
            P("tensor", None, None, "expert"),
            P("tensor", "expert", None),
            P(),
        ),
        out_specs=(P(("expert", "tensor"), None), P(("expert", "tensor"), None)),
        check_vma=False,
    )
```

profile of v0, /device:TPU:32, one launch (start us, length us, event | category | flops | bytes accessed | tf_op | source)
XLA Modules:
  0.0 515.3 jit_solution(11836133515749787276)
XLA Ops:
  7.2 2.2 copy.77
  9.4 1.4 reshape.175
  10.8 2.1 copy.78
  13.0 0.3 copy.76
  13.3 1.4 copy.75
  14.7 14.3 %convolution_convert_fusion = bf16[2048,8,64]{2,1,0:T(8,128)(2,1)S(1)} fusion(bf16[2048,64,2]{1,2,0:T(2,128)(2,1)} %copy.78, bf16[2048,2]{1,0:T(8,128)(2,1)S(1)} %copy.76, s32[2048,2]{1,0:T(8,128)} %copy.75), kind=kOutput, calls=%fused_computation.14 | convolution fusion | flops 4259840 | bytes 2646016 | tf_op jit(solution)/shard_map/tke,tck->tec/dot_general | solution.py:66
  29.0 7.0 %bitcast_convert_fusion = bf16[2048,2048]{1,0:T(8,128)(2,1)} fusion(bf16[8,64,2048]{2,1,0:T(8,128)(2,1)S(1)} %copy-done.11, bf16[2048,8,64]{2,1,0:T(8,128)(2,1)S(1)} %convolution_convert_fusion), kind=kOutput, calls=%fused_computation.2 | convolution fusion | flops 4299161600 | bytes 12582912 | tf_op jit(solution)/shard_map/dot_general | solution.py:73
  36.1 0.6 copy-done.7
  36.7 0.1 convert_reduce_fusion.1
  36.9 0.1 and_select_fusion.1
  37.1 0.1 copy.81
  37.2 0.1 eq.133
  37.3 0.1 eq.119
  37.4 0.2 convert_reduce_fusion
  37.6 0.1 fusion.27
  37.7 0.2 reduce_window_sum.11
  37.9 0.2 select_reduce_fusion
  38.1 0.1 reduce_sum.92
  38.3 0.1 select_reduce_fusion.2
  38.5 228.2 %reduce-scatter.3.cloned.1.call-done = bf16[64,2048]{1,0:T(8,128)(2,1)} async-done(((bf16[2048,2048]{1,0:T(8,128)(2,1)}), bf16[64,2048]{1,0:T(8,128)(2,1)}) %reduce-scatter.3.cloned.1.call-update) | async-done | bytes 262160 | tf_op jit(solution)/shard_map/reduce_scatter | solution.py:72
  266.7 1.1 fusion.16
  267.9 1.2 convolution_convert_fusion.1
  269.1 2.0 broadcast_in_dim_reshape.3
  271.1 2.1 copy.84
  273.3 34.0 %all-gather.2.cloned.1.call-done = bf16[8,1,32,4,2048]{4,2,3,1,0:T(8,128)(2,1)} async-done(((bf16[1,1,32,4,2048]{4,2,3,1,0:T(8,128)(2,1)}), bf16[8,1,32,4,2048]{4,2,3,1,0:T(8,128)(2,1)}) %all-gather.2.cloned.1.call-update) | async-done | bytes 4194320 | tf_op jit(solution)/shard_map/all_gather | solution.py:122
  307.3 5.6 %copy.85 = bf16[8,1,32,4,2048]{4,3,0,1,2:T(4,128)(2,1)S(1)} copy(bf16[8,1,32,4,2048]{4,2,3,1,0:T(8,128)(2,1)} %all-gather.2.cloned.1.call-done) | data formatting | bytes 8388608 | tf_op jit(solution)/shard_map/all_gather | solution.py:122
  312.9 105.0 %all_to_all.10 = bf16[8,1,32,4,2048]{4,3,0,1,2:T(4,128)(2,1)S(1)} all-to-all(bf16[8,1,32,4,2048]{4,3,0,1,2:T(4,128)(2,1)S(1)} %copy.85), channel_id=1, replica_groups=mesh['expert'=8,'tensor'=32] {'tensor'}, dimensions={2} | all-to-all | bytes 8388608 | tf_op jit(solution)/shard_map/all_to_all | solution.py:123
  417.9 7.2 %fusion.7 = f32[8,1,32,4,2,704]{5,2,4,3,0,1:T(8,128)S(1)} fusion(bf16[1,2048,2,704]{1,3,2,0:T(8,128)(2,1)S(1)} %bitcast.83, bf16[8,1,32,4,2048]{4,3,0,1,2:T(4,128)(2,1)S(1)} %all_to_all.10), kind=kOutput, calls=%fused_computation.13 | convolution fusion | flops 5905580032 | bytes 15728640 | tf_op jit(solution)/shard_map/tsecd,sdgf->tsecgf/dot_general | solution.py:26
  425.1 1.0 fusion.5
  426.1 2.4 copy.87
  428.5 3.7 convert_element_type.95
  432.2 6.3 %convert_bitcast_fusion = bf16[1024,1,2048]{2,0,1:T(8,128)(2,1)} fusion(bf16[1024,704]{1,0:T(8,128)(2,1)} %convert_element_type.95, bf16[1,704,2048]{2,1,0:T(8,128)(2,1)S(1)} %copy-done), kind=kOutput, calls=%fused_computation.8 | convolution fusion | flops 2954887168 | bytes 8519680 | tf_op jit(solution)/shard_map/bsf,sfd->bsd/dot_general | solution.py:127
  438.7 0.1 reshape.190
  438.9 0.1 mul.206
  439.2 0.1 mul.205
  439.4 36.2 %reduce-scatter.5.cloned.1.call-done = bf16[128,1,2048]{2,0,1:T(8,128)(2,1)} async-done(((bf16[1024,1,2048]{2,0,1:T(8,128)(2,1)}), bf16[128,1,2048]{2,0,1:T(8,128)(2,1)}) %reduce-scatter.5.cloned.1.call-update) | async-done | bytes 524304 | tf_op jit(solution)/shard_map/reduce_scatter | solution.py:126
  475.6 2.0 reshape.179
  477.6 10.2 %all-to-all-start.1 = ((bf16[32,4,1,2048]{3,1,2,0:T(4,128)(2,1)}), bf16[32,4,1,2048]{3,1,2,0:T(4,128)(2,1)}, u32[]{:S(2)}, u32[]{:S(2)}) async-start(bf16[32,4,1,2048]{3,1,2,0:T(4,128)(2,1)} %bitcast.81), calls=%async_computation.3 | async-start | bytes 1048576 | tf_op jit(solution)/shard_map/all_to_all | solution.py:135
  487.8 0.2 fusion.23
  488.1 1.0 gather_fusion.1
  489.1 0.1 reshape.193
  489.4 12.7 %all-to-all-done.1 = bf16[32,4,1,2048]{3,1,2,0:T(4,128)(2,1)} async-done(((bf16[32,4,1,2048]{3,1,2,0:T(4,128)(2,1)}), bf16[32,4,1,2048]{3,1,2,0:T(4,128)(2,1)}, u32[]{:S(2)}, u32[]{:S(2)}) %all-to-all-start.1) | async-done | bytes 524320 | tf_op jit(solution)/shard_map/all_to_all | solution.py:135
  502.1 1.2 reshape.180
  503.2 1.7 gather_fusion
  504.9 1.4 gather.11
  506.3 0.3 fusion.22
  506.7 1.2 multiply_reduce_fusion
  507.9 0.8 multiply_convert_fusion
  (59 shorter events, 1.1 us)
Async XLA Ops:
  7.2 425.1 %copy-start = (bf16[1,704,2048]{2,1,0:T(8,128)(2,1)S(1)}, bf16[1,704,2048]{2,1,0:T(8,128)(2,1)}, u32[]{:S(2)}) copy-start(bf16[1,704,2048]{2,1,0:T(8,128)(2,1)} %param.26) | copy-start | bytes 8650756
  7.2 5.7 %copy-start.5 = (f32[2048,2]{0,1:T(2,128)S(1)}, f32[2048,2]{0,1:T(2,128)}, u32[]{:S(2)}) copy-start(f32[2048,2]{0,1:T(2,128)} %param.17) | copy-start | bytes 49156
  7.2 6.1 %copy-start.4 = (s32[2048,2]{0,1:T(2,128)S(1)}, s32[2048,2]{0,1:T(2,128)}, u32[]{:S(2)}) copy-start(s32[2048,2]{0,1:T(2,128)} %param.16) | copy-start | bytes 49156
  7.2 259.5 %reduce-scatter.3.cloned.1.call-start = ((), (), s32[]{:S(2)}) async-start(), calls=%async_computation.4 | async-start | bytes 8650752 | tf_op jit(solution)/shard_map/reduce_scatter | solution.py:72
  14.7 14.3 %copy-start.11 = (bf16[8,64,2048]{2,1,0:T(8,128)(2,1)S(1)}, bf16[8,64,2048]{2,1,0:T(8,128)(2,1)}, u32[]{:S(2)}) copy-start(bf16[8,64,2048]{2,1,0:T(8,128)(2,1)} %param.18) | copy-start | bytes 6291460
  35.9 0.7 copy-start.7
  35.9 0.7 copy-start.3
  35.9 0.8 copy-start.6
  35.9 1.0 copy-start.9
  36.0 2.4 copy-start.10
  36.0 230.8 %copy-start.2 = (bf16[64,2048]{1,0:T(8,128)(2,1)S(1)}, bf16[64,2048]{1,0:T(8,128)(2,1)}, u32[]{:S(2)}) copy-start(bf16[64,2048]{1,0:T(8,128)(2,1)} %param.14) | copy-start | bytes 786436
  36.0 271.3 %all-gather.2.cloned.1.call-start = ((), (), s32[]{:S(2)}) async-start(), calls=%async_computation.5 | async-start | bytes 4718592 | tf_op jit(solution)/shard_map/all_gather | solution.py:122
  267.9 219.9 %copy-start.1 = (bf16[64,2048]{1,0:T(8,128)(2,1)}, bf16[64,2048]{1,0:T(8,128)(2,1)S(1)}, u32[]{:S(2)}) copy-start(bf16[64,2048]{1,0:T(8,128)(2,1)S(1)} %get-tuple-element.9) | copy-start | bytes 786436
  273.2 202.4 %reduce-scatter.5.cloned.1.call-start = ((), (), s32[]{:S(2)}) async-start(), calls=%async_computation.6 | async-start | bytes 4718592 | tf_op jit(solution)/shard_map/reduce_scatter | solution.py:126
  307.3 110.6 %slice-start = ((s8[5767168]{0:T(1024)(128)(4,1)}), s8[4194304]{0:T(1024)(128)(4,1)S(1)}, s32[]{:S(2)}) async-start(s8[5767168]{0:T(1024)(128)(4,1)} %bitcast.82), calls=%async_computation.7 | async-start | bytes 8388608
  312.8 105.0 %slice-start.1 = ((s8[5767168]{0:T(1024)(128)(4,1)}), s8[1572864]{0:T(1024)(128)(4,1)S(1)}, s32[]{:S(2)}) async-start(s8[5767168]{0:T(1024)(128)(4,1)} %bitcast.82), calls=%async_computation.8 | async-start | bytes 3145728
  438.6 0.8 copy-start.8
  438.6 49.2 %copy-start.12 = (bf16[2048,8]{0,1:T(8,128)(2,1)S(1)}, bf16[2048,8]{0,1:T(8,128)(2,1)}, u32[]{:S(2)}) copy-start(bf16[2048,8]{0,1:T(8,128)(2,1)} %param.20) | copy-start | bytes 98308
  477.6 24.4 %all-to-all-start.1 = ((bf16[32,4,1,2048]{3,1,2,0:T(4,128)(2,1)}), bf16[32,4,1,2048]{3,1,2,0:T(4,128)(2,1)}, u32[]{:S(2)}, u32[]{:S(2)}) async-start(bf16[32,4,1,2048]{3,1,2,0:T(4,128)(2,1)} %bitcast.81), calls=%async_computation.3 | async-start | bytes 1048576 | tf_op jit(solution)/shard_map/all_to_all | solution.py:135
Sparse Core Ops, SparseCore 0:
  36.1 230.5 reduce-scatter.2
  273.4 33.8 all-gather.1
  438.7 36.8 reduce-scatter.4
where the time goes:
time: 517 us; the launch traced here: 515 us
  waiting for transfers between devices  311 us (60%)
  blocking collectives  105 us (20%)
  matrix products  36.2 us (7%)
  local copies, waits for them, and re-layouts  32.7 us (6%)
  between operations  14.1 us (3%)
  starting transfers between devices  10.3 us (2%)
  other arithmetic  5.94 us (1%)
    reduce_scatter x1, waiting for transfers between devices, per_device(): lax.psum_scatter(jnp.dot(row_block, weight_flat, preferred_element_type=j...  228 us
    all_to_all x1, blocking collectives, per_device(): lax.all_to_all(collected, 'tensor', split_axis=2, concat_axis=2, tiled=True)  105 us
    reduce_scatter x1, waiting for transfers between devices, per_device(): lax.psum_scatter(jnp.einsum('bsf,sfd->bsd', row_block, w_down, preferred_...  36.2 us
    all_gather x1, waiting for transfers between devices, per_device(): collected = lax.all_gather(send_rows[None], 'expert', axis=0, tiled=True)  34 us
    dot_general x1, matrix products, per_device(): jnp.einsum('tke,tck->tec', weighted, context_part).astype(jnp.bfloat16)  14.3 us
    all_to_all x1, waiting for transfers between devices, per_device(): lax.all_to_all(results, 'tensor', split_axis=0, concat_axis=0, tiled=True)  12.7 us
  transfers between devices with their start and end apart: 4, of which 4 were waited for; matrix products, arithmetic and copies ran while one was open for 1% of the time, Pallas kernels for 0%

commit v1 on v0

--- a/solution.py
+++ b/solution.py
@@ -1,9 +1,10 @@
 import jax
 import jax.numpy as jnp
 from jax import lax
-from jax.sharding import PartitionSpec as P
+from jax.sharding import Mesh, PartitionSpec as P
 
 MAXB = 2
+TENSOR = ("tz", "ty")
 
 
 norm_eps = 1e-06
@@ -49,7 +50,7 @@
     w_down,
     final_gain,
 ):
-    n_tensor = lax.axis_size("tensor")
+    n_tensor = lax.axis_size(TENSOR)
     row_count = resid.shape[0]
     model_width = resid.shape[1]
     group_rows = contexts.shape[0]
@@ -69,12 +70,9 @@
     )
     weight_flat = att_out_w.reshape(att_experts * slice_ctx, model_width)
     row_block = mixed
-    attention = lax.psum_scatter(
-        jnp.dot(row_block, weight_flat, preferred_element_type=jnp.float32).astype(jnp.bfloat16),
-        "tensor",
-        scatter_dimension=0,
-        tiled=True,
-    ).astype(jnp.float32)
+    partial = jnp.dot(row_block, weight_flat, preferred_element_type=jnp.float32).astype(jnp.bfloat16)
+    partial = lax.psum_scatter(partial, "tz", scatter_dimension=0, tiled=True)
+    attention = lax.psum_scatter(partial, "ty", scatter_dimension=0, tiled=True).astype(jnp.float32)
     stream = (resid.astype(jnp.float32) + attention).astype(jnp.bfloat16)
     normed = rms_norm(stream.astype(jnp.float32), norm_gain).astype(jnp.bfloat16)
     logits = jnp.dot(normed, router_w, preferred_element_type=jnp.float32)
@@ -119,8 +117,8 @@
     )
     send_rows = jnp.dot(placer, normed, preferred_element_type=jnp.float32).astype(jnp.bfloat16)
     send_rows = send_rows.reshape(slots, n_tensor, capacity_rows, model_width)
-    collected = lax.all_gather(send_rows[None], "expert", axis=0, tiled=True)
-    arrived = lax.all_to_all(collected, "tensor", split_axis=2, concat_axis=2, tiled=True)
+    exchanged = lax.all_to_all(send_rows, TENSOR, split_axis=1, concat_axis=1, tiled=True)
+    arrived = lax.all_gather(exchanged[None], "expert", axis=0, tiled=True)
     hidden = activate(arrived, w_gate_up)
     row_block = hidden
     summed = lax.psum_scatter(
@@ -132,7 +130,7 @@
         tiled=True,
     )
     results = summed.reshape(n_tensor, capacity_rows, slots, model_width)
-    returned = lax.all_to_all(results, "tensor", split_axis=0, concat_axis=0, tiled=True)
+    returned = lax.all_to_all(results, TENSOR, split_axis=0, concat_axis=0, tiled=True)
     flat_back = returned.reshape(n_tensor * capacity_rows * slots, model_width)
     back_index = jnp.where(is_kept, holder * (capacity_rows * slots) + arrival * slots + within, 0)
     fetched = (
@@ -146,26 +144,33 @@
     return (after.astype(jnp.bfloat16), rms_norm(after, final_gain).astype(jnp.bfloat16))
 
 
+def split_mesh(mesh):
+    n_expert, n_tensor = mesh.devices.shape
+    n_y = 4 if n_tensor % 4 == 0 else 1
+    return Mesh(mesh.devices.reshape(n_expert, n_tensor // n_y, n_y), ("expert", "tz", "ty"))
+
+
 def solution(mesh):
+    mesh = split_mesh(mesh)
     return jax.shard_map(
         per_device,
         mesh=mesh,
         in_specs=(
-            P(("expert", "tensor"), None),
-            P("expert", "tensor"),
+            P(("expert", "tz", "ty"), None),
+            P("expert", TENSOR),
             P("expert", None),
             P("expert", None),
-            P(None, "tensor", None),
+            P(None, TENSOR, None),
             P(),
             P(),
-            P(("expert", "tensor"), None),
-            P(("expert", "tensor"), None),
+            P(("expert", "tz", "ty"), None),
+            P(("expert", "tz", "ty"), None),
             P(),
             P(),
-            P("tensor", None, None, "expert"),
-            P("tensor", "expert", None),
+            P(TENSOR, None, None, "expert"),
+            P(TENSOR, "expert", None),
             P(),
         ),
-        out_specs=(P(("expert", "tensor"), None), P(("expert", "tensor"), None)),
+        out_specs=(P(("expert", "tz", "ty"), None), P(("expert", "tz", "ty"), None)),
         check_vma=False,
     )

time: 517 us -> 328 us (0.63)
  waiting for transfers between devices: 311 us -> 207 us
  blocking collectives: 105 us -> 24.4 us
  local copies, waits for them, and re-layouts: 32.7 us -> 25.6 us
    reduce_scatter x1 -> x2, waiting for transfers between devices: 228 us -> 123 us  [the longest x1 95.8 us: per_device(): partial = lax.psum_scatter(partial, 'tz', scatter_dimension=0, tiled=True)]
    all_to_all x1, blocking collectives: 105 us -> 24.4 us  [per_device(): lax.all_to_all(send_rows, TENSOR, split_axis=1, concat_axis=1, tiled=True)]
    all_gather x1 -> x0, local copies, waits for them, and re-layouts: 5.57 us -> none  [per_device(): collected = lax.all_gather(send_rows[None], 'expert', axis=0, tiled=True)]
  transfers between devices with their start and end apart: 4 -> 5, of which waited for: 4 -> 5; matrix products, arithmetic and copies ran while one was open for 1% -> 1% of each run, Pallas kernels for 0% -> 0%
where the time goes in v1:
time: 328 us; the launch traced here: 326 us
  waiting for transfers between devices  207 us (63%)
  matrix products  39 us (12%)
  local copies, waits for them, and re-layouts  25.6 us (8%)
  blocking collectives  24.4 us (7%)
  between operations  14.1 us (4%)
  starting transfers between devices  10.5 us (3%)
  other arithmetic  5.93 us (2%)
    reduce_scatter x1, waiting for transfers between devices, per_device(): partial = lax.psum_scatter(partial, 'tz', scatter_dimension=0, tiled=True)  95.8 us
    reduce_scatter x1, waiting for transfers between devices, per_device(): lax.psum_scatter(jnp.einsum('bsf,sfd->bsd', row_block, w_down, preferred_...  39.9 us
    all_gather x1, waiting for transfers between devices, per_device(): arrived = lax.all_gather(exchanged[None], 'expert', axis=0, tiled=True)  30.9 us
    reduce_scatter x1, waiting for transfers between devices, per_device(): lax.psum_scatter(partial, 'ty', scatter_dimension=0, tiled=True)  27.1 us
    all_to_all x1, blocking collectives, per_device(): lax.all_to_all(send_rows, TENSOR, split_axis=1, concat_axis=1, tiled=True)  24.4 us
    dot_general x1, matrix products, per_device(): jnp.einsum('tke,tck->tec', weighted, context_part).astype(jnp.bfloat16)  14.3 us
    all_to_all x1, waiting for transfers between devices, per_device(): lax.all_to_all(results, TENSOR, split_axis=0, concat_axis=0, tiled=True)  12.7 us
    all_to_all x1, starting transfers between devices, per_device(): lax.all_to_all(results, TENSOR, split_axis=0, concat_axis=0, tiled=True)  10.2 us
  transfers between devices with their start and end apart: 5, of which 5 were waited for; matrix products, arithmetic and copies ran while one was open for 1% of the time, Pallas kernels for 0%

profile of v1, /device:TPU:32, one launch (start us, length us, event | category | flops | bytes accessed | tf_op | source)
XLA Modules:
  0.0 326.0 jit_solution(1362483452195812732)
XLA Ops:
  7.2 2.2 copy.76
  9.4 1.4 reshape.178
  10.8 2.1 copy.77
  13.0 0.3 copy.75
  13.3 1.4 copy.74
  14.7 14.3 %convolution_convert_fusion = bf16[2048,8,64]{2,1,0:T(8,128)(2,1)S(1)} fusion(bf16[2048,64,2]{1,2,0:T(2,128)(2,1)} %copy.77, bf16[2048,2]{1,0:T(8,128)(2,1)S(1)} %copy.75, s32[2048,2]{1,0:T(8,128)} %copy.74), kind=kOutput, calls=%fused_computation.13 | convolution fusion | flops 4259840 | bytes 2646016 | tf_op jit(solution)/shard_map/tke,tck->tec/dot_general | solution.py:67
  29.0 7.0 %bitcast_convert_fusion = bf16[2048,2048]{1,0:T(8,128)(2,1)} fusion(bf16[8,64,2048]{2,1,0:T(8,128)(2,1)S(1)} %copy-done.11, bf16[2048,8,64]{2,1,0:T(8,128)(2,1)S(1)} %convolution_convert_fusion), kind=kOutput, calls=%fused_computation.2 | convolution fusion | flops 4299161600 | bytes 12582912 | tf_op jit(solution)/shard_map/dot_general | solution.py:73
  36.1 95.8 %reduce-scatter.4.cloned.1.call-done = bf16[256,2048]{1,0:T(8,128)(2,1)} async-done(((bf16[2048,2048]{1,0:T(8,128)(2,1)}), bf16[256,2048]{1,0:T(8,128)(2,1)}) %reduce-scatter.4.cloned.1.call-update) | async-done | bytes 1048592 | tf_op jit(solution)/shard_map/reduce_scatter | solution.py:74
  132.0 0.1 copy.79
  132.1 0.1 convert_reduce_fusion.1
  132.3 0.1 and_select_fusion.1
  132.6 0.1 eq.133
  132.7 0.1 eq.119
  132.8 0.2 convert_reduce_fusion
  133.0 0.1 fusion.26
  133.1 0.2 reduce_window_sum.11
  133.3 0.2 select_reduce_fusion
  133.5 0.1 reduce_sum.92
  133.7 0.1 select_reduce_fusion.2
  133.9 27.1 %reduce-scatter.6.cloned.1.call-done = bf16[64,2048]{1,0:T(8,128)(2,1)} async-done(((bf16[256,2048]{1,0:T(8,128)(2,1)}), bf16[64,2048]{1,0:T(8,128)(2,1)}) %reduce-scatter.6.cloned.1.call-update) | async-done | bytes 262160 | tf_op jit(solution)/shard_map/reduce_scatter | solution.py:75
  161.1 1.1 fusion.15
  162.2 1.1 convolution_convert_fusion.1
  163.4 2.0 reshape.179
  165.4 24.4 %all_to_all.10 = bf16[1,32,4,2048]{3,2,0,1:T(4,128)(2,1)S(1)} all-to-all(bf16[1,32,4,2048]{3,2,0,1:T(4,128)(2,1)} %bitcast.82), channel_id=1, replica_groups=mesh['expert'=8,'tz'=8,'ty'=4] {'tz','ty'}, dimensions={1} | all-to-all | bytes 1048576 | tf_op jit(solution)/shard_map/all_to_all | solution.py:120
  189.9 1.1 copy.84
  191.0 0.2 reduce-scatter.8.cloned.1.call-start
  191.2 30.9 %all-gather.3.cloned.1.call-done = bf16[8,32,4,2048]{3,1,2,0:T(8,128)(2,1)} async-done(((bf16[1,32,4,2048]{3,1,2,0:T(8,128)(2,1)}), bf16[8,32,4,2048]{3,1,2,0:T(8,128)(2,1)}) %all-gather.3.cloned.1.call-update) | async-done | bytes 4194320 | tf_op jit(solution)/shard_map/all_gather | solution.py:121
  222.1 10.0 %fusion.6 = f32[8,1,32,4,2,704]{5,2,4,3,0,1:T(8,128)S(1)} fusion(bf16[1,2048,2,704]{1,3,2,0:T(8,128)(2,1)} %param.25, bf16[8,32,4,2048]{3,1,2,0:T(8,128)(2,1)} %all-gather.3.cloned.1.call-done), kind=kOutput, calls=%fused_computation.12 | convolution fusion | flops 5905580032 | bytes 15728640 | tf_op jit(solution)/shard_map/tsecd,sdgf->tsecgf/dot_general | solution.py:27
  232.1 1.0 fusion.4
  233.1 2.4 copy.85
  235.4 3.7 %convert_element_type.95 = bf16[1024,704]{1,0:T(8,128)(2,1)} reshape(bf16[8,1,32,4,1,704]{5,3,2,0,4,1:T(4,128)(2,1)} %copy.85) | data formatting | bytes 2883584 | tf_op jit(solution)/shard_map/convert_element_type | solution.py:30
  239.2 6.4 %convert_bitcast_fusion = bf16[1024,1,2048]{2,0,1:T(8,128)(2,1)} fusion(bf16[1024,704]{1,0:T(8,128)(2,1)} %convert_element_type.95, bf16[1,704,2048]{2,1,0:T(8,128)(2,1)S(1)} %copy-done), kind=kOutput, calls=%fused_computation.7 | convolution fusion | flops 2954887168 | bytes 8519680 | tf_op jit(solution)/shard_map/bsf,sfd->bsd/dot_general | solution.py:125
  245.7 0.1 reshape.194
  245.9 0.1 mul.206
  246.2 0.1 mul.205
  246.4 39.9 %reduce-scatter.8.cloned.1.call-done = bf16[128,1,2048]{2,0,1:T(8,128)(2,1)} async-done(((bf16[1024,1,2048]{2,0,1:T(8,128)(2,1)}), bf16[128,1,2048]{2,0,1:T(8,128)(2,1)}) %reduce-scatter.8.cloned.1.call-update) | async-done | bytes 524304 | tf_op jit(solution)/shard_map/reduce_scatter | solution.py:124
  286.2 2.0 reshape.183
  288.3 10.2 %all-to-all-start.1 = ((bf16[32,4,1,2048]{3,1,2,0:T(4,128)(2,1)}), bf16[32,4,1,2048]{3,1,2,0:T(4,128)(2,1)}, u32[]{:S(2)}, u32[]{:S(2)}) async-start(bf16[32,4,1,2048]{3,1,2,0:T(4,128)(2,1)} %bitcast.81), calls=%async_computation.4 | async-start | bytes 1048576 | tf_op jit(solution)/shard_map/all_to_all | solution.py:133
  298.5 0.2 fusion.22
  298.7 1.0 gather_fusion.1
  299.7 0.1 reshape.197
  300.0 12.7 %all-to-all-done.1 = bf16[32,4,1,2048]{3,1,2,0:T(4,128)(2,1)} async-done(((bf16[32,4,1,2048]{3,1,2,0:T(4,128)(2,1)}), bf16[32,4,1,2048]{3,1,2,0:T(4,128)(2,1)}, u32[]{:S(2)}, u32[]{:S(2)}) %all-to-all-start.1) | async-done | bytes 524320 | tf_op jit(solution)/shard_map/all_to_all | solution.py:133
  312.7 1.2 reshape.184
  313.9 1.7 gather_fusion
  315.6 1.4 gather.11
  317.0 0.3 fusion.21
  317.4 1.2 multiply_reduce_fusion
  318.6 0.8 multiply_convert_fusion
  (56 shorter events, 1.1 us)
Async XLA Ops:
  7.2 232.0 %copy-start = (bf16[1,704,2048]{2,1,0:T(8,128)(2,1)S(1)}, bf16[1,704,2048]{2,1,0:T(8,128)(2,1)}, u32[]{:S(2)}) copy-start(bf16[1,704,2048]{2,1,0:T(8,128)(2,1)} %param.26) | copy-start | bytes 8650756
  7.2 5.7 %copy-start.5 = (f32[2048,2]{0,1:T(2,128)S(1)}, f32[2048,2]{0,1:T(2,128)}, u32[]{:S(2)}) copy-start(f32[2048,2]{0,1:T(2,128)} %param.17) | copy-start | bytes 49156
  7.2 6.1 %copy-start.4 = (s32[2048,2]{0,1:T(2,128)S(1)}, s32[2048,2]{0,1:T(2,128)}, u32[]{:S(2)}) copy-start(s32[2048,2]{0,1:T(2,128)} %param.16) | copy-start | bytes 49156
  7.2 124.7 %reduce-scatter.4.cloned.1.call-start = ((), (), s32[]{:S(2)}) async-start(), calls=%async_computation.5 | async-start | bytes 9437184 | tf_op jit(solution)/shard_map/reduce_scatter | solution.py:74
  14.7 14.3 %copy-start.11 = (bf16[8,64,2048]{2,1,0:T(8,128)(2,1)S(1)}, bf16[8,64,2048]{2,1,0:T(8,128)(2,1)}, u32[]{:S(2)}) copy-start(bf16[8,64,2048]{2,1,0:T(8,128)(2,1)} %param.18) | copy-start | bytes 6291460
  36.0 96.0 %copy-start.7 = (bf16[2048]{0:T(1024)(128)(2,1)S(1)}, bf16[2048]{0:T(1024)(128)(2,1)}, u32[]{:S(2)}) copy-start(bf16[2048]{0:T(1024)(128)(2,1)} %param.19) | copy-start | bytes 12292
  36.0 96.0 %copy-start.3 = (s32[64,2]{0,1:T(2,128)S(1)}, s32[64,2]{0,1:T(2,128)}, u32[]{:S(2)}) copy-start(s32[64,2]{0,1:T(2,128)} %param.21) | copy-start | bytes 1540
  36.0 96.2 %copy-start.6 = (s32[32]{0:T(128)S(1)}, s32[32]{0:T(128)}, u32[]{:S(2)}) copy-start(s32[32]{0:T(128)} %param.23) | copy-start | bytes 388
  36.0 96.4 %copy-start.9 = (s32[64,2]{0,1:T(2,128)S(1)}, s32[64,2]{0,1:T(2,128)}, u32[]{:S(2)}) copy-start(s32[64,2]{0,1:T(2,128)} %param.22) | copy-start | bytes 1540
  36.0 97.7 %copy-start.10 = (s32[32]{0:T(128)S(1)}, s32[32]{0:T(128)}, u32[]{:S(2)}) copy-start(s32[32]{0:T(128)} %param.24) | copy-start | bytes 388
  36.0 125.1 %copy-start.2 = (bf16[64,2048]{1,0:T(8,128)(2,1)S(1)}, bf16[64,2048]{1,0:T(8,128)(2,1)}, u32[]{:S(2)}) copy-start(bf16[64,2048]{1,0:T(8,128)(2,1)} %param.14) | copy-start | bytes 786436
  36.0 125.0 %reduce-scatter.6.cloned.1.call-start = ((), (), s32[]{:S(2)}) async-start(), calls=%async_computation.6 | async-start | bytes 1310720 | tf_op jit(solution)/shard_map/reduce_scatter | solution.py:75
  131.9 90.1 %all-gather.3.cloned.1.call-start = ((), (), s32[]{:S(2)}) async-start(), calls=%async_computation.8 | async-start | bytes 4718592 | tf_op jit(solution)/shard_map/all_gather | solution.py:121
  162.2 136.2 %copy-start.1 = (bf16[64,2048]{1,0:T(8,128)(2,1)}, bf16[64,2048]{1,0:T(8,128)(2,1)S(1)}, u32[]{:S(2)}) copy-start(bf16[64,2048]{1,0:T(8,128)(2,1)S(1)} %get-tuple-element.9) | copy-start | bytes 786436
  191.0 95.3 %reduce-scatter.8.cloned.1.call-start = ((), (), s32[]{:S(2)}) async-start(), calls=%async_computation.7 | async-start | bytes 4718592 | tf_op jit(solution)/shard_map/reduce_scatter | solution.py:124
  245.5 0.8 copy-start.8
  245.5 52.9 %copy-start.12 = (bf16[2048,8]{0,1:T(8,128)(2,1)S(1)}, bf16[2048,8]{0,1:T(8,128)(2,1)}, u32[]{:S(2)}) copy-start(bf16[2048,8]{0,1:T(8,128)(2,1)} %param.20) | copy-start | bytes 98308
  288.3 24.5 %all-to-all-start.1 = ((bf16[32,4,1,2048]{3,1,2,0:T(4,128)(2,1)}), bf16[32,4,1,2048]{3,1,2,0:T(4,128)(2,1)}, u32[]{:S(2)}, u32[]{:S(2)}) async-start(bf16[32,4,1,2048]{3,1,2,0:T(4,128)(2,1)} %bitcast.81), calls=%async_computation.4 | async-start | bytes 1048576 | tf_op jit(solution)/shard_map/all_to_all | solution.py:133
Sparse Core Ops, SparseCore 0:
  36.1 95.7 reduce-scatter.3
  134.5 26.5 reduce-scatter.5
  191.1 30.9 all-gather.2
  245.7 40.5 reduce-scatter.7

commit v2 on v1

--- a/solution.py
+++ b/solution.py
@@ -16,22 +16,8 @@
 
 
 def pair_gates(scores):
-    first = jax.nn.silu(scores[:, 0:1] * 0.0) * 0.0 + jax.nn.sigmoid(
-        scores[:, 0:1] - scores[:, 1:2]
-    )
-    first = first[:, 0]
+    first = jax.nn.sigmoid(scores[:, 0] - scores[:, 1])
     return jnp.stack([first, 1.0 - first], axis=1)
-
-
-def activate(shard_piece, w_gate_up):
-    both = jnp.einsum(
-        "tsecd,sdgf->tsecgf", shard_piece, w_gate_up, preferred_element_type=jnp.float32
-    )
-    hidden = (jax.nn.silu(both[:, :, :, :, 0, :]) * both[:, :, :, :, 1, :]).astype(jnp.bfloat16)
-    hidden = jnp.transpose(hidden, (0, 2, 3, 1, 4))
-    return hidden.reshape(
-        hidden.shape[0] * hidden.shape[1] * hidden.shape[2], hidden.shape[3], hidden.shape[4]
-    )
 
 
 def per_device(
@@ -58,18 +44,17 @@
     slice_ctx = att_out_w.shape[1]
     top_count = att_routes.shape[1]
     gate_att = pair_gates(att_scores)
-    chosen = (
-        att_routes[:, :, None] == jnp.arange(att_experts, dtype=jnp.int32)[None, None, :]
-    ).astype(jnp.float32)
-    weighted = chosen * gate_att[:, :, None]
-    context_part = contexts.reshape(group_rows, slice_ctx, top_count).astype(jnp.float32)
-    mixed = (
-        jnp.einsum("tke,tck->tec", weighted, context_part)
-        .astype(jnp.bfloat16)
-        .reshape(group_rows, att_experts * slice_ctx)
-    )
-    weight_flat = att_out_w.reshape(att_experts * slice_ctx, model_width)
-    row_block = mixed
+    width = att_experts * slice_ctx
+    column = jnp.arange(width, dtype=jnp.int32)
+    source = jnp.arange(slice_ctx * top_count, dtype=jnp.int32)[:, None]
+    mixed = jnp.zeros((group_rows, width), jnp.float32)
+    for choice in range(top_count):
+        spread = (source == (column % slice_ctx)[None, :] * top_count + choice).astype(jnp.bfloat16)
+        picked = jnp.dot(contexts, spread, preferred_element_type=jnp.float32)
+        chosen = att_routes[:, choice : choice + 1] == (column // slice_ctx)[None, :]
+        mixed = mixed + jnp.where(chosen, picked * gate_att[:, choice : choice + 1], 0.0)
+    row_block = mixed.astype(jnp.bfloat16)
+    weight_flat = att_out_w.reshape(width, model_width)
     partial = jnp.dot(row_block, weight_flat, preferred_element_type=jnp.float32).astype(jnp.bfloat16)
     partial = lax.psum_scatter(partial, "tz", scatter_dimension=0, tiled=True)
     attention = lax.psum_scatter(partial, "ty", scatter_dimension=0, tiled=True).astype(jnp.float32)
@@ -119,27 +104,34 @@
     send_rows = send_rows.reshape(slots, n_tensor, capacity_rows, model_width)
     exchanged = lax.all_to_all(send_rows, TENSOR, split_axis=1, concat_axis=1, tiled=True)
     arrived = lax.all_gather(exchanged[None], "expert", axis=0, tiled=True)
-    hidden = activate(arrived, w_gate_up)
-    row_block = hidden
-    summed = lax.psum_scatter(
-        jnp.einsum("bsf,sfd->bsd", row_block, w_down, preferred_element_type=jnp.float32).astype(
-            jnp.bfloat16
-        ),
-        "expert",
-        scatter_dimension=0,
-        tiled=True,
+    hidden_units = w_gate_up.shape[3]
+    rows_in = arrived.reshape(-1, model_width)
+    both = jnp.dot(
+        rows_in, w_gate_up.reshape(model_width, 2 * hidden_units), preferred_element_type=jnp.float32
     )
-    results = summed.reshape(n_tensor, capacity_rows, slots, model_width)
+    hidden = (jax.nn.silu(both[:, :hidden_units]) * both[:, hidden_units:]).astype(jnp.bfloat16)
+    down = jnp.dot(
+        hidden, w_down.reshape(hidden_units, model_width), preferred_element_type=jnp.float32
+    ).astype(jnp.bfloat16)
+    summed = lax.psum_scatter(down, "expert", scatter_dimension=0, tiled=True)
+    results = summed.reshape(n_tensor, capacity_rows * slots, model_width)
     returned = lax.all_to_all(results, TENSOR, split_axis=0, concat_axis=0, tiled=True)
     flat_back = returned.reshape(n_tensor * capacity_rows * slots, model_width)
     back_index = jnp.where(is_kept, holder * (capacity_rows * slots) + arrival * slots + within, 0)
-    fetched = (
-        jnp.take(flat_back, back_index.reshape(-1), axis=0)
-        .reshape(row_count, top_count, model_width)
-        .astype(jnp.float32)
+    factors = gate_mlp * is_kept.astype(jnp.float32)
+    back_rows = flat_back.shape[0]
+    select = jnp.sum(
+        jnp.where(
+            back_index[:, :, None] == jnp.arange(back_rows, dtype=jnp.int32)[None, None, :],
+            factors[:, :, None],
+            0.0,
+        ),
+        axis=1,
     )
-    factors = gate_mlp * is_kept.astype(jnp.float32)
-    expert_mix = fetched[:, 0, :] * factors[:, 0:1] + fetched[:, 1, :] * factors[:, 1:2]
+    expert_mix = jnp.dot(
+        select, flat_back.astype(jnp.float32), precision=lax.Precision.HIGHEST,
+        preferred_element_type=jnp.float32,
+    )
     after = stream.astype(jnp.float32) + expert_mix
     return (after.astype(jnp.bfloat16), rms_norm(after, final_gain).astype(jnp.bfloat16))
 

time: 328 us -> 319 us (0.973)
  matrix products: 39 us -> 32.3 us
    dot_general x3 -> x4, matrix products: 30.6 us -> 21.1 us  [the longest x1 10.6 us: per_device(): jnp.dot(rows_in, w_gate_up.reshape(model_width, 2 * hidden_units), prefer...]
    all_gather x0 -> x1, local copies, waits for them, and re-layouts: none -> 7.45 us  [per_device(): arrived = lax.all_gather(exchanged[None], 'expert', axis=0, tiled=True)]
    convert_element_type x2 -> x0, local copies, waits for them, and re-layouts: 6.1 us -> none  [activate(): (jax.nn.silu(both[:, :, :, :, 0, :]) * both[:, :, :, :, 1, :]).astype(jnp...]
    reshape x3 -> x4, local copies, waits for them, and re-layouts: 5.49 us -> 9.16 us  [the longest x1 6.91 us: per_device(): rows_in = arrived.reshape(-1, model_width)]
where the time goes in v2:
time: 319 us; the launch traced here: 317 us
  waiting for transfers between devices  207 us (65%)
  matrix products  32.3 us (10%)
  local copies, waits for them, and re-layouts  25 us (8%)
  blocking collectives  24.4 us (8%)
  between operations  14 us (4%)
  starting transfers between devices  10.4 us (3%)
  other arithmetic  4.17 us (1%)
    reduce_scatter x1, waiting for transfers between devices, per_device(): partial = lax.psum_scatter(partial, 'tz', scatter_dimension=0, tiled=True)  95.8 us
    reduce_scatter x1, waiting for transfers between devices, per_device(): summed = lax.psum_scatter(down, 'expert', scatter_dimension=0, tiled=True)  40 us
    all_gather x1, waiting for transfers between devices, per_device(): arrived = lax.all_gather(exchanged[None], 'expert', axis=0, tiled=True)  30.9 us
    reduce_scatter x1, waiting for transfers between devices, per_device(): lax.psum_scatter(partial, 'ty', scatter_dimension=0, tiled=True)  27.1 us
    all_to_all x1, blocking collectives, per_device(): lax.all_to_all(send_rows, TENSOR, split_axis=1, concat_axis=1, tiled=True)  24.4 us
    all_to_all x1, waiting for transfers between devices, per_device(): lax.all_to_all(results, TENSOR, split_axis=0, concat_axis=0, tiled=True)  12.7 us
    dot_general x1, matrix products, per_device(): jnp.dot(rows_in, w_gate_up.reshape(model_width, 2 * hidden_units), prefer...  10.6 us
    all_to_all x1, starting transfers between devices, per_device(): lax.all_to_all(results, TENSOR, split_axis=0, concat_axis=0, tiled=True)  10 us
  transfers between devices with their start and end apart: 5, of which 5 were waited for; matrix products, arithmetic and copies ran while one was open for 1% of the time, Pallas kernels for 0%

profile of v2, /device:TPU:32, one launch (start us, length us, event | category | flops | bytes accessed | tf_op | source)
XLA Modules:
  0.0 316.9 jit_solution(18410673396125855981)
XLA Ops:
  7.3 0.9 fusion.35
  8.2 0.8 broadcast_subtract_fusion
  9.0 3.8 %fusion.13 = f32[512,2048]{1,0:T(8,128)} fusion(bf16[2048,128]{1,0:T(8,128)(2,1)} %param.15, s32[512]{0:T(512)S(1)} %fusion.29), kind=kOutput, calls=%fused_computation.25 | convolution fusion | flops 268566528 | bytes 4720640 | tf_op jit(solution)/shard_map/dot_general | solution.py:53
  12.8 9.8 %convolution_convert_fusion = bf16[2048,2048]{1,0:T(8,128)(2,1)} fusion(bf16[512,2048]{1,0:T(8,128)(2,1)} %bitcast.43, f32[512,2048]{1,0:T(8,128)} %fusion.13, bf16[2048,128]{1,0:T(8,128)(2,1)S(1)} %copy-done.1, f32[2048]{0:T(1024)S(1)} %bitcast.40, s32[2048]{0:T(1024)S(1)} %bitcast.39, f32[2048]{0:T(1024)S(1)} %bitcast.41, s32[2048]{0:T(1024)S(1)} %bitcast.38, ...), kind=kOutput, calls=%fused_computation.1 | convolution fusion | flops 4576116736 | bytes 15241216 | tf_op jit(solution)/shard_map/dot_general | solution.py:58
  22.7 0.0 reduce-scatter.6.cloned.1.call-start
  22.8 95.8 %reduce-scatter.4.cloned.1.call-done = bf16[256,2048]{1,0:T(8,128)(2,1)} async-done(((bf16[2048,2048]{1,0:T(8,128)(2,1)}), bf16[256,2048]{1,0:T(8,128)(2,1)}) %reduce-scatter.4.cloned.1.call-update) | async-done | bytes 1048592 | tf_op jit(solution)/shard_map/reduce_scatter | solution.py:59
  118.7 0.1 copy.71
  118.8 0.1 convert_reduce_fusion.1
  118.9 0.1 select_reduce_fusion.4
  119.0 0.1 and_select_fusion.1
  119.1 0.1 copy.72
  119.2 0.1 eq.202
  119.4 0.1 eq.188
  119.5 0.2 convert_reduce_fusion
  119.7 0.1 fusion.22
  119.8 0.2 reduce_window_sum.11
  120.0 0.2 select_reduce_fusion.1
  120.2 0.1 reshape.152
  120.3 0.1 copy.73
  120.4 0.1 select_reduce_fusion.2
  120.5 0.1 fusion.23
  120.6 27.1 %reduce-scatter.6.cloned.1.call-done = bf16[64,2048]{1,0:T(8,128)(2,1)} async-done(((bf16[256,2048]{1,0:T(8,128)(2,1)}), bf16[64,2048]{1,0:T(8,128)(2,1)}) %reduce-scatter.6.cloned.1.call-update) | async-done | bytes 262160 | tf_op jit(solution)/shard_map/reduce_scatter | solution.py:60
  147.7 1.1 fusion.6
  148.9 1.2 convolution_convert_fusion.2
  150.1 2.0 reshape.154
  152.1 24.4 %all_to_all.10 = bf16[1,32,4,2048]{3,2,0,1:T(4,128)(2,1)S(1)} all-to-all(bf16[1,32,4,2048]{3,2,0,1:T(4,128)(2,1)} %bitcast.37), channel_id=1, replica_groups=mesh['expert'=8,'tz'=8,'ty'=4] {'tz','ty'}, dimensions={1} | all-to-all | bytes 1048576 | tf_op jit(solution)/shard_map/all_to_all | solution.py:105
  176.5 1.1 copy.78
  177.6 0.2 reduce-scatter.8.cloned.1.call-start
  177.8 30.9 %all-gather.3.cloned.1.call-done = bf16[8,32,4,2048]{3,1,2,0:T(8,128)(2,1)} async-done(((bf16[1,32,4,2048]{3,1,2,0:T(8,128)(2,1)}), bf16[8,32,4,2048]{3,1,2,0:T(8,128)(2,1)}) %all-gather.3.cloned.1.call-update) | async-done | bytes 4194320 | tf_op jit(solution)/shard_map/all_gather | solution.py:106
  208.7 7.4 %copy.79 = bf16[8,32,4,2048]{3,2,1,0:T(4,128)(2,1)} copy(bf16[8,32,4,2048]{3,1,2,0:T(8,128)(2,1)} %all-gather.3.cloned.1.call-done) | data formatting | bytes 8388608 | tf_op jit(solution)/shard_map/all_gather | solution.py:106
  216.2 6.9 %reshape.155 = bf16[1024,2048]{1,0:T(8,128)(2,1)} reshape(bf16[8,32,4,2048]{3,2,1,0:T(4,128)(2,1)} %copy.79) | data formatting | bytes 8388608 | tf_op jit(solution)/shard_map/reshape | solution.py:108
  223.1 10.6 %fusion.36 = f32[1024,1408]{1,0:T(8,128)S(1)} fusion(bf16[1024,2048]{1,0:T(8,128)(2,1)} %reshape.155, bf16[2048,1408]{0,1:T(8,128)(2,1)} %bitcast.42), kind=kOutput, calls=%fused_computation.79 | convolution fusion | flops 5905580032 | bytes 15728640 | tf_op jit(solution)/shard_map/dot_general | solution.py:109
  233.7 5.2 %convolution_convert_fusion.1 = bf16[1024,2048]{1,0:T(8,128)(2,1)} fusion(bf16[1,704,2048]{2,1,0:T(8,128)(2,1)S(1)} %copy-done, f32[1024,1408]{1,0:T(8,128)S(1)} %fusion.36), kind=kOutput, calls=%fused_computation.6 | convolution fusion | flops 2959212544 | bytes 13369344 | tf_op jit(solution)/shard_map/dot_general | solution.py:113
  238.9 0.1 copy.75
  239.0 0.1 reshape.160
  239.1 0.4 copy-done.6
  239.6 40.0 %reduce-scatter.8.cloned.1.call-done = bf16[128,2048]{1,0:T(8,128)(2,1)} async-done(((bf16[1024,2048]{1,0:T(8,128)(2,1)}), bf16[128,2048]{1,0:T(8,128)(2,1)}) %reduce-scatter.8.cloned.1.call-update) | async-done | bytes 524304 | tf_op jit(solution)/shard_map/reduce_scatter | solution.py:116
  279.5 2.0 reshape.158
  281.6 10.0 %all-to-all-start.1 = ((bf16[32,4,2048]{2,1,0:T(4,128)(2,1)}), bf16[32,4,2048]{2,1,0:T(4,128)(2,1)}, u32[]{:S(2)}, u32[]{:S(2)}) async-start(bf16[32,4,2048]{2,1,0:T(4,128)(2,1)} %reshape.158), calls=%async_computation.4 | async-start | bytes 1048576 | tf_op jit(solution)/shard_map/all_to_all | solution.py:118
  291.6 0.2 fusion.19
  291.9 1.0 gather_fusion
  292.9 0.1 reshape.163
  293.0 0.1 copy.76
  293.2 0.1 select_reduce_fusion
  293.3 12.7 %all-to-all-done.1 = bf16[32,4,2048]{2,1,0:T(4,128)(2,1)} async-done(((bf16[32,4,2048]{2,1,0:T(4,128)(2,1)}), bf16[32,4,2048]{2,1,0:T(4,128)(2,1)}, u32[]{:S(2)}, u32[]{:S(2)}) %all-to-all-start.1) | async-done | bytes 524320 | tf_op jit(solution)/shard_map/all_to_all | solution.py:118
  306.0 2.0 reshape.159
  307.9 1.6 multiply_reduce_fusion
  309.5 0.8 multiply_convert_fusion
  (36 shorter events, 0.3 us)
Async XLA Ops:
  7.2 226.5 %copy-start = (bf16[1,704,2048]{2,1,0:T(8,128)(2,1)S(1)}, bf16[1,704,2048]{2,1,0:T(8,128)(2,1)}, u32[]{:S(2)}) copy-start(bf16[1,704,2048]{2,1,0:T(8,128)(2,1)} %param.26) | copy-start | bytes 8650756
  7.2 5.6 %copy-start.1 = (bf16[2048,128]{1,0:T(8,128)(2,1)S(1)}, bf16[2048,128]{1,0:T(8,128)(2,1)}, u32[]{:S(2)}) copy-start(bf16[2048,128]{1,0:T(8,128)(2,1)} %param.15) | copy-start | bytes 1572868
  7.2 111.4 %reduce-scatter.4.cloned.1.call-start = ((), (), s32[]{:S(2)}) async-start(), calls=%async_computation.5 | async-start | bytes 9437184 | tf_op jit(solution)/shard_map/reduce_scatter | solution.py:59
  22.6 96.0 %copy-start.5 = (bf16[2048]{0:T(1024)(128)(2,1)S(1)}, bf16[2048]{0:T(1024)(128)(2,1)}, u32[]{:S(2)}) copy-start(bf16[2048]{0:T(1024)(128)(2,1)} %param.19) | copy-start | bytes 12292
  22.6 96.1 %copy-start.3 = (s32[64,2]{0,1:T(2,128)S(1)}, s32[64,2]{0,1:T(2,128)}, u32[]{:S(2)}) copy-start(s32[64,2]{0,1:T(2,128)} %param.21) | copy-start | bytes 1540
  22.6 96.2 %copy-start.4 = (s32[32]{0:T(128)S(1)}, s32[32]{0:T(128)}, u32[]{:S(2)}) copy-start(s32[32]{0:T(128)} %param.23) | copy-start | bytes 388
  22.6 96.4 %copy-start.7 = (s32[64,2]{0,1:T(2,128)S(1)}, s32[64,2]{0,1:T(2,128)}, u32[]{:S(2)}) copy-start(s32[64,2]{0,1:T(2,128)} %param.22) | copy-start | bytes 1540
  22.7 97.7 %copy-start.8 = (s32[32]{0:T(128)S(1)}, s32[32]{0:T(128)}, u32[]{:S(2)}) copy-start(s32[32]{0:T(128)} %param.24) | copy-start | bytes 388
  22.7 125.1 %copy-start.2 = (bf16[64,2048]{1,0:T(8,128)(2,1)S(1)}, bf16[64,2048]{1,0:T(8,128)(2,1)}, u32[]{:S(2)}) copy-start(bf16[64,2048]{1,0:T(8,128)(2,1)} %param.14) | copy-start | bytes 786436
  22.7 125.0 %reduce-scatter.6.cloned.1.call-start = ((), (), s32[]{:S(2)}) async-start(), calls=%async_computation.6 | async-start | bytes 1310720 | tf_op jit(solution)/shard_map/reduce_scatter | solution.py:60
  118.6 90.1 %all-gather.3.cloned.1.call-start = ((), (), s32[]{:S(2)}) async-start(), calls=%async_computation.8 | async-start | bytes 4718592 | tf_op jit(solution)/shard_map/all_gather | solution.py:106
  177.6 101.9 %reduce-scatter.8.cloned.1.call-start = ((), (), s32[]{:S(2)}) async-start(), calls=%async_computation.7 | async-start | bytes 4718592 | tf_op jit(solution)/shard_map/reduce_scatter | solution.py:116
  238.9 0.7 copy-start.6
  238.9 52.7 %copy-start.9 = (bf16[2048,8]{0,1:T(8,128)(2,1)S(1)}, bf16[2048,8]{0,1:T(8,128)(2,1)}, u32[]{:S(2)}) copy-start(bf16[2048,8]{0,1:T(8,128)(2,1)} %param.20) | copy-start | bytes 98308
  281.6 24.4 %all-to-all-start.1 = ((bf16[32,4,2048]{2,1,0:T(4,128)(2,1)}), bf16[32,4,2048]{2,1,0:T(4,128)(2,1)}, u32[]{:S(2)}, u32[]{:S(2)}) async-start(bf16[32,4,2048]{2,1,0:T(4,128)(2,1)} %reshape.158), calls=%async_computation.4 | async-start | bytes 1048576 | tf_op jit(solution)/shard_map/all_to_all | solution.py:118
Sparse Core Ops, SparseCore 0:
  22.8 95.7 reduce-scatter.3
  121.1 26.5 reduce-scatter.5
  177.7 30.9 all-gather.2
  239.0 40.4 reduce-scatter.7

commit v3 on v2

--- a/solution.py
+++ b/solution.py
@@ -101,9 +101,8 @@
         axis=2,
     )
     send_rows = jnp.dot(placer, normed, preferred_element_type=jnp.float32).astype(jnp.bfloat16)
-    send_rows = send_rows.reshape(slots, n_tensor, capacity_rows, model_width)
-    exchanged = lax.all_to_all(send_rows, TENSOR, split_axis=1, concat_axis=1, tiled=True)
-    arrived = lax.all_gather(exchanged[None], "expert", axis=0, tiled=True)
+    exchanged = lax.all_to_all(send_rows, TENSOR, split_axis=0, concat_axis=0, tiled=True)
+    arrived = lax.all_gather(exchanged, "expert", axis=0, tiled=True)
     hidden_units = w_gate_up.shape[3]
     rows_in = arrived.reshape(-1, model_width)
     both = jnp.dot(
@@ -114,9 +113,7 @@
         hidden, w_down.reshape(hidden_units, model_width), preferred_element_type=jnp.float32
     ).astype(jnp.bfloat16)
     summed = lax.psum_scatter(down, "expert", scatter_dimension=0, tiled=True)
-    results = summed.reshape(n_tensor, capacity_rows * slots, model_width)
-    returned = lax.all_to_all(results, TENSOR, split_axis=0, concat_axis=0, tiled=True)
-    flat_back = returned.reshape(n_tensor * capacity_rows * slots, model_width)
+    flat_back = lax.all_to_all(summed, TENSOR, split_axis=0, concat_axis=0, tiled=True)
     back_index = jnp.where(is_kept, holder * (capacity_rows * slots) + arrival * slots + within, 0)
     factors = gate_mlp * is_kept.astype(jnp.float32)
     back_rows = flat_back.shape[0]

time: 319 us -> 305 us (0.956)
  local copies, waits for them, and re-layouts: 25 us -> 11.5 us
    reshape x4 -> x0, local copies, waits for them, and re-layouts: 13 us -> none  [the longest x1 6.91 us: per_device(): rows_in = arrived.reshape(-1, model_width)]
    all_gather x1 -> x0, local copies, waits for them, and re-layouts: 7.45 us -> none  [per_device(): arrived = lax.all_gather(exchanged[None], 'expert', axis=0, tiled=True)]
    all_to_all x1 -> x4, local copies, waits for them, and re-layouts: 1.09 us -> 7.99 us  [the longest x2 4.02 us: per_device(): lax.all_to_all(summed, TENSOR, split_axis=0, concat_axis=0, tiled=True)]
where the time goes in v3:
time: 305 us; the launch traced here: 304 us
  waiting for transfers between devices  207 us (68%)
  matrix products  32.3 us (11%)
  blocking collectives  24.6 us (8%)
  between operations  14 us (5%)
  local copies, waits for them, and re-layouts  11.5 us (4%)
  starting transfers between devices  10.2 us (3%)
  other arithmetic  4.17 us (1%)
    reduce_scatter x1, waiting for transfers between devices, per_device(): partial = lax.psum_scatter(partial, 'tz', scatter_dimension=0, tiled=True)  95.8 us
    reduce_scatter x1, waiting for transfers between devices, per_device(): summed = lax.psum_scatter(down, 'expert', scatter_dimension=0, tiled=True)  40 us
    all_gather x1, waiting for transfers between devices, per_device(): arrived = lax.all_gather(exchanged, 'expert', axis=0, tiled=True)  31 us
    reduce_scatter x1, waiting for transfers between devices, per_device(): lax.psum_scatter(partial, 'ty', scatter_dimension=0, tiled=True)  27.1 us
    all_to_all x1, blocking collectives, per_device(): lax.all_to_all(send_rows, TENSOR, split_axis=0, concat_axis=0, tiled=True)  24.6 us
    all_to_all x1, waiting for transfers between devices, per_device(): lax.all_to_all(summed, TENSOR, split_axis=0, concat_axis=0, tiled=True)  12.7 us
    dot_general x1, matrix products, per_device(): jnp.dot(rows_in, w_gate_up.reshape(model_width, 2 * hidden_units), prefer...  10.6 us
    all_to_all x1, starting transfers between devices, per_device(): lax.all_to_all(summed, TENSOR, split_axis=0, concat_axis=0, tiled=True)  10.1 us
  transfers between devices with their start and end apart: 5, of which 5 were waited for; matrix products, arithmetic and copies ran while one was open for 1% of the time, Pallas kernels for 0%

profile of v3, /device:TPU:32, one launch (start us, length us, event | category | flops | bytes accessed | tf_op | source)
XLA Modules:
  0.0 303.5 jit_solution(5338287872564839005)
XLA Ops:
  7.2 0.0 reduce-scatter.4.cloned.1.call-start
  7.3 0.9 fusion.35
  8.2 0.8 broadcast_subtract_fusion
  9.0 3.8 %fusion.13 = f32[512,2048]{1,0:T(8,128)} fusion(bf16[2048,128]{1,0:T(8,128)(2,1)} %param.15, s32[512]{0:T(512)S(1)} %fusion.29), kind=kOutput, calls=%fused_computation.25 | convolution fusion | flops 268566528 | bytes 4720640 | tf_op jit(solution)/shard_map/dot_general | solution.py:53
  12.8 9.8 %convolution_convert_fusion = bf16[2048,2048]{1,0:T(8,128)(2,1)} fusion(bf16[512,2048]{1,0:T(8,128)(2,1)} %bitcast.41, f32[512,2048]{1,0:T(8,128)} %fusion.13, bf16[2048,128]{1,0:T(8,128)(2,1)S(1)} %copy-done.1, f32[2048]{0:T(1024)S(1)} %bitcast.38, s32[2048]{0:T(1024)S(1)} %bitcast.37, f32[2048]{0:T(1024)S(1)} %bitcast.39, s32[2048]{0:T(1024)S(1)} %bitcast.36, ...), kind=kOutput, calls=%fused_computation.1 | convolution fusion | flops 4576116736 | bytes 15241216 | tf_op jit(solution)/shard_map/dot_general | solution.py:58
  22.7 0.0 reduce-scatter.6.cloned.1.call-start
  22.8 95.8 %reduce-scatter.4.cloned.1.call-done = bf16[256,2048]{1,0:T(8,128)(2,1)} async-done(((bf16[2048,2048]{1,0:T(8,128)(2,1)}), bf16[256,2048]{1,0:T(8,128)(2,1)}) %reduce-scatter.4.cloned.1.call-update) | async-done | bytes 1048592 | tf_op jit(solution)/shard_map/reduce_scatter | solution.py:59
  118.6 0.0 all-gather.2.cloned.1.call-start
  118.7 0.1 copy.52
  118.8 0.1 convert_reduce_fusion.1
  118.9 0.1 select_reduce_fusion.4
  119.0 0.1 and_select_fusion.1
  119.1 0.1 copy.53
  119.2 0.1 eq.202
  119.4 0.1 eq.188
  119.5 0.2 convert_reduce_fusion
  119.7 0.1 fusion.22
  119.8 0.2 reduce_window_sum.11
  120.0 0.2 select_reduce_fusion.1
  120.2 0.1 reshape.144
  120.3 0.1 copy.54
  120.4 0.1 select_reduce_fusion.2
  120.5 0.1 fusion.23
  120.6 27.1 %reduce-scatter.6.cloned.1.call-done = bf16[64,2048]{1,0:T(8,128)(2,1)} async-done(((bf16[256,2048]{1,0:T(8,128)(2,1)}), bf16[64,2048]{1,0:T(8,128)(2,1)}) %reduce-scatter.6.cloned.1.call-update) | async-done | bytes 262160 | tf_op jit(solution)/shard_map/reduce_scatter | solution.py:60
  147.7 1.1 fusion.6
  148.9 1.2 convolution_convert_fusion.2
  150.1 2.0 all_to_all.16
  152.1 24.6 %all_to_all.24 = bf16[32,4,2048]{2,1,0:T(4,128)(2,1)} all-to-all(bf16[32,4,2048]{2,1,0:T(4,128)(2,1)} %all_to_all.16), channel_id=1, replica_groups=mesh['expert'=8,'tz'=8,'ty'=4] {'tz','ty'}, dimensions={0} | all-to-all | bytes 1048576 | tf_op jit(solution)/shard_map/all_to_all | solution.py:104
  176.7 2.0 all_to_all.18
  178.6 0.0 reduce-scatter.8.cloned.1.call-start
  178.7 31.0 %all-gather.2.cloned.1.call-done = bf16[1024,2048]{1,0:T(8,128)(2,1)} async-done(((bf16[128,2048]{1,0:T(8,128)(2,1)}), bf16[1024,2048]{1,0:T(8,128)(2,1)}) %all-gather.2.cloned.1.call-update) | async-done | bytes 4194320 | tf_op jit(solution)/shard_map/all_gather | solution.py:105
  209.7 10.6 %fusion.36 = f32[1024,1408]{1,0:T(8,128)S(1)} fusion(bf16[1024,2048]{1,0:T(8,128)(2,1)} %all-gather.2.cloned.1.call-done, bf16[2048,1408]{0,1:T(8,128)(2,1)} %bitcast.40), kind=kOutput, calls=%fused_computation.79 | convolution fusion | flops 5905580032 | bytes 15728640 | tf_op jit(solution)/shard_map/dot_general | solution.py:108
  220.3 5.2 %convolution_convert_fusion.1 = bf16[1024,2048]{1,0:T(8,128)(2,1)} fusion(bf16[1,704,2048]{2,1,0:T(8,128)(2,1)S(1)} %copy-done, f32[1024,1408]{1,0:T(8,128)S(1)} %fusion.36), kind=kOutput, calls=%fused_computation.6 | convolution fusion | flops 2959212544 | bytes 13369344 | tf_op jit(solution)/shard_map/dot_general | solution.py:112
  225.5 0.1 copy.56
  225.6 0.1 reshape.148
  225.8 0.4 copy-done.6
  226.2 40.0 %reduce-scatter.8.cloned.1.call-done = bf16[128,2048]{1,0:T(8,128)(2,1)} async-done(((bf16[1024,2048]{1,0:T(8,128)(2,1)}), bf16[128,2048]{1,0:T(8,128)(2,1)}) %reduce-scatter.8.cloned.1.call-update) | async-done | bytes 524304 | tf_op jit(solution)/shard_map/reduce_scatter | solution.py:115
  266.1 2.0 all_to_all.19
  268.2 10.1 %all-to-all-start.1 = ((bf16[32,4,2048]{2,1,0:T(4,128)(2,1)}), bf16[32,4,2048]{2,1,0:T(4,128)(2,1)}, u32[]{:S(2)}, u32[]{:S(2)}) async-start(bf16[32,4,2048]{2,1,0:T(4,128)(2,1)} %all_to_all.19), calls=%async_computation.4 | async-start | bytes 1048576 | tf_op jit(solution)/shard_map/all_to_all | solution.py:116
  278.3 0.2 fusion.19
  278.5 1.0 gather_fusion
  279.5 0.1 reshape.151
  279.7 0.1 copy.57
  279.8 0.1 select_reduce_fusion
  279.9 12.7 %all-to-all-done.1 = bf16[32,4,2048]{2,1,0:T(4,128)(2,1)} async-done(((bf16[32,4,2048]{2,1,0:T(4,128)(2,1)}), bf16[32,4,2048]{2,1,0:T(4,128)(2,1)}, u32[]{:S(2)}, u32[]{:S(2)}) %all-to-all-start.1) | async-done | bytes 524320 | tf_op jit(solution)/shard_map/all_to_all | solution.py:116
  292.6 2.0 all_to_all.21
  294.6 1.5 multiply_reduce_fusion
  296.1 0.8 multiply_convert_fusion
  (34 shorter events, 0.2 us)
Async XLA Ops:
  7.2 213.1 %copy-start = (bf16[1,704,2048]{2,1,0:T(8,128)(2,1)S(1)}, bf16[1,704,2048]{2,1,0:T(8,128)(2,1)}, u32[]{:S(2)}) copy-start(bf16[1,704,2048]{2,1,0:T(8,128)(2,1)} %param.26) | copy-start | bytes 8650756
  7.2 5.6 %copy-start.1 = (bf16[2048,128]{1,0:T(8,128)(2,1)S(1)}, bf16[2048,128]{1,0:T(8,128)(2,1)}, u32[]{:S(2)}) copy-start(bf16[2048,128]{1,0:T(8,128)(2,1)} %param.15) | copy-start | bytes 1572868
  7.2 111.4 %reduce-scatter.4.cloned.1.call-start = ((), (), s32[]{:S(2)}) async-start(), calls=%async_computation.5 | async-start | bytes 9437184 | tf_op jit(solution)/shard_map/reduce_scatter | solution.py:59
  22.6 96.0 %copy-start.5 = (bf16[2048]{0:T(1024)(128)(2,1)S(1)}, bf16[2048]{0:T(1024)(128)(2,1)}, u32[]{:S(2)}) copy-start(bf16[2048]{0:T(1024)(128)(2,1)} %param.19) | copy-start | bytes 12292
  22.6 96.1 %copy-start.3 = (s32[64,2]{0,1:T(2,128)S(1)}, s32[64,2]{0,1:T(2,128)}, u32[]{:S(2)}) copy-start(s32[64,2]{0,1:T(2,128)} %param.21) | copy-start | bytes 1540
  22.6 96.2 %copy-start.4 = (s32[32]{0:T(128)S(1)}, s32[32]{0:T(128)}, u32[]{:S(2)}) copy-start(s32[32]{0:T(128)} %param.23) | copy-start | bytes 388
  22.6 96.4 %copy-start.7 = (s32[64,2]{0,1:T(2,128)S(1)}, s32[64,2]{0,1:T(2,128)}, u32[]{:S(2)}) copy-start(s32[64,2]{0,1:T(2,128)} %param.22) | copy-start | bytes 1540
  22.7 97.7 %copy-start.8 = (s32[32]{0:T(128)S(1)}, s32[32]{0:T(128)}, u32[]{:S(2)}) copy-start(s32[32]{0:T(128)} %param.24) | copy-start | bytes 388
  22.7 125.1 %copy-start.2 = (bf16[64,2048]{1,0:T(8,128)(2,1)S(1)}, bf16[64,2048]{1,0:T(8,128)(2,1)}, u32[]{:S(2)}) copy-start(bf16[64,2048]{1,0:T(8,128)(2,1)} %param.14) | copy-start | bytes 786436
  22.7 125.0 %reduce-scatter.6.cloned.1.call-start = ((), (), s32[]{:S(2)}) async-start(), calls=%async_computation.6 | async-start | bytes 1310720 | tf_op jit(solution)/shard_map/reduce_scatter | solution.py:60
  118.6 91.1 %all-gather.2.cloned.1.call-start = ((), (), s32[]{:S(2)}) async-start(), calls=%async_computation.7 | async-start | bytes 4718592 | tf_op jit(solution)/shard_map/all_gather | solution.py:105
  178.6 87.5 %reduce-scatter.8.cloned.1.call-start = ((), (), s32[]{:S(2)}) async-start(), calls=%async_computation.8 | async-start | bytes 4718592 | tf_op jit(solution)/shard_map/reduce_scatter | solution.py:115
  225.5 0.7 copy-start.6
  225.5 52.8 %copy-start.9 = (bf16[2048,8]{0,1:T(8,128)(2,1)S(1)}, bf16[2048,8]{0,1:T(8,128)(2,1)}, u32[]{:S(2)}) copy-start(bf16[2048,8]{0,1:T(8,128)(2,1)} %param.20) | copy-start | bytes 98308
  268.2 24.4 %all-to-all-start.1 = ((bf16[32,4,2048]{2,1,0:T(4,128)(2,1)}), bf16[32,4,2048]{2,1,0:T(4,128)(2,1)}, u32[]{:S(2)}, u32[]{:S(2)}) async-start(bf16[32,4,2048]{2,1,0:T(4,128)(2,1)} %all_to_all.19), calls=%async_computation.4 | async-start | bytes 1048576 | tf_op jit(solution)/shard_map/all_to_all | solution.py:116
Sparse Core Ops, SparseCore 0:
  22.8 95.7 reduce-scatter.3
  121.1 26.5 reduce-scatter.5
  178.8 30.8 all-gather.1
  225.6 40.4 reduce-scatter.7

commit v4 on v3

--- a/solution.py
+++ b/solution.py
@@ -57,7 +57,9 @@
     weight_flat = att_out_w.reshape(width, model_width)
     partial = jnp.dot(row_block, weight_flat, preferred_element_type=jnp.float32).astype(jnp.bfloat16)
     partial = lax.psum_scatter(partial, "tz", scatter_dimension=0, tiled=True)
-    attention = lax.psum_scatter(partial, "ty", scatter_dimension=0, tiled=True).astype(jnp.float32)
+    n_y = lax.axis_size("ty")
+    gathered = lax.all_to_all(partial, "ty", split_axis=0, concat_axis=0, tiled=True)
+    attention = jnp.sum(gathered.reshape(n_y, -1, model_width).astype(jnp.float32), axis=0)
     stream = (resid.astype(jnp.float32) + attention).astype(jnp.bfloat16)
     normed = rms_norm(stream.astype(jnp.float32), norm_gain).astype(jnp.bfloat16)
     logits = jnp.dot(normed, router_w, preferred_element_type=jnp.float32)

time: 305 us -> 296 us (0.970)
  waiting for transfers between devices: 207 us -> 193 us
  starting transfers between devices: 10.2 us -> 14.4 us
    reduce_scatter x1 -> x0, waiting for transfers between devices: 27.1 us -> none  [per_device(): lax.psum_scatter(partial, 'ty', scatter_dimension=0, tiled=True)]
    all_to_all x0 -> x1, waiting for transfers between devices: none -> 14.5 us  [per_device(): lax.all_to_all(partial, 'ty', split_axis=0, concat_axis=0, tiled=True)]
    all_to_all x0 -> x1, starting transfers between devices: none -> 4.3 us  [per_device(): lax.all_to_all(partial, 'ty', split_axis=0, concat_axis=0, tiled=True)]
where the time goes in v4:
time: 296 us; the launch traced here: 294 us
  waiting for transfers between devices  193 us (65%)
  matrix products  32.3 us (11%)
  blocking collectives  23.8 us (8%)
  starting transfers between devices  14.4 us (5%)
  between operations  14 us (5%)
  local copies, waits for them, and re-layouts  12.1 us (4%)
  other arithmetic  4.63 us (2%)
    reduce_scatter x1, waiting for transfers between devices, per_device(): partial = lax.psum_scatter(partial, 'tz', scatter_dimension=0, tiled=True)  94.3 us
    reduce_scatter x1, waiting for transfers between devices, per_device(): summed = lax.psum_scatter(down, 'expert', scatter_dimension=0, tiled=True)  40 us
    all_gather x1, waiting for transfers between devices, per_device(): arrived = lax.all_gather(exchanged, 'expert', axis=0, tiled=True)  31.1 us
    all_to_all x1, blocking collectives, per_device(): lax.all_to_all(send_rows, TENSOR, split_axis=0, concat_axis=0, tiled=True)  23.8 us
    all_to_all x1, waiting for transfers between devices, per_device(): lax.all_to_all(partial, 'ty', split_axis=0, concat_axis=0, tiled=True)  14.5 us
    all_to_all x1, waiting for transfers between devices, per_device(): lax.all_to_all(summed, TENSOR, split_axis=0, concat_axis=0, tiled=True)  12.7 us
    dot_general x1, matrix products, per_device(): jnp.dot(rows_in, w_gate_up.reshape(model_width, 2 * hidden_units), prefer...  10.6 us
    all_to_all x1, starting transfers between devices, per_device(): lax.all_to_all(summed, TENSOR, split_axis=0, concat_axis=0, tiled=True)  10.1 us
  transfers between devices with their start and end apart: 5, of which 5 were waited for; matrix products, arithmetic and copies ran while one was open for 1% of the time, Pallas kernels for 0%

profile of v4, /device:TPU:32, one launch (start us, length us, event | category | flops | bytes accessed | tf_op | source)
XLA Modules:
  0.0 293.9 jit_solution(12488470999225325126)
XLA Ops:
  7.3 0.9 fusion.35
  8.2 0.8 broadcast_subtract_fusion
  9.0 3.8 %fusion.13 = f32[512,2048]{1,0:T(8,128)} fusion(bf16[2048,128]{1,0:T(8,128)(2,1)} %param.15, s32[512]{0:T(512)S(1)} %fusion.29), kind=kOutput, calls=%fused_computation.26 | convolution fusion | flops 268566528 | bytes 4720640 | tf_op jit(solution)/shard_map/dot_general | solution.py:53
  12.8 9.8 %convolution_convert_fusion = bf16[2048,2048]{1,0:T(8,128)(2,1)} fusion(bf16[512,2048]{1,0:T(8,128)(2,1)} %bitcast.43, f32[512,2048]{1,0:T(8,128)} %fusion.13, bf16[2048,128]{1,0:T(8,128)(2,1)S(1)} %copy-done.1, f32[2048]{0:T(1024)S(1)} %bitcast.40, s32[2048]{0:T(1024)S(1)} %bitcast.39, f32[2048]{0:T(1024)S(1)} %bitcast.41, s32[2048]{0:T(1024)S(1)} %bitcast.38, ...), kind=kOutput, calls=%fused_computation.1 | convolution fusion | flops 4576116736 | bytes 15241216 | tf_op jit(solution)/shard_map/dot_general | solution.py:58
  22.7 0.6 copy-done.5
  23.3 0.1 copy.52
  23.4 0.1 convert_reduce_fusion.2
  23.5 0.1 select_reduce_fusion.4
  23.6 0.1 and_select_fusion.1
  23.8 0.1 copy.53
  23.9 0.1 eq.202
  24.0 0.1 eq.188
  24.1 0.2 convert_reduce_fusion.1
  24.3 94.3 %reduce-scatter.3.cloned.1.call-done = bf16[256,2048]{1,0:T(8,128)(2,1)} async-done(((bf16[2048,2048]{1,0:T(8,128)(2,1)}), bf16[256,2048]{1,0:T(8,128)(2,1)}) %reduce-scatter.3.cloned.1.call-update) | async-done | bytes 1048592 | tf_op jit(solution)/shard_map/reduce_scatter | solution.py:59
  118.6 4.3 %all-to-all-start = ((bf16[4,64,2048]{2,1,0:T(8,128)(2,1)}), bf16[4,64,2048]{2,1,0:T(8,128)(2,1)}, u32[]{:S(2)}, u32[]{:S(2)}) async-start(bf16[4,64,2048]{2,1,0:T(8,128)(2,1)} %bitcast.37), calls=%async_computation.1 | async-start | bytes 2097152 | tf_op jit(solution)/shard_map/all_to_all | solution.py:61
  122.9 0.1 fusion.22
  123.0 0.2 reduce_window_sum.11
  123.2 0.2 select_reduce_fusion.1
  123.3 0.1 reshape.148
  123.5 0.1 copy.54
  123.6 0.1 select_reduce_fusion.2
  123.7 0.1 fusion.23
  123.8 14.5 %all-to-all-done = bf16[4,64,2048]{2,1,0:T(8,128)(2,1)} async-done(((bf16[4,64,2048]{2,1,0:T(8,128)(2,1)}), bf16[4,64,2048]{2,1,0:T(8,128)(2,1)}, u32[]{:S(2)}, u32[]{:S(2)}) %all-to-all-start) | async-done | bytes 1048608 | tf_op jit(solution)/shard_map/all_to_all | solution.py:61
  138.3 1.4 convert_reduce_fusion
  139.8 0.2 fusion.6
  140.0 1.2 convolution_convert_fusion.2
  141.1 2.0 all_to_all.24
  143.2 23.8 %all_to_all.33 = bf16[32,4,2048]{2,1,0:T(4,128)(2,1)} all-to-all(bf16[32,4,2048]{2,1,0:T(4,128)(2,1)} %all_to_all.24), channel_id=1, replica_groups=mesh['expert'=8,'tz'=8,'ty'=4] {'tz','ty'}, dimensions={0} | all-to-all | bytes 1048576 | tf_op jit(solution)/shard_map/all_to_all | solution.py:106
  167.0 2.0 all_to_all.26
  169.0 0.0 reduce-scatter.5.cloned.1.call-start
  169.0 31.1 %all-gather.2.cloned.1.call-done = bf16[1024,2048]{1,0:T(8,128)(2,1)} async-done(((bf16[128,2048]{1,0:T(8,128)(2,1)}), bf16[1024,2048]{1,0:T(8,128)(2,1)}) %all-gather.2.cloned.1.call-update) | async-done | bytes 4194320 | tf_op jit(solution)/shard_map/all_gather | solution.py:107
  200.1 10.6 %fusion.36 = f32[1024,1408]{1,0:T(8,128)S(1)} fusion(bf16[1024,2048]{1,0:T(8,128)(2,1)} %all-gather.2.cloned.1.call-done, bf16[2048,1408]{0,1:T(8,128)(2,1)} %bitcast.42), kind=kOutput, calls=%fused_computation.80 | convolution fusion | flops 5905580032 | bytes 15728640 | tf_op jit(solution)/shard_map/dot_general | solution.py:110
  210.7 5.2 %convolution_convert_fusion.1 = bf16[1024,2048]{1,0:T(8,128)(2,1)} fusion(bf16[1,704,2048]{2,1,0:T(8,128)(2,1)S(1)} %copy-done, f32[1024,1408]{1,0:T(8,128)S(1)} %fusion.36), kind=kOutput, calls=%fused_computation.6 | convolution fusion | flops 2959212544 | bytes 13369344 | tf_op jit(solution)/shard_map/dot_general | solution.py:114
  215.9 0.1 copy.56
  216.0 0.1 reshape.152
  216.2 0.4 copy-done.6
  216.6 40.0 %reduce-scatter.5.cloned.1.call-done = bf16[128,2048]{1,0:T(8,128)(2,1)} async-done(((bf16[1024,2048]{1,0:T(8,128)(2,1)}), bf16[128,2048]{1,0:T(8,128)(2,1)}) %reduce-scatter.5.cloned.1.call-update) | async-done | bytes 524304 | tf_op jit(solution)/shard_map/reduce_scatter | solution.py:117
  256.5 2.0 all_to_all.27
  258.6 10.1 %all-to-all-start.2 = ((bf16[32,4,2048]{2,1,0:T(4,128)(2,1)}), bf16[32,4,2048]{2,1,0:T(4,128)(2,1)}, u32[]{:S(2)}, u32[]{:S(2)}) async-start(bf16[32,4,2048]{2,1,0:T(4,128)(2,1)} %all_to_all.27), calls=%async_computation.4 | async-start | bytes 1048576 | tf_op jit(solution)/shard_map/all_to_all | solution.py:118
  268.7 0.2 fusion.19
  268.9 1.0 gather_fusion
  269.9 0.1 reshape.155
  270.1 0.1 copy.57
  270.2 0.1 select_reduce_fusion
  270.3 12.7 %all-to-all-done.2 = bf16[32,4,2048]{2,1,0:T(4,128)(2,1)} async-done(((bf16[32,4,2048]{2,1,0:T(4,128)(2,1)}), bf16[32,4,2048]{2,1,0:T(4,128)(2,1)}, u32[]{:S(2)}, u32[]{:S(2)}) %all-to-all-start.2) | async-done | bytes 524320 | tf_op jit(solution)/shard_map/all_to_all | solution.py:118
  283.0 2.0 all_to_all.29
  285.0 1.5 multiply_reduce_fusion
  286.6 0.8 multiply_convert_fusion
  (34 shorter events, 0.2 us)
Async XLA Ops:
  7.2 203.5 %copy-start = (bf16[1,704,2048]{2,1,0:T(8,128)(2,1)S(1)}, bf16[1,704,2048]{2,1,0:T(8,128)(2,1)}, u32[]{:S(2)}) copy-start(bf16[1,704,2048]{2,1,0:T(8,128)(2,1)} %param.26) | copy-start | bytes 8650756
  7.2 5.6 %copy-start.1 = (bf16[2048,128]{1,0:T(8,128)(2,1)S(1)}, bf16[2048,128]{1,0:T(8,128)(2,1)}, u32[]{:S(2)}) copy-start(bf16[2048,128]{1,0:T(8,128)(2,1)} %param.15) | copy-start | bytes 1572868
  7.2 111.4 %reduce-scatter.3.cloned.1.call-start = ((), (), s32[]{:S(2)}) async-start(), calls=%async_computation.5 | async-start | bytes 9437184 | tf_op jit(solution)/shard_map/reduce_scatter | solution.py:59
  22.6 0.7 copy-start.5
  22.6 0.7 copy-start.3
  22.6 0.8 copy-start.4
  22.6 1.0 copy-start.7
  22.7 100.9 %copy-start.8 = (s32[32]{0:T(128)S(1)}, s32[32]{0:T(128)}, u32[]{:S(2)}) copy-start(s32[32]{0:T(128)} %param.24) | copy-start | bytes 388
  23.3 116.4 %copy-start.2 = (bf16[64,2048]{1,0:T(8,128)(2,1)S(1)}, bf16[64,2048]{1,0:T(8,128)(2,1)}, u32[]{:S(2)}) copy-start(bf16[64,2048]{1,0:T(8,128)(2,1)} %param.14) | copy-start | bytes 786436
  118.6 19.7 %all-to-all-start = ((bf16[4,64,2048]{2,1,0:T(8,128)(2,1)}), bf16[4,64,2048]{2,1,0:T(8,128)(2,1)}, u32[]{:S(2)}, u32[]{:S(2)}) async-start(bf16[4,64,2048]{2,1,0:T(8,128)(2,1)} %bitcast.37), calls=%async_computation.1 | async-start | bytes 2097152 | tf_op jit(solution)/shard_map/all_to_all | solution.py:61
  122.9 77.2 %all-gather.2.cloned.1.call-start = ((), (), s32[]{:S(2)}) async-start(), calls=%async_computation.6 | async-start | bytes 4718592 | tf_op jit(solution)/shard_map/all_gather | solution.py:107
  169.0 87.6 %reduce-scatter.5.cloned.1.call-start = ((), (), s32[]{:S(2)}) async-start(), calls=%async_computation.7 | async-start | bytes 4718592 | tf_op jit(solution)/shard_map/reduce_scatter | solution.py:117
  215.9 0.7 copy-start.6
  215.9 52.8 %copy-start.9 = (bf16[2048,8]{0,1:T(8,128)(2,1)S(1)}, bf16[2048,8]{0,1:T(8,128)(2,1)}, u32[]{:S(2)}) copy-start(bf16[2048,8]{0,1:T(8,128)(2,1)} %param.20) | copy-start | bytes 98308
  258.6 24.4 %all-to-all-start.2 = ((bf16[32,4,2048]{2,1,0:T(4,128)(2,1)}), bf16[32,4,2048]{2,1,0:T(4,128)(2,1)}, u32[]{:S(2)}, u32[]{:S(2)}) async-start(bf16[32,4,2048]{2,1,0:T(4,128)(2,1)} %all_to_all.27), calls=%async_computation.4 | async-start | bytes 1048576 | tf_op jit(solution)/shard_map/all_to_all | solution.py:118
Sparse Core Ops, SparseCore 0:
  22.8 95.7 reduce-scatter.2
  169.1 30.9 all-gather.1
  216.0 40.4 reduce-scatter.4

commit v5 on v4

--- a/solution.py
+++ b/solution.py
@@ -5,6 +5,7 @@
 
 MAXB = 2
 TENSOR = ("tz", "ty")
+Z_SHARE = 4
 
 
 norm_eps = 1e-06
@@ -55,11 +56,19 @@
         mixed = mixed + jnp.where(chosen, picked * gate_att[:, choice : choice + 1], 0.0)
     row_block = mixed.astype(jnp.bfloat16)
     weight_flat = att_out_w.reshape(width, model_width)
-    partial = jnp.dot(row_block, weight_flat, preferred_element_type=jnp.float32).astype(jnp.bfloat16)
-    partial = lax.psum_scatter(partial, "tz", scatter_dimension=0, tiled=True)
     n_y = lax.axis_size("ty")
-    gathered = lax.all_to_all(partial, "ty", split_axis=0, concat_axis=0, tiled=True)
-    attention = jnp.sum(gathered.reshape(n_y, -1, model_width).astype(jnp.float32), axis=0)
+    n_z = lax.axis_size("tz")
+    split = model_width * Z_SHARE // 8
+    z_first = jnp.dot(row_block, weight_flat[:, :split], preferred_element_type=jnp.float32)
+    z_first = lax.psum_scatter(z_first.astype(jnp.bfloat16), "tz", scatter_dimension=0, tiled=True)
+    z_first = lax.all_to_all(z_first, "ty", split_axis=0, concat_axis=0, tiled=True)
+    z_first = jnp.sum(z_first.reshape(n_y, -1, split).astype(jnp.float32), axis=0)
+    by_y = row_block.reshape(n_z, n_y, -1, width).transpose(1, 0, 2, 3).reshape(group_rows, width)
+    y_first = jnp.dot(by_y, weight_flat[:, split:], preferred_element_type=jnp.float32)
+    y_first = lax.all_to_all(y_first.astype(jnp.bfloat16), "ty", split_axis=0, concat_axis=0, tiled=True)
+    y_first = jnp.sum(y_first.reshape(n_y, -1, model_width - split).astype(jnp.float32), axis=0)
+    y_first = lax.psum_scatter(y_first.astype(jnp.bfloat16), "tz", scatter_dimension=0, tiled=True)
+    attention = jnp.concatenate([z_first, y_first.astype(jnp.float32)], axis=1)
     stream = (resid.astype(jnp.float32) + attention).astype(jnp.bfloat16)
     normed = rms_norm(stream.astype(jnp.float32), norm_gain).astype(jnp.bfloat16)
     logits = jnp.dot(normed, router_w, preferred_element_type=jnp.float32)

time: 296 us -> 280 us (0.946)
  waiting for transfers between devices: 193 us -> 117 us
  blocking collectives: 23.8 us -> 74.5 us
  local copies, waits for them, and re-layouts: 12.1 us -> 19 us
  other arithmetic: 4.63 us -> 10.4 us
  matrix products: 32.3 us -> 28.7 us
    reduce_scatter x1 -> x2, waiting for transfers between devices: 94.3 us -> 33.3 us  [the longest x1 33.3 us: per_device(): lax.psum_scatter(y_first.astype(jnp.bfloat16), 'tz', scatter_dimension=0,...]
    all_to_all x0 -> x1, blocking collectives: none -> 53.2 us  [per_device(): lax.all_to_all(y_first.astype(jnp.bfloat16), 'ty', split_axis=0, concat_a...]
    all_to_all x1, waiting for transfers between devices: 14.5 us -> 0.01 us  [per_device(): lax.all_to_all(z_first, 'ty', split_axis=0, concat_axis=0, tiled=True)]
    convert_element_type x0 -> x1, local copies, waits for them, and re-layouts: none -> 3.94 us  [per_device(): row_block = mixed.astype(jnp.bfloat16)]
    dot_general x1 -> x2, matrix products: 9.84 us -> 6.67 us  [the longest x1 4.33 us: per_device(): jnp.dot(row_block, weight_flat[:, :split], preferred_element_type=jnp.flo...]
    reduce_sum x1 -> x2, other arithmetic: 1.43 us -> 4.57 us  [the longest x1 4.49 us: per_device(): jnp.sum(y_first.reshape(n_y, -1, model_width - split).astype(jnp.float32)...]
  transfers between devices with their start and end apart: 5 -> 6, of which waited for: 5 -> 4; matrix products, arithmetic and copies ran while one was open for 1% -> 6% of each run, Pallas kernels for 0% -> 0%
where the time goes in v5:
time: 280 us; the launch traced here: 277 us
  waiting for transfers between devices  117 us (42%)
  blocking collectives  74.5 us (27%)
  matrix products  28.7 us (10%)
  local copies, waits for them, and re-layouts  19 us (7%)
  starting transfers between devices  14.1 us (5%)
  between operations  14.1 us (5%)
  other arithmetic  10.4 us (4%)
    all_to_all x1, blocking collectives, per_device(): lax.all_to_all(y_first.astype(jnp.bfloat16), 'ty', split_axis=0, concat_a...  53.2 us
    reduce_scatter x1, waiting for transfers between devices, per_device(): summed = lax.psum_scatter(down, 'expert', scatter_dimension=0, tiled=True)  39.9 us
    reduce_scatter x1, waiting for transfers between devices, per_device(): lax.psum_scatter(y_first.astype(jnp.bfloat16), 'tz', scatter_dimension=0,...  33.3 us
    all_gather x1, waiting for transfers between devices, per_device(): arrived = lax.all_gather(exchanged, 'expert', axis=0, tiled=True)  30.7 us
    all_to_all x1, blocking collectives, per_device(): lax.all_to_all(send_rows, TENSOR, split_axis=0, concat_axis=0, tiled=True)  21.4 us
    all_to_all x1, waiting for transfers between devices, per_device(): lax.all_to_all(summed, TENSOR, split_axis=0, concat_axis=0, tiled=True)  12.7 us
    dot_general x1, matrix products, per_device(): jnp.dot(rows_in, w_gate_up.reshape(model_width, 2 * hidden_units), prefer...  10.6 us
    all_to_all x1, starting transfers between devices, per_device(): lax.all_to_all(summed, TENSOR, split_axis=0, concat_axis=0, tiled=True)  10.2 us
  transfers between devices with their start and end apart: 6, of which 4 were waited for; matrix products, arithmetic and copies ran while one was open for 6% of the time, Pallas kernels for 0%

profile of v5, /device:TPU:32, one launch (start us, length us, event | category | flops | bytes accessed | tf_op | source)
XLA Modules:
  0.0 277.5 jit_solution(7883541028345914010)
XLA Ops:
  7.3 0.9 fusion.36
  8.2 0.8 broadcast_subtract_fusion
  9.0 1.8 fusion.15
  10.8 1.5 fusion.1
  12.4 1.3 copy-done.1
  13.7 4.3 %convolution_convert_fusion.2 = bf16[2048,1024]{1,0:T(8,128)(2,1)} fusion(bf16[2048,512]{0,1:T(8,128)(2,1)S(1)} %fusion.1, bf16[512,2048]{1,0:T(8,128)(2,1)S(1)} %bitcast.48), kind=kOutput, calls=%fused_computation.7 | convolution fusion | flops 2149580800 | bytes 7340032 | tf_op jit(solution)/shard_map/dot_general | solution.py:62
  18.1 3.9 %copy.56 = bf16[2048,512]{1,0:T(8,128)(2,1)} copy(bf16[2048,512]{0,1:T(8,128)(2,1)} %copy-done.1) | data formatting | bytes 4194304 | tf_op jit(solution)/shard_map/convert_element_type | solution.py:57
  22.1 1.9 copy.57
  24.0 0.3 copy-done.10
  24.3 2.3 convolution_convert_fusion.1
  26.6 53.2 %all_to_all.42 = bf16[4,512,1024]{2,1,0:T(8,128)(2,1)} all-to-all(bf16[4,512,1024]{2,1,0:T(8,128)(2,1)S(1)} %bitcast.40), channel_id=1, replica_groups=mesh['expert'=8,'tz'=8,'ty'=4] {'ty'}, dimensions={0} | all-to-all | bytes 8388608 | tf_op jit(solution)/shard_map/all_to_all | solution.py:68
  79.8 4.5 %reduce_sum.115 = bf16[512,1024]{1,0:T(8,128)(2,1)} reduce(bf16[4,512,1024]{2,1,0:T(8,128)(2,1)} %all_to_all.42, bf16[]{:T(256)} %constant.107.clone.1), dimensions={0}, to_apply=%region_2.3 | reduce | flops 1572864 | bytes 5242882 | tf_op jit(solution)/shard_map/reduce_sum | solution.py:69
  84.4 0.1 copy.58
  84.5 0.1 convert_reduce_fusion.2
  84.7 0.1 and_select_fusion.1
  84.9 0.1 eq.202
  85.0 0.1 eq.188
  85.2 0.2 convert_reduce_fusion.1
  85.3 0.1 fusion.23
  85.5 0.2 reduce_window_sum.11
  85.6 0.2 select_reduce_fusion.1
  85.8 3.5 %all-to-all-start = ((bf16[4,64,1024]{2,1,0:T(8,128)(2,1)}), bf16[4,64,1024]{2,1,0:T(8,128)(2,1)S(1)}, u32[]{:S(2)}, u32[]{:S(2)}) async-start(bf16[4,64,1024]{2,1,0:T(8,128)(2,1)} %bitcast.42), calls=%async_computation.1 | async-start | bytes 1048576 | tf_op jit(solution)/shard_map/all_to_all | solution.py:64
  89.5 0.1 reshape.160
  89.7 0.1 fusion.24
  89.8 33.3 %reduce-scatter.6.cloned.1.call-done = bf16[64,1024]{1,0:T(8,128)(2,1)} async-done(((bf16[512,1024]{1,0:T(8,128)(2,1)}), bf16[64,1024]{1,0:T(8,128)(2,1)}) %reduce-scatter.6.cloned.1.call-update) | async-done | bytes 131088 | tf_op jit(solution)/shard_map/reduce_scatter | solution.py:70
  123.2 1.6 convert_element_type.76
  124.9 1.2 fusion.8
  126.1 1.2 convolution_convert_fusion.3
  127.3 2.0 all_to_all.32
  129.3 21.4 %all_to_all.43 = bf16[32,4,2048]{2,1,0:T(4,128)(2,1)} all-to-all(bf16[32,4,2048]{2,1,0:T(4,128)(2,1)} %all_to_all.32), channel_id=1, replica_groups=mesh['expert'=8,'tz'=8,'ty'=4] {'tz','ty'}, dimensions={0} | all-to-all | bytes 1048576 | tf_op jit(solution)/shard_map/all_to_all | solution.py:115
  150.7 2.0 all_to_all.34
  152.6 0.2 reduce-scatter.8.cloned.1.call-start
  152.9 30.7 %all-gather.2.cloned.1.call-done = bf16[1024,2048]{1,0:T(8,128)(2,1)} async-done(((bf16[128,2048]{1,0:T(8,128)(2,1)}), bf16[1024,2048]{1,0:T(8,128)(2,1)}) %all-gather.2.cloned.1.call-update) | async-done | bytes 4194320 | tf_op jit(solution)/shard_map/all_gather | solution.py:116
  183.6 10.6 %fusion.37 = f32[1024,1408]{1,0:T(8,128)S(1)} fusion(bf16[1024,2048]{1,0:T(8,128)(2,1)} %all-gather.2.cloned.1.call-done, bf16[2048,1408]{0,1:T(8,128)(2,1)} %bitcast.47), kind=kOutput, calls=%fused_computation.83 | convolution fusion | flops 5905580032 | bytes 15728640 | tf_op jit(solution)/shard_map/dot_general | solution.py:119
  194.1 5.2 %convolution_convert_fusion = bf16[1024,2048]{1,0:T(8,128)(2,1)} fusion(bf16[1,704,2048]{2,1,0:T(8,128)(2,1)S(1)} %copy-done, f32[1024,1408]{1,0:T(8,128)S(1)} %fusion.37), kind=kOutput, calls=%fused_computation.5 | convolution fusion | flops 2959212544 | bytes 13369344 | tf_op jit(solution)/shard_map/dot_general | solution.py:123
  199.5 0.1 reshape.164
  199.6 0.4 copy-done.6
  200.0 39.9 %reduce-scatter.8.cloned.1.call-done = bf16[128,2048]{1,0:T(8,128)(2,1)} async-done(((bf16[1024,2048]{1,0:T(8,128)(2,1)}), bf16[128,2048]{1,0:T(8,128)(2,1)}) %reduce-scatter.8.cloned.1.call-update) | async-done | bytes 524304 | tf_op jit(solution)/shard_map/reduce_scatter | solution.py:126
  239.9 2.0 all_to_all.35
  241.9 10.2 %all-to-all-start.3 = ((bf16[32,4,2048]{2,1,0:T(4,128)(2,1)}), bf16[32,4,2048]{2,1,0:T(4,128)(2,1)}, u32[]{:S(2)}, u32[]{:S(2)}) async-start(bf16[32,4,2048]{2,1,0:T(4,128)(2,1)} %all_to_all.35), calls=%async_computation.6 | async-start | bytes 1048576 | tf_op jit(solution)/shard_map/all_to_all | solution.py:127
  252.2 0.2 fusion.20
  252.4 1.0 gather_fusion
  253.5 0.1 reshape.167
  253.7 0.1 select_reduce_fusion
  253.8 12.7 %all-to-all-done.3 = bf16[32,4,2048]{2,1,0:T(4,128)(2,1)} async-done(((bf16[32,4,2048]{2,1,0:T(4,128)(2,1)}), bf16[32,4,2048]{2,1,0:T(4,128)(2,1)}, u32[]{:S(2)}, u32[]{:S(2)}) %all-to-all-start.3) | async-done | bytes 524320 | tf_op jit(solution)/shard_map/all_to_all | solution.py:127
  266.6 2.0 all_to_all.37
  268.5 1.6 multiply_reduce_fusion
  270.1 0.8 multiply_convert_fusion
  (48 shorter events, 0.9 us)
Async XLA Ops:
  7.2 187.0 %copy-start = (bf16[1,704,2048]{2,1,0:T(8,128)(2,1)S(1)}, bf16[1,704,2048]{2,1,0:T(8,128)(2,1)}, u32[]{:S(2)}) copy-start(bf16[1,704,2048]{2,1,0:T(8,128)(2,1)} %param.26) | copy-start | bytes 8650756
  7.2 3.6 %copy-start.2 = (bf16[2048,128]{1,0:T(8,128)(2,1)S(1)}, bf16[2048,128]{1,0:T(8,128)(2,1)}, u32[]{:S(2)}) copy-start(bf16[2048,128]{1,0:T(8,128)(2,1)} %param.15) | copy-start | bytes 1572868
  7.2 78.6 %reduce-scatter.4.cloned.1.call-start = ((), (), s32[]{:S(2)}) async-start(), calls=%async_computation.7 | async-start | bytes 4718592 | tf_op jit(solution)/shard_map/reduce_scatter | solution.py:63
  10.8 2.9 %copy-start.9 = (bf16[8,64,2048]{2,1,0:T(8,128)(2,1)S(1)}, bf16[8,64,2048]{2,1,0:T(8,128)(2,1)}, u32[]{:S(2)}) copy-start(bf16[8,64,2048]{2,1,0:T(8,128)(2,1)} %param.18) | copy-start | bytes 6291460
  12.4 1.3 copy-start.1
  18.1 105.1 %reduce-scatter.6.cloned.1.call-start = ((), (), s32[]{:S(2)}) async-start(), calls=%async_computation.8 | async-start | bytes 1179648 | tf_op jit(solution)/shard_map/reduce_scatter | solution.py:70
  22.1 2.2 copy-start.10
  79.8 4.5 %copy-start.3 = (s32[64,2]{0,1:T(2,128)S(1)}, s32[64,2]{0,1:T(2,128)}, u32[]{:S(2)}) copy-start(s32[64,2]{0,1:T(2,128)} %param.21) | copy-start | bytes 1540
  79.8 4.6 %copy-start.4 = (s32[32]{0:T(128)S(1)}, s32[32]{0:T(128)}, u32[]{:S(2)}) copy-start(s32[32]{0:T(128)} %param.23) | copy-start | bytes 388
  79.8 4.8 %copy-start.7 = (s32[64,2]{0,1:T(2,128)S(1)}, s32[64,2]{0,1:T(2,128)}, u32[]{:S(2)}) copy-start(s32[64,2]{0,1:T(2,128)} %param.22) | copy-start | bytes 1540
  79.8 9.6 %copy-start.8 = (s32[32]{0:T(128)S(1)}, s32[32]{0:T(128)}, u32[]{:S(2)}) copy-start(s32[32]{0:T(128)} %param.24) | copy-start | bytes 388
  79.8 9.7 %copy-start.5 = (bf16[2048]{0:T(1024)(128)(2,1)S(1)}, bf16[2048]{0:T(1024)(128)(2,1)}, u32[]{:S(2)}) copy-start(bf16[2048]{0:T(1024)(128)(2,1)} %param.19) | copy-start | bytes 12292
  85.8 38.9 %all-to-all-start = ((bf16[4,64,1024]{2,1,0:T(8,128)(2,1)}), bf16[4,64,1024]{2,1,0:T(8,128)(2,1)S(1)}, u32[]{:S(2)}, u32[]{:S(2)}) async-start(bf16[4,64,1024]{2,1,0:T(8,128)(2,1)} %bitcast.42), calls=%async_computation.1 | async-start | bytes 1048576 | tf_op jit(solution)/shard_map/all_to_all | solution.py:64
  89.3 94.2 %all-gather.2.cloned.1.call-start = ((), (), s32[]{:S(2)}) async-start(), calls=%async_computation.9 | async-start | bytes 4718592 | tf_op jit(solution)/shard_map/all_gather | solution.py:116
  152.6 87.3 %reduce-scatter.8.cloned.1.call-start = ((), (), s32[]{:S(2)}) async-start(), calls=%async_computation.10 | async-start | bytes 4718592 | tf_op jit(solution)/shard_map/reduce_scatter | solution.py:126
  199.3 0.7 copy-start.6
  199.3 52.8 %copy-start.11 = (bf16[2048,8]{0,1:T(8,128)(2,1)S(1)}, bf16[2048,8]{0,1:T(8,128)(2,1)}, u32[]{:S(2)}) copy-start(bf16[2048,8]{0,1:T(8,128)(2,1)} %param.20) | copy-start | bytes 98308
  241.9 24.6 %all-to-all-start.3 = ((bf16[32,4,2048]{2,1,0:T(4,128)(2,1)}), bf16[32,4,2048]{2,1,0:T(4,128)(2,1)}, u32[]{:S(2)}, u32[]{:S(2)}) async-start(bf16[32,4,2048]{2,1,0:T(4,128)(2,1)} %all_to_all.35), calls=%async_computation.6 | async-start | bytes 1048576 | tf_op jit(solution)/shard_map/all_to_all | solution.py:127
Sparse Core Ops, SparseCore 0:
  18.2 56.1 reduce-scatter.3
  84.5 38.6 reduce-scatter.5
  152.8 30.7 all-gather.1
  199.5 40.3 reduce-scatter.7

commit v6 on v5

--- a/solution.py
+++ b/solution.py
@@ -5,6 +5,8 @@
 
 MAXB = 2
 TENSOR = ("tz", "ty")
+EXPERT = ("ex", "ec")
+ALL = ("ex", "ec", "tz", "ty")
 Z_SHARE = 4
 
 
@@ -113,17 +115,23 @@
     )
     send_rows = jnp.dot(placer, normed, preferred_element_type=jnp.float32).astype(jnp.bfloat16)
     exchanged = lax.all_to_all(send_rows, TENSOR, split_axis=0, concat_axis=0, tiled=True)
-    arrived = lax.all_gather(exchanged, "expert", axis=0, tiled=True)
+    arrived = lax.all_gather(exchanged, "ex", axis=0, tiled=True)
+    swap = [(0, 1), (1, 0)]
+    paired_gate_up = lax.ppermute(w_gate_up, "ec", swap)
+    paired_down = lax.ppermute(w_down, "ec", swap)
     hidden_units = w_gate_up.shape[3]
-    rows_in = arrived.reshape(-1, model_width)
-    both = jnp.dot(
-        rows_in, w_gate_up.reshape(model_width, 2 * hidden_units), preferred_element_type=jnp.float32
-    )
-    hidden = (jax.nn.silu(both[:, :hidden_units]) * both[:, hidden_units:]).astype(jnp.bfloat16)
-    down = jnp.dot(
-        hidden, w_down.reshape(hidden_units, model_width), preferred_element_type=jnp.float32
-    ).astype(jnp.bfloat16)
-    summed = lax.psum_scatter(down, "expert", scatter_dimension=0, tiled=True)
+
+    def expert_part(gate_up, down_w):
+        both = jnp.dot(
+            arrived, gate_up.reshape(model_width, 2 * hidden_units), preferred_element_type=jnp.float32
+        )
+        hidden = (jax.nn.silu(both[:, :hidden_units]) * both[:, hidden_units:]).astype(jnp.bfloat16)
+        return jnp.dot(
+            hidden, down_w.reshape(hidden_units, model_width), preferred_element_type=jnp.float32
+        )
+
+    down = expert_part(w_gate_up, w_down) + expert_part(paired_gate_up, paired_down)
+    summed = lax.psum_scatter(down.astype(jnp.bfloat16), "ex", scatter_dimension=0, tiled=True)
     flat_back = lax.all_to_all(summed, TENSOR, split_axis=0, concat_axis=0, tiled=True)
     back_index = jnp.where(is_kept, holder * (capacity_rows * slots) + arrival * slots + within, 0)
     factors = gate_mlp * is_kept.astype(jnp.float32)
@@ -147,7 +155,8 @@
 def split_mesh(mesh):
     n_expert, n_tensor = mesh.devices.shape
     n_y = 4 if n_tensor % 4 == 0 else 1
-    return Mesh(mesh.devices.reshape(n_expert, n_tensor // n_y, n_y), ("expert", "tz", "ty"))
+    shape = (n_expert // 2, 2, n_tensor // n_y, n_y)
+    return Mesh(mesh.devices.reshape(shape), ALL)
 
 
 def solution(mesh):
@@ -156,21 +165,21 @@
         per_device,
         mesh=mesh,
         in_specs=(
-            P(("expert", "tz", "ty"), None),
-            P("expert", TENSOR),
-            P("expert", None),
-            P("expert", None),
+            P(ALL, None),
+            P(EXPERT, TENSOR),
+            P(EXPERT, None),
+            P(EXPERT, None),
             P(None, TENSOR, None),
             P(),
             P(),
-            P(("expert", "tz", "ty"), None),
-            P(("expert", "tz", "ty"), None),
+            P(ALL, None),
+            P(ALL, None),
             P(),
             P(),
-            P(TENSOR, None, None, "expert"),
-            P(TENSOR, "expert", None),
+            P(TENSOR, None, None, EXPERT),
+            P(TENSOR, EXPERT, None),
             P(),
         ),
-        out_specs=(P(("expert", "tz", "ty"), None), P(("expert", "tz", "ty"), None)),
+        out_specs=(P(ALL, None), P(ALL, None)),
         check_vma=False,
     )

time: 280 us -> 264 us (0.943)
  local copies, waits for them, and re-layouts: 19 us -> 12 us
  waiting for transfers between devices: 117 us -> 110 us
    reduce_scatter x1, waiting for transfers between devices: 39.9 us -> 32.1 us  [per_device(): lax.psum_scatter(down.astype(jnp.bfloat16), 'ex', scatter_dimension=0, ti...]
    dot_general x2 -> x4, matrix products: 15.7 us -> 19.5 us  [the longest x2 12.4 us: expert_part(): jnp.dot(arrived, gate_up.reshape(model_width, 2 * hidden_units), preferre...]
    all_to_all x2, local copies, waits for them, and re-layouts: 3.98 us -> 1.11 us  [per_device(): lax.all_to_all(send_rows, TENSOR, split_axis=0, concat_axis=0, tiled=True)]
    all_to_all x1, waiting for transfers between devices: 12.7 us -> 15.6 us  [per_device(): lax.all_to_all(summed, TENSOR, split_axis=0, concat_axis=0, tiled=True)]
  transfers between devices with their start and end apart: 6 -> 8, of which waited for: 4 -> 4; matrix products, arithmetic and copies ran while one was open for 6% -> 11% of each run, Pallas kernels for 0% -> 0%
where the time goes in v6:
time: 264 us; the launch traced here: 263 us
  waiting for transfers between devices  110 us (42%)
  blocking collectives  74.1 us (28%)
  matrix products  29.6 us (11%)
  between operations  14.2 us (5%)
  starting transfers between devices  14.1 us (5%)
  local copies, waits for them, and re-layouts  12 us (5%)
  other arithmetic  8.63 us (3%)
    all_to_all x1, blocking collectives, per_device(): lax.all_to_all(y_first.astype(jnp.bfloat16), 'ty', split_axis=0, concat_a...  53.2 us
    reduce_scatter x1, waiting for transfers between devices, per_device(): lax.psum_scatter(y_first.astype(jnp.bfloat16), 'tz', scatter_dimension=0,...  33.3 us
    reduce_scatter x1, waiting for transfers between devices, per_device(): lax.psum_scatter(down.astype(jnp.bfloat16), 'ex', scatter_dimension=0, ti...  32.1 us
    all_gather x1, waiting for transfers between devices, per_device(): arrived = lax.all_gather(exchanged, 'ex', axis=0, tiled=True)  29.3 us
    all_to_all x1, blocking collectives, per_device(): lax.all_to_all(send_rows, TENSOR, split_axis=0, concat_axis=0, tiled=True)  21 us
    all_to_all x1, waiting for transfers between devices, per_device(): lax.all_to_all(summed, TENSOR, split_axis=0, concat_axis=0, tiled=True)  15.6 us
    dot_general x2, matrix products, expert_part(): jnp.dot(arrived, gate_up.reshape(model_width, 2 * hidden_units), preferre...  12.4 us
    all_to_all x1, starting transfers between devices, per_device(): lax.all_to_all(summed, TENSOR, split_axis=0, concat_axis=0, tiled=True)  10.1 us
  transfers between devices with their start and end apart: 8, of which 4 were waited for; matrix products, arithmetic and copies ran while one was open for 11% of the time, Pallas kernels for 0%

profile of v6, /device:TPU:32, one launch (start us, length us, event | category | flops | bytes accessed | tf_op | source)
XLA Modules:
  0.0 263.1 jit_solution(8024055861332591138)
XLA Ops:
  7.2 0.8 fusion.42
  8.1 0.8 broadcast_subtract_fusion
  8.9 0.7 fusion.20
  9.7 1.5 fusion.1
  11.2 1.3 copy-done.1
  12.6 4.4 %convolution_convert_fusion.1 = bf16[2048,1024]{1,0:T(8,128)(2,1)} fusion(bf16[2048,512]{0,1:T(8,128)(2,1)S(1)} %fusion.1, bf16[512,2048]{1,0:T(8,128)(2,1)S(1)} %bitcast.54), kind=kOutput, calls=%fused_computation.7 | convolution fusion | flops 2149580800 | bytes 7340032 | tf_op jit(solution)/shard_map/dot_general | solution.py:64
  17.1 2.9 %copy.56 = bf16[2048,512]{1,0:T(8,128)(2,1)S(1)} copy(bf16[2048,512]{0,1:T(8,128)(2,1)} %copy-done.1) | data formatting | bytes 4194304 | tf_op jit(solution)/shard_map/convert_element_type | solution.py:59
  19.9 0.2 copy.57
  20.2 1.4 copy-done.11
  21.5 2.3 convolution_convert_fusion
  23.9 53.2 %all_to_all.42 = bf16[4,512,1024]{2,1,0:T(8,128)(2,1)} all-to-all(bf16[4,512,1024]{2,1,0:T(8,128)(2,1)S(1)} %bitcast.46), channel_id=1, replica_groups=mesh['ex'=4,'ec'=2,'tz'=8,'ty'=4] {'ty'}, dimensions={0} | all-to-all | bytes 8388608 | tf_op jit(solution)/shard_map/all_to_all | solution.py:70
  77.1 4.4 %reduce_sum.115 = bf16[512,1024]{1,0:T(8,128)(2,1)} reduce(bf16[4,512,1024]{2,1,0:T(8,128)(2,1)} %all_to_all.42, bf16[]{:T(256)} %constant.108.clone.1), dimensions={0}, to_apply=%region_2.3 | reduce | flops 1572864 | bytes 5242882 | tf_op jit(solution)/shard_map/reduce_sum | solution.py:71
  81.6 0.1 copy.58
  81.7 0.1 convert_reduce_fusion.2
  81.9 0.1 and_select_fusion.1
  82.2 0.1 eq.202
  82.3 0.1 eq.188
  82.4 0.2 convert_reduce_fusion.1
  82.6 0.1 fusion.28
  82.7 0.2 reduce_window_sum.11
  82.9 0.2 select_reduce_fusion.1
  83.1 3.5 %all-to-all-start = ((bf16[4,64,1024]{2,1,0:T(8,128)(2,1)}), bf16[4,64,1024]{2,1,0:T(8,128)(2,1)S(1)}, u32[]{:S(2)}, u32[]{:S(2)}) async-start(bf16[4,64,1024]{2,1,0:T(8,128)(2,1)} %bitcast.48), calls=%async_computation.1 | async-start | bytes 1048576 | tf_op jit(solution)/shard_map/all_to_all | solution.py:66
  86.8 0.1 reshape.166
  87.1 33.3 %reduce-scatter.6.cloned.1.call-done = bf16[64,1024]{1,0:T(8,128)(2,1)} async-done(((bf16[512,1024]{1,0:T(8,128)(2,1)}), bf16[64,1024]{1,0:T(8,128)(2,1)}) %reduce-scatter.6.cloned.1.call-update) | async-done | bytes 131088 | tf_op jit(solution)/shard_map/reduce_scatter | solution.py:72
  120.4 0.9 convert_element_type.79
  121.4 0.2 fusion.13
  121.6 0.4 convolution_convert_fusion.2
  122.0 0.2 all_to_all.32
  122.2 21.0 %all_to_all.43 = bf16[32,4,2048]{2,1,0:T(4,128)(2,1)S(1)} all-to-all(bf16[32,4,2048]{2,1,0:T(4,128)(2,1)S(1)} %all_to_all.32), channel_id=1, replica_groups=mesh['ex'=4,'ec'=2,'tz'=8,'ty'=4] {'tz','ty'}, dimensions={0} | all-to-all | bytes 1048576 | tf_op jit(solution)/shard_map/all_to_all | solution.py:117
  143.1 0.9 all_to_all.34
  144.1 0.3 collective-permute-start.1
  144.4 29.3 %all-gather.2.cloned.1.call-done = bf16[512,2048]{1,0:T(8,128)(2,1)} async-done(((bf16[128,2048]{1,0:T(8,128)(2,1)}), bf16[512,2048]{1,0:T(8,128)(2,1)}) %all-gather.2.cloned.1.call-update) | async-done | bytes 2097168 | tf_op jit(solution)/shard_map/all_gather | solution.py:118
  173.7 6.6 %fusion.43 = f32[512,1408]{1,0:T(8,128)S(1)} fusion(bf16[512,2048]{1,0:T(8,128)(2,1)} %all-gather.2.cloned.1.call-done, bf16[2048,1408]{0,1:T(8,128)(2,1)} %bitcast.53), kind=kOutput, calls=%fused_computation.89 | convolution fusion | flops 2952790016 | bytes 10747904 | tf_op jit(solution)/shard_map/dot_general | solution.py:125
  180.4 1.9 fusion.3
  182.3 5.8 %fusion.44 = f32[512,1408]{1,0:T(8,128)S(1)} fusion(bf16[512,2048]{1,0:T(8,128)(2,1)S(1)} %copy-done.12, bf16[2048,1408]{0,1:T(8,128)(2,1)} %bitcast.15), kind=kOutput, calls=%fused_computation.90 | convolution fusion | flops 2952790016 | bytes 10747904 | tf_op jit(solution)/shard_map/dot_general | solution.py:125
  188.2 5.1 %add_convert_fusion = bf16[512,2048]{1,0:T(8,128)(2,1)} fusion(f32[512,2048]{1,0:T(8,128)S(1)} %fusion.3, bf16[1,704,2048]{2,1,0:T(8,128)(2,1)} %collective-permute-done.1, f32[512,1408]{1,0:T(8,128)S(1)} %fusion.44), kind=kOutput, calls=%fused_computation.5 | convolution fusion | flops 1480654848 | bytes 12320768 | tf_op jit(solution)/shard_map/dot_general | solution.py:129
  193.4 0.1 reshape.172
  193.6 32.1 %reduce-scatter.8.cloned.1.call-done = bf16[128,2048]{1,0:T(8,128)(2,1)} async-done(((bf16[512,2048]{1,0:T(8,128)(2,1)}), bf16[128,2048]{1,0:T(8,128)(2,1)}) %reduce-scatter.8.cloned.1.call-update) | async-done | bytes 524304 | tf_op jit(solution)/shard_map/reduce_scatter | solution.py:134
  225.7 2.0 all_to_all.35
  227.8 10.1 %all-to-all-start.3 = ((bf16[32,4,2048]{2,1,0:T(4,128)(2,1)}), bf16[32,4,2048]{2,1,0:T(4,128)(2,1)S(1)}, u32[]{:S(2)}, u32[]{:S(2)}) async-start(bf16[32,4,2048]{2,1,0:T(4,128)(2,1)} %all_to_all.35), calls=%async_computation.6 | async-start | bytes 1048576 | tf_op jit(solution)/shard_map/all_to_all | solution.py:135
  237.9 0.2 fusion.25
  238.1 1.0 gather_fusion
  239.1 0.1 reshape.175
  239.4 0.1 select_reduce_fusion
  239.5 15.6 %all-to-all-done.3 = bf16[32,4,2048]{2,1,0:T(4,128)(2,1)S(1)} async-done(((bf16[32,4,2048]{2,1,0:T(4,128)(2,1)}), bf16[32,4,2048]{2,1,0:T(4,128)(2,1)S(1)}, u32[]{:S(2)}, u32[]{:S(2)}) %all-to-all-start.3) | async-done | bytes 524320 | tf_op jit(solution)/shard_map/all_to_all | solution.py:135
  255.1 0.1 all_to_all.37
  255.2 0.5 multiply_reduce_fusion
  255.8 0.8 multiply_convert_fusion
  (58 shorter events, 1.2 us)
Async XLA Ops:
  7.2 1.7 copy-start
  7.2 75.9 %reduce-scatter.4.cloned.1.call-start = ((), (), s32[]{:S(2)}) async-start(), calls=%async_computation.7 | async-start | bytes 4718592 | tf_op jit(solution)/shard_map/reduce_scatter | solution.py:65
  9.6 2.9 %copy-start.10 = (bf16[8,64,2048]{2,1,0:T(8,128)(2,1)S(1)}, bf16[8,64,2048]{2,1,0:T(8,128)(2,1)}, u32[]{:S(2)}) copy-start(bf16[8,64,2048]{2,1,0:T(8,128)(2,1)} %param.18) | copy-start | bytes 6291460
  11.2 1.4 copy-start.1
  17.0 103.4 %reduce-scatter.6.cloned.1.call-start = ((), (), s32[]{:S(2)}) async-start(), calls=%async_computation.8 | async-start | bytes 1179648 | tf_op jit(solution)/shard_map/reduce_scatter | solution.py:72
  19.9 1.6 copy-start.11
  77.0 4.6 %copy-start.3 = (s32[64,2]{0,1:T(2,128)S(1)}, s32[64,2]{0,1:T(2,128)}, u32[]{:S(2)}) copy-start(s32[64,2]{0,1:T(2,128)} %param.21) | copy-start | bytes 1540
  77.0 4.7 %copy-start.4 = (s32[32]{0:T(128)S(1)}, s32[32]{0:T(128)}, u32[]{:S(2)}) copy-start(s32[32]{0:T(128)} %param.23) | copy-start | bytes 388
  77.0 4.9 %copy-start.7 = (s32[64,2]{0,1:T(2,128)S(1)}, s32[64,2]{0,1:T(2,128)}, u32[]{:S(2)}) copy-start(s32[64,2]{0,1:T(2,128)} %param.22) | copy-start | bytes 1540
  77.0 9.6 %copy-start.8 = (s32[32]{0:T(128)S(1)}, s32[32]{0:T(128)}, u32[]{:S(2)}) copy-start(s32[32]{0:T(128)} %param.24) | copy-start | bytes 388
  77.0 9.9 %copy-start.5 = (bf16[2048]{0:T(1024)(128)(2,1)S(1)}, bf16[2048]{0:T(1024)(128)(2,1)}, u32[]{:S(2)}) copy-start(bf16[2048]{0:T(1024)(128)(2,1)} %param.19) | copy-start | bytes 12292
  81.5 39.9 %copy-start.2 = (bf16[64,2048]{1,0:T(8,128)(2,1)S(1)}, bf16[64,2048]{1,0:T(8,128)(2,1)}, u32[]{:S(2)}) copy-start(bf16[64,2048]{1,0:T(8,128)(2,1)} %param.14) | copy-start | bytes 786436
  81.5 100.8 %collective-permute-start = (bf16[1,2048,2,704]{1,3,2,0:T(8,128)(2,1)}, bf16[1,2048,2,704]{1,3,2,0:T(8,128)(2,1)}, u32[]{:S(2)}, u32[]{:S(2)}) collective-permute-start(bf16[1,2048,2,704]{1,3,2,0:T(8,128)(2,1)} %param.25), channel_id=1, source_target_pairs={{0,32},{32,0},{1,33},{33,1},{2,34},{34,2},{3,35},{35,3},{4,36},{36... | collective-permute-start | bytes 17301512 | tf_op jit(solution)/shard_map/ppermute | solution.py:120
  83.1 38.2 %all-to-all-start = ((bf16[4,64,1024]{2,1,0:T(8,128)(2,1)}), bf16[4,64,1024]{2,1,0:T(8,128)(2,1)S(1)}, u32[]{:S(2)}, u32[]{:S(2)}) async-start(bf16[4,64,1024]{2,1,0:T(8,128)(2,1)} %bitcast.48), calls=%async_computation.1 | async-start | bytes 1048576 | tf_op jit(solution)/shard_map/all_to_all | solution.py:66
  86.6 87.1 %all-gather.2.cloned.1.call-start = ((), (), s32[]{:S(2)}) async-start(), calls=%async_computation.9 | async-start | bytes 2621440 | tf_op jit(solution)/shard_map/all_gather | solution.py:118
  144.1 81.7 %reduce-scatter.8.cloned.1.call-start = ((), (), s32[]{:S(2)}) async-start(), calls=%async_computation.10 | async-start | bytes 2621440 | tf_op jit(solution)/shard_map/reduce_scatter | solution.py:134
  144.1 44.0 %collective-permute-start.1 = (bf16[1,704,2048]{2,1,0:T(8,128)(2,1)}, bf16[1,704,2048]{2,1,0:T(8,128)(2,1)}, u32[]{:S(2)}, u32[]{:S(2)}) collective-permute-start(bf16[1,704,2048]{2,1,0:T(8,128)(2,1)} %param.26), channel_id=1, source_target_pairs={{0,32},{32,0},{1,33},{33,1},{2,34},{34,2},{3,35},{35,3},{4,36},{36... | collective-permute-start | bytes 8650760 | tf_op jit(solution)/shard_map/ppermute | solution.py:121
  173.7 6.6 %copy-start.9 = (bf16[1,704,2048]{2,1,0:T(8,128)(2,1)S(1)}, bf16[1,704,2048]{2,1,0:T(8,128)(2,1)}, u32[]{:S(2)}) copy-start(bf16[1,704,2048]{2,1,0:T(8,128)(2,1)} %param.26) | copy-start | bytes 8650756
  180.4 1.9 copy-start.12
  188.2 5.4 %copy-start.6 = (bf16[2048]{0:T(1024)(128)(2,1)S(1)}, bf16[2048]{0:T(1024)(128)(2,1)}, u32[]{:S(2)}) copy-start(bf16[2048]{0:T(1024)(128)(2,1)} %param.27) | copy-start | bytes 12292
  193.3 44.6 %copy-start.13 = (bf16[2048,8]{0,1:T(8,128)(2,1)S(1)}, bf16[2048,8]{0,1:T(8,128)(2,1)}, u32[]{:S(2)}) copy-start(bf16[2048,8]{0,1:T(8,128)(2,1)} %param.20) | copy-start | bytes 98308
  227.8 27.3 %all-to-all-start.3 = ((bf16[32,4,2048]{2,1,0:T(4,128)(2,1)}), bf16[32,4,2048]{2,1,0:T(4,128)(2,1)S(1)}, u32[]{:S(2)}, u32[]{:S(2)}) async-start(bf16[32,4,2048]{2,1,0:T(4,128)(2,1)} %all_to_all.35), calls=%async_computation.6 | async-start | bytes 1048576 | tf_op jit(solution)/shard_map/all_to_all | solution.py:135
Sparse Core Ops, SparseCore 0:
  17.1 56.1 reduce-scatter.3
  81.6 38.6 reduce-scatter.5
  144.2 29.4 all-gather.1
  193.4 32.2 reduce-scatter.7

commit v7 on v6

--- a/solution.py
+++ b/solution.py
@@ -69,8 +69,9 @@
     y_first = jnp.dot(by_y, weight_flat[:, split:], preferred_element_type=jnp.float32)
     y_first = lax.all_to_all(y_first.astype(jnp.bfloat16), "ty", split_axis=0, concat_axis=0, tiled=True)
     y_first = jnp.sum(y_first.reshape(n_y, -1, model_width - split).astype(jnp.float32), axis=0)
-    y_first = lax.psum_scatter(y_first.astype(jnp.bfloat16), "tz", scatter_dimension=0, tiled=True)
-    attention = jnp.concatenate([z_first, y_first.astype(jnp.float32)], axis=1)
+    y_first = lax.all_to_all(y_first.astype(jnp.bfloat16), "tz", split_axis=0, concat_axis=0, tiled=True)
+    y_first = jnp.sum(y_first.reshape(n_z, -1, model_width - split).astype(jnp.float32), axis=0)
+    attention = jnp.concatenate([z_first, y_first], axis=1)
     stream = (resid.astype(jnp.float32) + attention).astype(jnp.bfloat16)
     normed = rms_norm(stream.astype(jnp.float32), norm_gain).astype(jnp.bfloat16)
     logits = jnp.dot(normed, router_w, preferred_element_type=jnp.float32)
@@ -121,16 +122,17 @@
     paired_down = lax.ppermute(w_down, "ec", swap)
     hidden_units = w_gate_up.shape[3]
 
-    def expert_part(gate_up, down_w):
+    def activate(gate_up):
         both = jnp.dot(
             arrived, gate_up.reshape(model_width, 2 * hidden_units), preferred_element_type=jnp.float32
         )
-        hidden = (jax.nn.silu(both[:, :hidden_units]) * both[:, hidden_units:]).astype(jnp.bfloat16)
-        return jnp.dot(
-            hidden, down_w.reshape(hidden_units, model_width), preferred_element_type=jnp.float32
-        )
+        return (jax.nn.silu(both[:, :hidden_units]) * both[:, hidden_units:]).astype(jnp.bfloat16)
 
-    down = expert_part(w_gate_up, w_down) + expert_part(paired_gate_up, paired_down)
+    hidden = jnp.concatenate([activate(w_gate_up), activate(paired_gate_up)], axis=1)
+    down_w = jnp.concatenate(
+        [w_down.reshape(hidden_units, model_width), paired_down.reshape(hidden_units, model_width)], axis=0
+    )
+    down = jnp.dot(hidden, down_w, preferred_element_type=jnp.float32)
     summed = lax.psum_scatter(down.astype(jnp.bfloat16), "ex", scatter_dimension=0, tiled=True)
     flat_back = lax.all_to_all(summed, TENSOR, split_axis=0, concat_axis=0, tiled=True)
     back_index = jnp.where(is_kept, holder * (capacity_rows * slots) + arrival * slots + within, 0)

time: 264 us -> 275 us (1.042)
  starting transfers between devices: 14.1 us -> 22.7 us
    reduce_scatter x1 -> x0, waiting for transfers between devices: 33.3 us -> none  [per_device(): lax.psum_scatter(y_first.astype(jnp.bfloat16), 'tz', scatter_dimension=0,...]
    all_to_all x0 -> x1, waiting for transfers between devices: none -> 24.3 us  [per_device(): lax.all_to_all(y_first.astype(jnp.bfloat16), 'tz', split_axis=0, concat_a...]
    all_to_all x0 -> x1, starting transfers between devices: none -> 8.7 us  [per_device(): lax.all_to_all(y_first.astype(jnp.bfloat16), 'tz', split_axis=0, concat_a...]
    all_to_all x1, waiting for transfers between devices: 0.01 us -> 7.72 us  [per_device(): lax.all_to_all(z_first, 'ty', split_axis=0, concat_axis=0, tiled=True)]
    dot_general x4 -> x3, matrix products: 19.5 us -> 18.9 us  [the longest x2 12.3 us: activate(): jnp.dot(arrived, gate_up.reshape(model_width, 2 * hidden_units), preferre...]
  transfers between devices with their start and end apart: 8 -> 8, of which waited for: 4 -> 5; matrix products, arithmetic and copies ran while one was open for 11% -> 10% of each run, Pallas kernels for 0% -> 0%
where the time goes in v7:
time: 275 us
  waiting for transfers between devices  109 us (40%)
  blocking collectives  76.1 us (28%)
  matrix products  29.1 us (11%)
  starting transfers between devices  22.7 us (8%)
  local copies, waits for them, and re-layouts  14.4 us (5%)
  between operations  14.1 us (5%)
  other arithmetic  8.85 us (3%)
    all_to_all x1, blocking collectives, per_device(): lax.all_to_all(y_first.astype(jnp.bfloat16), 'ty', split_axis=0, concat_a...  53.2 us
    reduce_scatter x1, waiting for transfers between devices, per_device(): lax.psum_scatter(down.astype(jnp.bfloat16), 'ex', scatter_dimension=0, ti...  32.1 us
    all_gather x1, waiting for transfers between devices, per_device(): arrived = lax.all_gather(exchanged, 'ex', axis=0, tiled=True)  29.6 us
    all_to_all x1, waiting for transfers between devices, per_device(): lax.all_to_all(y_first.astype(jnp.bfloat16), 'tz', split_axis=0, concat_a...  24.3 us
    all_to_all x1, blocking collectives, per_device(): lax.all_to_all(send_rows, TENSOR, split_axis=0, concat_axis=0, tiled=True)  22.9 us
    all_to_all x1, waiting for transfers between devices, per_device(): lax.all_to_all(summed, TENSOR, split_axis=0, concat_axis=0, tiled=True)  15.6 us
    dot_general x2, matrix products, activate(): jnp.dot(arrived, gate_up.reshape(model_width, 2 * hidden_units), preferre...  12.3 us
    all_to_all x1, starting transfers between devices, per_device(): lax.all_to_all(summed, TENSOR, split_axis=0, concat_axis=0, tiled=True)  10.1 us
  transfers between devices with their start and end apart: 8, of which 5 were waited for; matrix products, arithmetic and copies ran while one was open for 10% of the time, Pallas kernels for 0%

profile of v7, /device:TPU:32, one launch (start us, length us, event | category | flops | bytes accessed | tf_op | source)
XLA Modules:
  0.0 274.6 jit_solution(3500614687750869418)
XLA Ops:
  7.2 0.8 fusion.44
  8.1 0.8 broadcast_subtract_fusion
  8.9 0.7 fusion.23
  9.7 1.5 fusion.5
  11.2 1.3 copy-done.1
  12.5 4.4 %convolution_convert_fusion.1 = bf16[2048,1024]{1,0:T(8,128)(2,1)} fusion(bf16[2048,512]{0,1:T(8,128)(2,1)S(1)} %fusion.5, bf16[512,2048]{1,0:T(8,128)(2,1)S(1)} %bitcast.52), kind=kOutput, calls=%fused_computation.10 | convolution fusion | flops 2149580800 | bytes 7340032 | tf_op jit(solution)/shard_map/dot_general | solution.py:64
  17.0 2.9 %copy.56 = bf16[2048,512]{1,0:T(8,128)(2,1)S(1)} copy(bf16[2048,512]{0,1:T(8,128)(2,1)} %copy-done.1) | data formatting | bytes 4194304 | tf_op jit(solution)/shard_map/convert_element_type | solution.py:59
  19.9 0.2 copy.57
  20.1 1.4 copy-done.11
  21.5 2.3 convolution_convert_fusion
  23.8 53.2 %all_to_all.51 = bf16[4,512,1024]{2,1,0:T(8,128)(2,1)} all-to-all(bf16[4,512,1024]{2,1,0:T(8,128)(2,1)S(1)} %bitcast.43), channel_id=1, replica_groups=mesh['ex'=4,'ec'=2,'tz'=8,'ty'=4] {'ty'}, dimensions={0} | all-to-all | bytes 8388608 | tf_op jit(solution)/shard_map/all_to_all | solution.py:70
  77.0 4.4 %reduce_sum.124 = bf16[512,1024]{1,0:T(8,128)(2,1)} reduce(bf16[4,512,1024]{2,1,0:T(8,128)(2,1)} %all_to_all.51, bf16[]{:T(256)} %constant.108.clone.1), dimensions={0}, to_apply=%region_2.3 | reduce | flops 1572864 | bytes 5242882 | tf_op jit(solution)/shard_map/reduce_sum | solution.py:71
  81.4 8.7 %all-to-all-start.2 = ((bf16[8,64,1024]{2,1,0:T(8,128)(2,1)}), bf16[8,64,1024]{2,1,0:T(8,128)(2,1)S(1)}, u32[]{:S(2)}, u32[]{:S(2)}) async-start(bf16[8,64,1024]{2,1,0:T(8,128)(2,1)} %bitcast.12), calls=%async_computation.3 | async-start | bytes 2097152 | tf_op jit(solution)/shard_map/all_to_all | solution.py:72
  90.5 0.1 and_select_fusion.1
  90.7 0.1 eq.202
  90.8 0.1 eq.188
  91.0 0.2 convert_reduce_fusion.2
  91.3 0.2 reduce_window_sum.11
  91.4 0.2 select_reduce_fusion.1
  91.6 0.1 reshape.170
  92.0 24.3 %all-to-all-done.2 = bf16[8,64,1024]{2,1,0:T(8,128)(2,1)S(1)} async-done(((bf16[8,64,1024]{2,1,0:T(8,128)(2,1)}), bf16[8,64,1024]{2,1,0:T(8,128)(2,1)S(1)}, u32[]{:S(2)}, u32[]{:S(2)}) %all-to-all-start.2) | async-done | bytes 1048608 | tf_op jit(solution)/shard_map/all_to_all | solution.py:72
  116.2 3.5 %all-to-all-start = ((bf16[4,64,1024]{2,1,0:T(8,128)(2,1)}), bf16[4,64,1024]{2,1,0:T(8,128)(2,1)S(1)}, u32[]{:S(2)}, u32[]{:S(2)}) async-start(bf16[4,64,1024]{2,1,0:T(8,128)(2,1)} %bitcast.45), calls=%async_computation.1 | async-start | bytes 1048576 | tf_op jit(solution)/shard_map/all_to_all | solution.py:66
  119.9 0.2 convert_reduce_fusion
  120.0 7.7 %all-to-all-done = bf16[4,64,1024]{2,1,0:T(8,128)(2,1)S(1)} async-done(((bf16[4,64,1024]{2,1,0:T(8,128)(2,1)}), bf16[4,64,1024]{2,1,0:T(8,128)(2,1)S(1)}, u32[]{:S(2)}, u32[]{:S(2)}) %all-to-all-start) | async-done | bytes 524320 | tf_op jit(solution)/shard_map/all_to_all | solution.py:66
  127.8 0.2 fusion.16
  128.0 0.4 convolution_convert_fusion.2
  128.4 0.2 all_to_all.40
  128.6 22.9 %all_to_all.52 = bf16[32,4,2048]{2,1,0:T(4,128)(2,1)S(1)} all-to-all(bf16[32,4,2048]{2,1,0:T(4,128)(2,1)S(1)} %all_to_all.40), channel_id=1, replica_groups=mesh['ex'=4,'ec'=2,'tz'=8,'ty'=4] {'tz','ty'}, dimensions={0} | all-to-all | bytes 1048576 | tf_op jit(solution)/shard_map/all_to_all | solution.py:118
  151.5 0.9 all_to_all.42
  152.5 0.3 collective-permute-start.1
  152.8 29.6 %all-gather.2.cloned.1.call-done = bf16[512,2048]{1,0:T(8,128)(2,1)} async-done(((bf16[128,2048]{1,0:T(8,128)(2,1)}), bf16[512,2048]{1,0:T(8,128)(2,1)}) %all-gather.2.cloned.1.call-update) | async-done | bytes 2097168 | tf_op jit(solution)/shard_map/all_gather | solution.py:119
  182.4 6.5 %fusion.46 = f32[512,1408]{1,0:T(8,128)S(1)} fusion(bf16[512,2048]{1,0:T(8,128)(2,1)} %all-gather.2.cloned.1.call-done, bf16[2048,1408]{0,1:T(8,128)(2,1)} %bitcast.15), kind=kOutput, calls=%fused_computation.92 | convolution fusion | flops 2952790016 | bytes 10747904 | tf_op jit(solution)/shard_map/dot_general | solution.py:126
  188.9 0.5 fusion.9
  189.4 1.1 copy-done.12
  190.4 5.8 %fusion.45 = f32[512,1408]{1,0:T(8,128)S(1)} fusion(bf16[512,2048]{1,0:T(8,128)(2,1)S(1)} %copy-done.12, bf16[2048,1408]{0,1:T(8,128)(2,1)} %bitcast.50), kind=kOutput, calls=%fused_computation.91 | convolution fusion | flops 2952790016 | bytes 10747904 | tf_op jit(solution)/shard_map/dot_general | solution.py:126
  196.3 0.5 fusion.10
  196.8 1.3 copy-done.9
  198.1 6.6 %fusion.6 = bf16[512,2048]{1,0:T(8,128)(2,1)} fusion(bf16[704,2048]{1,0:T(8,128)(2,1)} %bitcast.17, bf16[704,2048]{1,0:T(8,128)(2,1)S(1)} %bitcast.51, bf16[512,704]{1,0:T(8,128)(2,1)S(1)} %fusion.9, bf16[512,704]{1,0:T(8,128)(2,1)S(1)} %fusion.10), kind=kOutput, calls=%fused_computation.11 | convolution fusion | flops 2968256512 | bytes 9306112 | tf_op jit(solution)/shard_map/dot_general | solution.py:135
  204.9 0.1 reshape.176
  205.0 32.1 %reduce-scatter.5.cloned.1.call-done = bf16[128,2048]{1,0:T(8,128)(2,1)} async-done(((bf16[512,2048]{1,0:T(8,128)(2,1)}), bf16[128,2048]{1,0:T(8,128)(2,1)}) %reduce-scatter.5.cloned.1.call-update) | async-done | bytes 524304 | tf_op jit(solution)/shard_map/reduce_scatter | solution.py:136
  237.2 2.0 all_to_all.43
  239.2 10.1 %all-to-all-start.4 = ((bf16[32,4,2048]{2,1,0:T(4,128)(2,1)}), bf16[32,4,2048]{2,1,0:T(4,128)(2,1)S(1)}, u32[]{:S(2)}, u32[]{:S(2)}) async-start(bf16[32,4,2048]{2,1,0:T(4,128)(2,1)} %all_to_all.43), calls=%async_computation.6 | async-start | bytes 1048576 | tf_op jit(solution)/shard_map/all_to_all | solution.py:137
  249.3 0.2 fusion.28
  249.5 1.0 gather_fusion
  250.6 0.1 reshape.179
  251.0 15.6 %all-to-all-done.4 = bf16[32,4,2048]{2,1,0:T(4,128)(2,1)S(1)} async-done(((bf16[32,4,2048]{2,1,0:T(4,128)(2,1)}), bf16[32,4,2048]{2,1,0:T(4,128)(2,1)S(1)}, u32[]{:S(2)}, u32[]{:S(2)}) %all-to-all-start.4) | async-done | bytes 524320 | tf_op jit(solution)/shard_map/all_to_all | solution.py:137
  266.7 0.5 multiply_reduce_fusion
  267.2 0.8 multiply_convert_fusion
  (58 shorter events, 1.6 us)
Async XLA Ops:
  7.2 1.7 copy-start
  7.2 109.1 %reduce-scatter.3.cloned.1.call-start = ((), (), s32[]{:S(2)}) async-start(), calls=%async_computation.7 | async-start | bytes 4718592 | tf_op jit(solution)/shard_map/reduce_scatter | solution.py:65
  9.6 2.9 %copy-start.10 = (bf16[8,64,2048]{2,1,0:T(8,128)(2,1)S(1)}, bf16[8,64,2048]{2,1,0:T(8,128)(2,1)}, u32[]{:S(2)}) copy-start(bf16[8,64,2048]{2,1,0:T(8,128)(2,1)} %param.18) | copy-start | bytes 6291460
  11.2 1.4 copy-start.1
  19.9 1.6 copy-start.11
  77.0 13.2 %copy-start.3 = (s32[64,2]{0,1:T(2,128)S(1)}, s32[64,2]{0,1:T(2,128)}, u32[]{:S(2)}) copy-start(s32[64,2]{0,1:T(2,128)} %param.21) | copy-start | bytes 1540
  77.0 13.3 %copy-start.4 = (s32[32]{0:T(128)S(1)}, s32[32]{0:T(128)}, u32[]{:S(2)}) copy-start(s32[32]{0:T(128)} %param.23) | copy-start | bytes 388
  77.0 13.5 %copy-start.7 = (s32[64,2]{0,1:T(2,128)S(1)}, s32[64,2]{0,1:T(2,128)}, u32[]{:S(2)}) copy-start(s32[64,2]{0,1:T(2,128)} %param.22) | copy-start | bytes 1540
  77.0 14.8 %copy-start.5 = (bf16[2048]{0:T(1024)(128)(2,1)S(1)}, bf16[2048]{0:T(1024)(128)(2,1)}, u32[]{:S(2)}) copy-start(bf16[2048]{0:T(1024)(128)(2,1)} %param.19) | copy-start | bytes 12292
  77.0 14.8 %copy-start.8 = (s32[32]{0:T(128)S(1)}, s32[32]{0:T(128)}, u32[]{:S(2)}) copy-start(s32[32]{0:T(128)} %param.24) | copy-start | bytes 388
  81.4 46.4 %copy-start.2 = (bf16[64,2048]{1,0:T(8,128)(2,1)S(1)}, bf16[64,2048]{1,0:T(8,128)(2,1)}, u32[]{:S(2)}) copy-start(bf16[64,2048]{1,0:T(8,128)(2,1)} %param.14) | copy-start | bytes 786436
  81.4 34.8 %all-to-all-start.2 = ((bf16[8,64,1024]{2,1,0:T(8,128)(2,1)}), bf16[8,64,1024]{2,1,0:T(8,128)(2,1)S(1)}, u32[]{:S(2)}, u32[]{:S(2)}) async-start(bf16[8,64,1024]{2,1,0:T(8,128)(2,1)} %bitcast.12), calls=%async_computation.3 | async-start | bytes 2097152 | tf_op jit(solution)/shard_map/all_to_all | solution.py:72
  90.1 62.6 %collective-permute-start = (bf16[1,2048,2,704]{1,3,2,0:T(8,128)(2,1)}, bf16[1,2048,2,704]{1,3,2,0:T(8,128)(2,1)}, u32[]{:S(2)}, u32[]{:S(2)}) collective-permute-start(bf16[1,2048,2,704]{1,3,2,0:T(8,128)(2,1)} %param.25), channel_id=1, source_target_pairs={{0,32},{32,0},{1,33},{33,1},{2,34},{34,2},{3,35},{35,3},{4,36},{36... | collective-permute-start | bytes 17301512 | tf_op jit(solution)/shard_map/ppermute | solution.py:121
  116.2 11.5 %all-to-all-start = ((bf16[4,64,1024]{2,1,0:T(8,128)(2,1)}), bf16[4,64,1024]{2,1,0:T(8,128)(2,1)S(1)}, u32[]{:S(2)}, u32[]{:S(2)}) async-start(bf16[4,64,1024]{2,1,0:T(8,128)(2,1)} %bitcast.45), calls=%async_computation.1 | async-start | bytes 1048576 | tf_op jit(solution)/shard_map/all_to_all | solution.py:66
  119.7 62.7 %all-gather.2.cloned.1.call-start = ((), (), s32[]{:S(2)}) async-start(), calls=%async_computation.8 | async-start | bytes 2621440 | tf_op jit(solution)/shard_map/all_gather | solution.py:119
  152.4 84.7 %reduce-scatter.5.cloned.1.call-start = ((), (), s32[]{:S(2)}) async-start(), calls=%async_computation.9 | async-start | bytes 2621440 | tf_op jit(solution)/shard_map/reduce_scatter | solution.py:136
  152.5 44.3 %collective-permute-start.1 = (bf16[1,704,2048]{2,1,0:T(8,128)(2,1)}, bf16[1,704,2048]{2,1,0:T(8,128)(2,1)}, u32[]{:S(2)}, u32[]{:S(2)}) collective-permute-start(bf16[1,704,2048]{2,1,0:T(8,128)(2,1)} %param.26), channel_id=1, source_target_pairs={{0,32},{32,0},{1,33},{33,1},{2,34},{34,2},{3,35},{35,3},{4,36},{36... | collective-permute-start | bytes 8650760 | tf_op jit(solution)/shard_map/ppermute | solution.py:122
  188.8 1.6 copy-start.12
  196.3 1.8 copy-start.9
  198.1 6.9 %copy-start.6 = (bf16[2048]{0:T(1024)(128)(2,1)S(1)}, bf16[2048]{0:T(1024)(128)(2,1)}, u32[]{:S(2)}) copy-start(bf16[2048]{0:T(1024)(128)(2,1)} %param.27) | copy-start | bytes 12292
  204.7 44.6 %copy-start.13 = (bf16[2048,8]{0,1:T(8,128)(2,1)S(1)}, bf16[2048,8]{0,1:T(8,128)(2,1)}, u32[]{:S(2)}) copy-start(bf16[2048,8]{0,1:T(8,128)(2,1)} %param.20) | copy-start | bytes 98308
  239.2 27.3 %all-to-all-start.4 = ((bf16[32,4,2048]{2,1,0:T(4,128)(2,1)}), bf16[32,4,2048]{2,1,0:T(4,128)(2,1)S(1)}, u32[]{:S(2)}, u32[]{:S(2)}) async-start(bf16[32,4,2048]{2,1,0:T(4,128)(2,1)} %all_to_all.43), calls=%async_computation.6 | async-start | bytes 1048576 | tf_op jit(solution)/shard_map/all_to_all | solution.py:137
Sparse Core Ops, SparseCore 0:
  17.1 56.1 reduce-scatter.2
  152.6 29.7 all-gather.1
  204.9 32.2 reduce-scatter.4

commit v8 on v6

--- a/solution.py
+++ b/solution.py
@@ -50,22 +50,30 @@
     width = att_experts * slice_ctx
     column = jnp.arange(width, dtype=jnp.int32)
     source = jnp.arange(slice_ctx * top_count, dtype=jnp.int32)[:, None]
-    mixed = jnp.zeros((group_rows, width), jnp.float32)
-    for choice in range(top_count):
-        spread = (source == (column % slice_ctx)[None, :] * top_count + choice).astype(jnp.bfloat16)
-        picked = jnp.dot(contexts, spread, preferred_element_type=jnp.float32)
-        chosen = att_routes[:, choice : choice + 1] == (column // slice_ctx)[None, :]
-        mixed = mixed + jnp.where(chosen, picked * gate_att[:, choice : choice + 1], 0.0)
-    row_block = mixed.astype(jnp.bfloat16)
-    weight_flat = att_out_w.reshape(width, model_width)
+
+    def mix(ctx, routes, gates):
+        mixed = jnp.zeros((group_rows, width), jnp.float32)
+        for choice in range(top_count):
+            spread = (source == (column % slice_ctx)[None, :] * top_count + choice).astype(jnp.bfloat16)
+            picked = jnp.dot(ctx, spread, preferred_element_type=jnp.float32)
+            chosen = routes[:, choice : choice + 1] == (column // slice_ctx)[None, :]
+            mixed = mixed + jnp.where(chosen, picked * gates[:, choice : choice + 1], 0.0)
+        return mixed.astype(jnp.bfloat16)
+
     n_y = lax.axis_size("ty")
     n_z = lax.axis_size("tz")
+
+    def y_major(values):
+        return values.reshape(n_z, n_y, -1, values.shape[1]).transpose(1, 0, 2, 3).reshape(values.shape)
+
+    row_block = mix(contexts, att_routes, gate_att)
+    by_y = mix(y_major(contexts), y_major(att_routes), y_major(gate_att))
+    weight_flat = att_out_w.reshape(width, model_width)
     split = model_width * Z_SHARE // 8
     z_first = jnp.dot(row_block, weight_flat[:, :split], preferred_element_type=jnp.float32)
     z_first = lax.psum_scatter(z_first.astype(jnp.bfloat16), "tz", scatter_dimension=0, tiled=True)
     z_first = lax.all_to_all(z_first, "ty", split_axis=0, concat_axis=0, tiled=True)
     z_first = jnp.sum(z_first.reshape(n_y, -1, split).astype(jnp.float32), axis=0)
-    by_y = row_block.reshape(n_z, n_y, -1, width).transpose(1, 0, 2, 3).reshape(group_rows, width)
     y_first = jnp.dot(by_y, weight_flat[:, split:], preferred_element_type=jnp.float32)
     y_first = lax.all_to_all(y_first.astype(jnp.bfloat16), "ty", split_axis=0, concat_axis=0, tiled=True)
     y_first = jnp.sum(y_first.reshape(n_y, -1, model_width - split).astype(jnp.float32), axis=0)

time: 264 us -> 273 us (1.034)
  matrix products: 29.6 us -> 40.1 us
  local copies, waits for them, and re-layouts: 12 us -> 7.91 us
    dot_general x2, matrix products: 2.28 us -> 6.53 us  [mix(): picked = jnp.dot(ctx, spread, preferred_element_type=jnp.float32)]
    dot_general x1, matrix products: 2.34 us -> 6.45 us  [per_device(): jnp.dot(by_y, weight_flat[:, split:], preferred_element_type=jnp.float32)]
    convert_element_type x1 -> x0, local copies, waits for them, and re-layouts: 2.87 us -> none  [per_device(): row_block = mixed.astype(jnp.bfloat16)]
  transfers between devices with their start and end apart: 8 -> 8, of which waited for: 4 -> 4; matrix products, arithmetic and copies ran while one was open for 11% -> 13% of each run, Pallas kernels for 0% -> 0%
where the time goes in v8:
time: 273 us; the launch traced here: 272 us
  waiting for transfers between devices  110 us (40%)
  blocking collectives  76 us (28%)
  matrix products  40.1 us (15%)
  between operations  14.2 us (5%)
  starting transfers between devices  14.1 us (5%)
  other arithmetic  9.39 us (3%)
  local copies, waits for them, and re-layouts  7.91 us (3%)
    all_to_all x1, blocking collectives, per_device(): lax.all_to_all(y_first.astype(jnp.bfloat16), 'ty', split_axis=0, concat_a...  54.8 us
    reduce_scatter x1, waiting for transfers between devices, per_device(): lax.psum_scatter(y_first.astype(jnp.bfloat16), 'tz', scatter_dimension=0,...  33.2 us
    reduce_scatter x1, waiting for transfers between devices, per_device(): lax.psum_scatter(down.astype(jnp.bfloat16), 'ex', scatter_dimension=0, ti...  32.1 us
    all_gather x1, waiting for transfers between devices, per_device(): arrived = lax.all_gather(exchanged, 'ex', axis=0, tiled=True)  29.2 us
    all_to_all x1, blocking collectives, per_device(): lax.all_to_all(send_rows, TENSOR, split_axis=0, concat_axis=0, tiled=True)  21.2 us
    all_to_all x1, waiting for transfers between devices, per_device(): lax.all_to_all(summed, TENSOR, split_axis=0, concat_axis=0, tiled=True)  15.6 us
    dot_general x2, matrix products, expert_part(): jnp.dot(arrived, gate_up.reshape(model_width, 2 * hidden_units), preferre...  12.4 us
    all_to_all x1, starting transfers between devices, per_device(): lax.all_to_all(summed, TENSOR, split_axis=0, concat_axis=0, tiled=True)  10.1 us
  transfers between devices with their start and end apart: 8, of which 4 were waited for; matrix products, arithmetic and copies ran while one was open for 13% of the time, Pallas kernels for 0%

profile of v8, /device:TPU:32, one launch (start us, length us, event | category | flops | bytes accessed | tf_op | source)
XLA Modules:
  0.0 271.8 jit_solution(17533141408393006026)
XLA Ops:
  7.3 0.9 broadcast_subtract_fusion
  8.2 0.8 fusion.57
  9.0 3.7 %fusion.27 = f32[512,2048]{1,0:T(8,128)} fusion(bf16[2048,128]{1,0:T(8,128)(2,1)} %param.15, s32[512]{0:T(512)S(1)} %fusion.46), kind=kOutput, calls=%fused_computation.40 | convolution fusion | flops 268566528 | bytes 4720640 | tf_op jit(solution)/shard_map/dot_general | solution.py:58
  12.7 6.5 %convolution_convert_fusion.1 = bf16[2048,1024]{1,0:T(8,128)(2,1)} fusion(f32[512,2048]{1,0:T(8,128)} %fusion.27, bf16[2048,128]{1,0:T(8,128)(2,1)S(1)} %copy-done.1, f32[2048]{0:T(1024)S(1)} %bitcast.94, s32[2048]{0:T(1024)S(1)} %bitcast.96, f32[2048]{0:T(1024)S(1)} %bitcast.89, s32[2048]{0:T(1024)S(1)} %bitcast.95, s32[512]{0:T(512)S(1)} %get-tuple-element.24, ...), kind=kOutput, calls=%fused_computation.11 | convolution fusion | flops 2426535936 | bytes 9998336 | tf_op jit(solution)/shard_map/dot_general | solution.py:73
  19.3 0.6 copy-done.3
  20.0 0.1 reshape.176
  20.1 0.5 broadcast.332
  20.6 0.7 fusion.55
  21.7 2.8 %fusion.25 = f32[512,2048]{1,0:T(8,128)} fusion(bf16[2048,128]{1,0:T(8,128)(2,1)S(1)} %bitcast.85, s32[512]{0:T(512)S(1)} %fusion.46), kind=kOutput, calls=%fused_computation.39 | convolution fusion | flops 268566528 | bytes 4720640 | tf_op jit(solution)/shard_map/dot_general | solution.py:58
  24.6 6.5 %convolution_convert_fusion = bf16[2048,1024]{1,0:T(8,128)(2,1)} fusion(f32[512,2048]{1,0:T(8,128)} %fusion.25, bf16[2048,128]{1,0:T(8,128)(2,1)S(1)} %bitcast.86, f32[2048]{0:T(1024)S(1)} %bitcast.91, s32[2048]{0:T(1024)S(1)} %bitcast.93, f32[2048]{0:T(1024)S(1)} %bitcast.90, s32[2048]{0:T(1024)S(1)} %bitcast.92, s32[512]{0:T(512)S(1)} %get-tuple-element.24, ...), kind=kOutput, calls=%fused_computation.10 | convolution fusion | flops 2426535936 | bytes 9998336 | tf_op jit(solution)/shard_map/dot_general | solution.py:77
  31.0 54.8 %all_to_all.42 = bf16[4,512,1024]{2,1,0:T(8,128)(2,1)} all-to-all(bf16[4,512,1024]{2,1,0:T(8,128)(2,1)} %bitcast.83), channel_id=1, replica_groups=mesh['ex'=4,'ec'=2,'tz'=8,'ty'=4] {'ty'}, dimensions={0} | all-to-all | bytes 8388608 | tf_op jit(solution)/shard_map/all_to_all | solution.py:78
  85.9 4.4 %reduce_sum.115 = bf16[512,1024]{1,0:T(8,128)(2,1)} reduce(bf16[4,512,1024]{2,1,0:T(8,128)(2,1)} %all_to_all.42, bf16[]{:T(256)} %constant.118.clone.1), dimensions={0}, to_apply=%region_2.3 | reduce | flops 1572864 | bytes 5242882 | tf_op jit(solution)/shard_map/reduce_sum | solution.py:79
  90.5 0.1 convert_reduce_fusion.2
  90.7 0.1 and_select_fusion.1
  90.8 0.1 copy.79
  90.9 0.1 eq.266
  91.1 0.1 eq.252
  91.2 0.2 convert_reduce_fusion.1
  91.4 0.1 fusion.39
  91.5 0.2 reduce_window_sum.11
  91.7 0.2 select_reduce_fusion.1
  91.9 3.5 %all-to-all-start = ((bf16[4,64,1024]{2,1,0:T(8,128)(2,1)}), bf16[4,64,1024]{2,1,0:T(8,128)(2,1)S(1)}, u32[]{:S(2)}, u32[]{:S(2)}) async-start(bf16[4,64,1024]{2,1,0:T(8,128)(2,1)} %bitcast.87), calls=%async_computation.1 | async-start | bytes 1048576 | tf_op jit(solution)/shard_map/all_to_all | solution.py:75
  95.5 0.1 reshape.181
  95.9 33.2 %reduce-scatter.6.cloned.1.call-done = bf16[64,1024]{1,0:T(8,128)(2,1)} async-done(((bf16[512,1024]{1,0:T(8,128)(2,1)}), bf16[64,1024]{1,0:T(8,128)(2,1)}) %reduce-scatter.6.cloned.1.call-update) | async-done | bytes 131088 | tf_op jit(solution)/shard_map/reduce_scatter | solution.py:80
  129.0 0.9 convert_element_type.85
  130.1 0.2 fusion.15
  130.2 0.4 convolution_convert_fusion.2
  130.6 0.2 all_to_all.32
  130.8 21.2 %all_to_all.43 = bf16[32,4,2048]{2,1,0:T(4,128)(2,1)S(1)} all-to-all(bf16[32,4,2048]{2,1,0:T(4,128)(2,1)S(1)} %all_to_all.32), channel_id=1, replica_groups=mesh['ex'=4,'ec'=2,'tz'=8,'ty'=4] {'tz','ty'}, dimensions={0} | all-to-all | bytes 1048576 | tf_op jit(solution)/shard_map/all_to_all | solution.py:125
  152.0 0.9 all_to_all.34
  153.0 0.3 collective-permute-start.1
  153.3 29.2 %all-gather.2.cloned.1.call-done = bf16[512,2048]{1,0:T(8,128)(2,1)} async-done(((bf16[128,2048]{1,0:T(8,128)(2,1)}), bf16[512,2048]{1,0:T(8,128)(2,1)}) %all-gather.2.cloned.1.call-update) | async-done | bytes 2097168 | tf_op jit(solution)/shard_map/all_gather | solution.py:126
  182.5 6.6 %fusion.60 = f32[512,1408]{1,0:T(8,128)S(1)} fusion(bf16[512,2048]{1,0:T(8,128)(2,1)} %all-gather.2.cloned.1.call-done, bf16[2048,1408]{0,1:T(8,128)(2,1)} %bitcast.97), kind=kOutput, calls=%fused_computation.104 | convolution fusion | flops 2952790016 | bytes 10747904 | tf_op jit(solution)/shard_map/dot_general | solution.py:133
  189.1 1.9 fusion.5
  191.0 5.8 %fusion.61 = f32[512,1408]{1,0:T(8,128)S(1)} fusion(bf16[512,2048]{1,0:T(8,128)(2,1)S(1)} %copy-done.12, bf16[2048,1408]{0,1:T(8,128)(2,1)} %bitcast.23), kind=kOutput, calls=%fused_computation.105 | convolution fusion | flops 2952790016 | bytes 10747904 | tf_op jit(solution)/shard_map/dot_general | solution.py:133
  196.9 5.1 %add_convert_fusion = bf16[512,2048]{1,0:T(8,128)(2,1)} fusion(f32[512,2048]{1,0:T(8,128)S(1)} %fusion.5, bf16[1,704,2048]{2,1,0:T(8,128)(2,1)} %collective-permute-done.1, f32[512,1408]{1,0:T(8,128)S(1)} %fusion.61), kind=kOutput, calls=%fused_computation.9 | convolution fusion | flops 1480654848 | bytes 12320768 | tf_op jit(solution)/shard_map/dot_general | solution.py:137
  202.1 0.1 reshape.187
  202.3 32.1 %reduce-scatter.8.cloned.1.call-done = bf16[128,2048]{1,0:T(8,128)(2,1)} async-done(((bf16[512,2048]{1,0:T(8,128)(2,1)}), bf16[128,2048]{1,0:T(8,128)(2,1)}) %reduce-scatter.8.cloned.1.call-update) | async-done | bytes 524304 | tf_op jit(solution)/shard_map/reduce_scatter | solution.py:142
  234.4 2.0 all_to_all.35
  236.5 10.1 %all-to-all-start.3 = ((bf16[32,4,2048]{2,1,0:T(4,128)(2,1)}), bf16[32,4,2048]{2,1,0:T(4,128)(2,1)S(1)}, u32[]{:S(2)}, u32[]{:S(2)}) async-start(bf16[32,4,2048]{2,1,0:T(4,128)(2,1)} %all_to_all.35), calls=%async_computation.6 | async-start | bytes 1048576 | tf_op jit(solution)/shard_map/all_to_all | solution.py:143
  246.6 0.2 fusion.36
  246.8 1.0 gather_fusion
  247.8 0.1 reshape.190
  248.1 0.1 select_reduce_fusion
  248.2 15.6 %all-to-all-done.3 = bf16[32,4,2048]{2,1,0:T(4,128)(2,1)S(1)} async-done(((bf16[32,4,2048]{2,1,0:T(4,128)(2,1)}), bf16[32,4,2048]{2,1,0:T(4,128)(2,1)S(1)}, u32[]{:S(2)}, u32[]{:S(2)}) %all-to-all-start.3) | async-done | bytes 524320 | tf_op jit(solution)/shard_map/all_to_all | solution.py:143
  263.8 0.1 all_to_all.37
  263.9 0.5 multiply_reduce_fusion
  264.5 0.8 multiply_convert_fusion
  (68 shorter events, 1.6 us)
Async XLA Ops:
  7.2 239.4 %copy-start = (bf16[2048,8]{0,1:T(8,128)(2,1)S(1)}, bf16[2048,8]{0,1:T(8,128)(2,1)}, u32[]{:S(2)}) copy-start(bf16[2048,8]{0,1:T(8,128)(2,1)} %param.20) | copy-start | bytes 98308
  7.2 5.5 %copy-start.1 = (bf16[2048,128]{1,0:T(8,128)(2,1)S(1)}, bf16[2048,128]{1,0:T(8,128)(2,1)}, u32[]{:S(2)}) copy-start(bf16[2048,128]{1,0:T(8,128)(2,1)} %param.15) | copy-start | bytes 1572868
  7.2 5.5 %copy-start.11 = (bf16[8,64,2048]{2,1,0:T(8,128)(2,1)S(1)}, bf16[8,64,2048]{2,1,0:T(8,128)(2,1)}, u32[]{:S(2)}) copy-start(bf16[8,64,2048]{2,1,0:T(8,128)(2,1)} %param.18) | copy-start | bytes 6291460
  7.2 84.7 %reduce-scatter.4.cloned.1.call-start = ((), (), s32[]{:S(2)}) async-start(), calls=%async_computation.7 | async-start | bytes 4718592 | tf_op jit(solution)/shard_map/reduce_scatter | solution.py:74
  19.3 0.7 copy-start.3
  19.3 109.7 %reduce-scatter.6.cloned.1.call-start = ((), (), s32[]{:S(2)}) async-start(), calls=%async_computation.8 | async-start | bytes 1179648 | tf_op jit(solution)/shard_map/reduce_scatter | solution.py:80
  85.8 4.6 %copy-start.4 = (s32[64,2]{0,1:T(2,128)S(1)}, s32[64,2]{0,1:T(2,128)}, u32[]{:S(2)}) copy-start(s32[64,2]{0,1:T(2,128)} %param.21) | copy-start | bytes 1540
  85.8 4.7 %copy-start.5 = (s32[32]{0:T(128)S(1)}, s32[32]{0:T(128)}, u32[]{:S(2)}) copy-start(s32[32]{0:T(128)} %param.23) | copy-start | bytes 388
  85.8 4.9 %copy-start.8 = (s32[64,2]{0,1:T(2,128)S(1)}, s32[64,2]{0,1:T(2,128)}, u32[]{:S(2)}) copy-start(s32[64,2]{0,1:T(2,128)} %param.22) | copy-start | bytes 1540
  85.8 9.6 %copy-start.9 = (s32[32]{0:T(128)S(1)}, s32[32]{0:T(128)}, u32[]{:S(2)}) copy-start(s32[32]{0:T(128)} %param.24) | copy-start | bytes 388
  85.8 9.9 %copy-start.6 = (bf16[2048]{0:T(1024)(128)(2,1)S(1)}, bf16[2048]{0:T(1024)(128)(2,1)}, u32[]{:S(2)}) copy-start(bf16[2048]{0:T(1024)(128)(2,1)} %param.19) | copy-start | bytes 12292
  85.8 44.2 %copy-start.2 = (bf16[64,2048]{1,0:T(8,128)(2,1)S(1)}, bf16[64,2048]{1,0:T(8,128)(2,1)}, u32[]{:S(2)}) copy-start(bf16[64,2048]{1,0:T(8,128)(2,1)} %param.14) | copy-start | bytes 786436
  90.3 100.7 %collective-permute-start = (bf16[1,2048,2,704]{1,3,2,0:T(8,128)(2,1)}, bf16[1,2048,2,704]{1,3,2,0:T(8,128)(2,1)}, u32[]{:S(2)}, u32[]{:S(2)}) collective-permute-start(bf16[1,2048,2,704]{1,3,2,0:T(8,128)(2,1)} %param.25), channel_id=1, source_target_pairs={{0,32},{32,0},{1,33},{33,1},{2,34},{34,2},{3,35},{35,3},{4,36},{36... | collective-permute-start | bytes 17301512 | tf_op jit(solution)/shard_map/ppermute | solution.py:128
  91.9 38.1 %all-to-all-start = ((bf16[4,64,1024]{2,1,0:T(8,128)(2,1)}), bf16[4,64,1024]{2,1,0:T(8,128)(2,1)S(1)}, u32[]{:S(2)}, u32[]{:S(2)}) async-start(bf16[4,64,1024]{2,1,0:T(8,128)(2,1)} %bitcast.87), calls=%async_computation.1 | async-start | bytes 1048576 | tf_op jit(solution)/shard_map/all_to_all | solution.py:75
  95.4 87.1 %all-gather.2.cloned.1.call-start = ((), (), s32[]{:S(2)}) async-start(), calls=%async_computation.9 | async-start | bytes 2621440 | tf_op jit(solution)/shard_map/all_gather | solution.py:126
  152.9 81.5 %reduce-scatter.8.cloned.1.call-start = ((), (), s32[]{:S(2)}) async-start(), calls=%async_computation.10 | async-start | bytes 2621440 | tf_op jit(solution)/shard_map/reduce_scatter | solution.py:142
  153.0 43.9 %collective-permute-start.1 = (bf16[1,704,2048]{2,1,0:T(8,128)(2,1)}, bf16[1,704,2048]{2,1,0:T(8,128)(2,1)}, u32[]{:S(2)}, u32[]{:S(2)}) collective-permute-start(bf16[1,704,2048]{2,1,0:T(8,128)(2,1)} %param.26), channel_id=1, source_target_pairs={{0,32},{32,0},{1,33},{33,1},{2,34},{34,2},{3,35},{35,3},{4,36},{36... | collective-permute-start | bytes 8650760 | tf_op jit(solution)/shard_map/ppermute | solution.py:129
  182.5 6.6 %copy-start.10 = (bf16[1,704,2048]{2,1,0:T(8,128)(2,1)S(1)}, bf16[1,704,2048]{2,1,0:T(8,128)(2,1)}, u32[]{:S(2)}) copy-start(bf16[1,704,2048]{2,1,0:T(8,128)(2,1)} %param.26) | copy-start | bytes 8650756
  189.1 1.9 copy-start.12
  196.9 5.4 %copy-start.7 = (bf16[2048]{0:T(1024)(128)(2,1)S(1)}, bf16[2048]{0:T(1024)(128)(2,1)}, u32[]{:S(2)}) copy-start(bf16[2048]{0:T(1024)(128)(2,1)} %param.27) | copy-start | bytes 12292
  236.5 27.3 %all-to-all-start.3 = ((bf16[32,4,2048]{2,1,0:T(4,128)(2,1)}), bf16[32,4,2048]{2,1,0:T(4,128)(2,1)S(1)}, u32[]{:S(2)}, u32[]{:S(2)}) async-start(bf16[32,4,2048]{2,1,0:T(4,128)(2,1)} %all_to_all.35), calls=%async_computation.6 | async-start | bytes 1048576 | tf_op jit(solution)/shard_map/all_to_all | solution.py:143
Sparse Core Ops, SparseCore 0:
  19.4 56.1 reduce-scatter.3
  90.4 38.5 reduce-scatter.5
  153.1 29.3 all-gather.1
  202.1 32.2 reduce-scatter.7

commit v9 on v6

--- a/solution.py
+++ b/solution.py
@@ -7,7 +7,7 @@
 TENSOR = ("tz", "ty")
 EXPERT = ("ex", "ec")
 ALL = ("ex", "ec", "tz", "ty")
-Z_SHARE = 4
+Z_SHARE = 9
 
 
 norm_eps = 1e-06
@@ -60,7 +60,7 @@
     weight_flat = att_out_w.reshape(width, model_width)
     n_y = lax.axis_size("ty")
     n_z = lax.axis_size("tz")
-    split = model_width * Z_SHARE // 8
+    split = model_width * Z_SHARE // 16
     z_first = jnp.dot(row_block, weight_flat[:, :split], preferred_element_type=jnp.float32)
     z_first = lax.psum_scatter(z_first.astype(jnp.bfloat16), "tz", scatter_dimension=0, tiled=True)
     z_first = lax.all_to_all(z_first, "ty", split_axis=0, concat_axis=0, tiled=True)

time: 264 us -> 263 us (level)
  blocking collectives: 74.1 us -> 68.8 us
  waiting for transfers between devices: 110 us -> 115 us
    all_to_all x1, blocking collectives: 53.2 us -> 47.5 us  [per_device(): lax.all_to_all(y_first.astype(jnp.bfloat16), 'ty', split_axis=0, concat_a...]
    reduce_scatter x1, waiting for transfers between devices: 33.3 us -> 35.9 us  [per_device(): lax.psum_scatter(y_first.astype(jnp.bfloat16), 'tz', scatter_dimension=0,...]
  transfers between devices with their start and end apart: 8 -> 8, of which waited for: 4 -> 5; matrix products, arithmetic and copies ran while one was open for 11% -> 11% of each run, Pallas kernels for 0% -> 0%
where the time goes in v9:
time: 263 us; the launch traced here: 262 us
  waiting for transfers between devices  115 us (44%)
  blocking collectives  68.8 us (26%)
  matrix products  31.1 us (12%)
  starting transfers between devices  14.9 us (6%)
  between operations  14.1 us (5%)
  local copies, waits for them, and re-layouts  10.6 us (4%)
  other arithmetic  7.93 us (3%)
    all_to_all x1, blocking collectives, per_device(): lax.all_to_all(y_first.astype(jnp.bfloat16), 'ty', split_axis=0, concat_a...  47.5 us
    reduce_scatter x1, waiting for transfers between devices, per_device(): lax.psum_scatter(y_first.astype(jnp.bfloat16), 'tz', scatter_dimension=0,...  35.9 us
    reduce_scatter x1, waiting for transfers between devices, per_device(): lax.psum_scatter(down.astype(jnp.bfloat16), 'ex', scatter_dimension=0, ti...  32.1 us
    all_gather x1, waiting for transfers between devices, per_device(): arrived = lax.all_gather(exchanged, 'ex', axis=0, tiled=True)  29.4 us
    all_to_all x1, blocking collectives, per_device(): lax.all_to_all(send_rows, TENSOR, split_axis=0, concat_axis=0, tiled=True)  21.2 us
    all_to_all x1, waiting for transfers between devices, per_device(): lax.all_to_all(summed, TENSOR, split_axis=0, concat_axis=0, tiled=True)  15.6 us
    dot_general x2, matrix products, expert_part(): jnp.dot(arrived, gate_up.reshape(model_width, 2 * hidden_units), preferre...  12.4 us
    all_to_all x1, starting transfers between devices, per_device(): lax.all_to_all(summed, TENSOR, split_axis=0, concat_axis=0, tiled=True)  10.1 us
  transfers between devices with their start and end apart: 8, of which 5 were waited for; matrix products, arithmetic and copies ran while one was open for 11% of the time, Pallas kernels for 0%

profile of v9, /device:TPU:32, one launch (start us, length us, event | category | flops | bytes accessed | tf_op | source)
XLA Modules:
  0.0 262.0 jit_solution(8756778609999525386)
XLA Ops:
  7.2 0.8 fusion.42
  8.1 0.8 broadcast_subtract_fusion
  8.9 0.7 fusion.20
  9.7 1.5 fusion.1
  11.2 1.3 copy-done.1
  12.6 4.7 %convolution_convert_fusion = bf16[2048,1152]{1,0:T(8,128)(2,1)} fusion(bf16[2048,512]{0,1:T(8,128)(2,1)S(1)} %fusion.1, bf16[512,2048]{1,0:T(8,128)(2,1)S(1)} %bitcast.55), kind=kOutput, calls=%fused_computation.1 | convolution fusion | flops 2418278400 | bytes 7995392 | tf_op jit(solution)/shard_map/dot_general | solution.py:64
  17.3 2.9 %copy.56 = bf16[2048,512]{1,0:T(8,128)(2,1)S(1)} copy(bf16[2048,512]{0,1:T(8,128)(2,1)} %copy-done.1) | data formatting | bytes 4194304 | tf_op jit(solution)/shard_map/convert_element_type | solution.py:59
  20.2 0.1 copy.57
  20.3 3.6 %convolution_convert_fusion.1 = bf16[2048,896]{1,0:T(8,128)(2,1)S(1)} fusion(bf16[2048,512]{1,0:T(8,128)(2,1)S(1)} %bitcast.47, bf16[512,2048]{1,0:T(8,128)(2,1)} %bitcast.54), kind=kOutput, calls=%fused_computation.7 | convolution fusion | flops 1880883200 | bytes 6684672 | tf_op jit(solution)/shard_map/dot_general | solution.py:69
  23.9 47.5 %all_to_all.42 = bf16[4,512,896]{2,1,0:T(8,128)(2,1)} all-to-all(bf16[4,512,896]{2,1,0:T(8,128)(2,1)S(1)} %bitcast.46), channel_id=1, replica_groups=mesh['ex'=4,'ec'=2,'tz'=8,'ty'=4] {'ty'}, dimensions={0} | all-to-all | bytes 7340032 | tf_op jit(solution)/shard_map/all_to_all | solution.py:70
  71.5 3.7 %reduce_sum.115 = bf16[512,896]{1,0:T(8,128)(2,1)} reduce(bf16[4,512,896]{2,1,0:T(8,128)(2,1)} %all_to_all.42, bf16[]{:T(256)} %constant.108.clone.1), dimensions={0}, to_apply=%region_2.3 | reduce | flops 1376256 | bytes 4587522 | tf_op jit(solution)/shard_map/reduce_sum | solution.py:71
  75.4 0.1 copy.58
  75.5 0.1 convert_reduce_fusion.2
  75.7 0.1 and_select_fusion.1
  75.9 0.1 eq.202
  76.1 0.1 eq.188
  76.2 0.2 convert_reduce_fusion.1
  76.4 0.1 fusion.28
  76.5 0.2 reduce_window_sum.11
  76.7 0.2 select_reduce_fusion.1
  76.9 0.1 reshape.166
  77.1 1.4 reduce-scatter.4.cloned.1.call-done
  78.5 4.3 %all-to-all-start = ((bf16[4,64,1152]{2,1,0:T(8,128)(2,1)}), bf16[4,64,1152]{2,1,0:T(8,128)(2,1)S(1)}, u32[]{:S(2)}, u32[]{:S(2)}) async-start(bf16[4,64,1152]{2,1,0:T(8,128)(2,1)} %bitcast.48), calls=%async_computation.1 | async-start | bytes 1179648 | tf_op jit(solution)/shard_map/all_to_all | solution.py:66
  83.0 35.9 %reduce-scatter.6.cloned.1.call-done = bf16[64,896]{1,0:T(8,128)(2,1)} async-done(((bf16[512,896]{1,0:T(8,128)(2,1)}), bf16[64,896]{1,0:T(8,128)(2,1)}) %reduce-scatter.6.cloned.1.call-update) | async-done | bytes 114704 | tf_op jit(solution)/shard_map/reduce_scatter | solution.py:72
  118.9 0.9 convert_element_type.79
  119.9 0.2 fusion.13
  120.1 0.4 convolution_convert_fusion.2
  120.5 0.2 all_to_all.32
  120.7 21.2 %all_to_all.43 = bf16[32,4,2048]{2,1,0:T(4,128)(2,1)S(1)} all-to-all(bf16[32,4,2048]{2,1,0:T(4,128)(2,1)S(1)} %all_to_all.32), channel_id=1, replica_groups=mesh['ex'=4,'ec'=2,'tz'=8,'ty'=4] {'tz','ty'}, dimensions={0} | all-to-all | bytes 1048576 | tf_op jit(solution)/shard_map/all_to_all | solution.py:117
  141.9 0.9 all_to_all.34
  142.9 0.3 collective-permute-start.1
  143.2 29.4 %all-gather.2.cloned.1.call-done = bf16[512,2048]{1,0:T(8,128)(2,1)} async-done(((bf16[128,2048]{1,0:T(8,128)(2,1)}), bf16[512,2048]{1,0:T(8,128)(2,1)}) %all-gather.2.cloned.1.call-update) | async-done | bytes 2097168 | tf_op jit(solution)/shard_map/all_gather | solution.py:118
  172.6 6.6 %fusion.43 = f32[512,1408]{1,0:T(8,128)S(1)} fusion(bf16[512,2048]{1,0:T(8,128)(2,1)} %all-gather.2.cloned.1.call-done, bf16[2048,1408]{0,1:T(8,128)(2,1)} %bitcast.53), kind=kOutput, calls=%fused_computation.89 | convolution fusion | flops 2952790016 | bytes 10747904 | tf_op jit(solution)/shard_map/dot_general | solution.py:125
  179.2 1.9 fusion.3
  181.2 5.8 %fusion.44 = f32[512,1408]{1,0:T(8,128)S(1)} fusion(bf16[512,2048]{1,0:T(8,128)(2,1)S(1)} %copy-done.11, bf16[2048,1408]{0,1:T(8,128)(2,1)} %bitcast.15), kind=kOutput, calls=%fused_computation.90 | convolution fusion | flops 2952790016 | bytes 10747904 | tf_op jit(solution)/shard_map/dot_general | solution.py:125
  187.0 5.1 %add_convert_fusion = bf16[512,2048]{1,0:T(8,128)(2,1)} fusion(f32[512,2048]{1,0:T(8,128)S(1)} %fusion.3, bf16[1,704,2048]{2,1,0:T(8,128)(2,1)} %collective-permute-done.1, f32[512,1408]{1,0:T(8,128)S(1)} %fusion.44), kind=kOutput, calls=%fused_computation.6 | convolution fusion | flops 1480654848 | bytes 12320768 | tf_op jit(solution)/shard_map/dot_general | solution.py:129
  192.3 0.1 reshape.172
  192.5 32.1 %reduce-scatter.8.cloned.1.call-done = bf16[128,2048]{1,0:T(8,128)(2,1)} async-done(((bf16[512,2048]{1,0:T(8,128)(2,1)}), bf16[128,2048]{1,0:T(8,128)(2,1)}) %reduce-scatter.8.cloned.1.call-update) | async-done | bytes 524304 | tf_op jit(solution)/shard_map/reduce_scatter | solution.py:134
  224.6 2.0 all_to_all.35
  226.6 10.1 %all-to-all-start.3 = ((bf16[32,4,2048]{2,1,0:T(4,128)(2,1)}), bf16[32,4,2048]{2,1,0:T(4,128)(2,1)S(1)}, u32[]{:S(2)}, u32[]{:S(2)}) async-start(bf16[32,4,2048]{2,1,0:T(4,128)(2,1)} %all_to_all.35), calls=%async_computation.6 | async-start | bytes 1048576 | tf_op jit(solution)/shard_map/all_to_all | solution.py:135
  236.8 0.2 fusion.25
  237.0 1.0 gather_fusion
  238.0 0.1 reshape.175
  238.3 0.1 select_reduce_fusion
  238.4 15.6 %all-to-all-done.3 = bf16[32,4,2048]{2,1,0:T(4,128)(2,1)S(1)} async-done(((bf16[32,4,2048]{2,1,0:T(4,128)(2,1)}), bf16[32,4,2048]{2,1,0:T(4,128)(2,1)S(1)}, u32[]{:S(2)}, u32[]{:S(2)}) %all-to-all-start.3) | async-done | bytes 524320 | tf_op jit(solution)/shard_map/all_to_all | solution.py:135
  254.0 0.1 all_to_all.37
  254.1 0.5 multiply_reduce_fusion
  254.6 0.8 multiply_convert_fusion
  (56 shorter events, 1.1 us)
Async XLA Ops:
  7.2 1.7 copy-start
  7.2 71.3 %reduce-scatter.4.cloned.1.call-start = ((), (), s32[]{:S(2)}) async-start(), calls=%async_computation.7 | async-start | bytes 5308416 | tf_op jit(solution)/shard_map/reduce_scatter | solution.py:65
  9.6 2.9 %copy-start.10 = (bf16[8,64,2048]{2,1,0:T(8,128)(2,1)S(1)}, bf16[8,64,2048]{2,1,0:T(8,128)(2,1)}, u32[]{:S(2)}) copy-start(bf16[8,64,2048]{2,1,0:T(8,128)(2,1)} %param.18) | copy-start | bytes 6291460
  11.2 1.4 copy-start.1
  17.2 101.7 %reduce-scatter.6.cloned.1.call-start = ((), (), s32[]{:S(2)}) async-start(), calls=%async_computation.8 | async-start | bytes 1032192 | tf_op jit(solution)/shard_map/reduce_scatter | solution.py:72
  71.5 3.9 %copy-start.3 = (s32[64,2]{0,1:T(2,128)S(1)}, s32[64,2]{0,1:T(2,128)}, u32[]{:S(2)}) copy-start(s32[64,2]{0,1:T(2,128)} %param.21) | copy-start | bytes 1540
  71.5 4.0 %copy-start.4 = (s32[32]{0:T(128)S(1)}, s32[32]{0:T(128)}, u32[]{:S(2)}) copy-start(s32[32]{0:T(128)} %param.23) | copy-start | bytes 388
  71.5 4.2 %copy-start.7 = (s32[64,2]{0,1:T(2,128)S(1)}, s32[64,2]{0,1:T(2,128)}, u32[]{:S(2)}) copy-start(s32[64,2]{0,1:T(2,128)} %param.22) | copy-start | bytes 1540
  71.5 5.6 %copy-start.5 = (bf16[2048]{0:T(1024)(128)(2,1)S(1)}, bf16[2048]{0:T(1024)(128)(2,1)}, u32[]{:S(2)}) copy-start(bf16[2048]{0:T(1024)(128)(2,1)} %param.19) | copy-start | bytes 12292
  71.5 11.3 %copy-start.8 = (s32[32]{0:T(128)S(1)}, s32[32]{0:T(128)}, u32[]{:S(2)}) copy-start(s32[32]{0:T(128)} %param.24) | copy-start | bytes 388
  75.3 44.6 %copy-start.2 = (bf16[64,2048]{1,0:T(8,128)(2,1)S(1)}, bf16[64,2048]{1,0:T(8,128)(2,1)}, u32[]{:S(2)}) copy-start(bf16[64,2048]{1,0:T(8,128)(2,1)} %param.14) | copy-start | bytes 786436
  75.3 105.9 %collective-permute-start = (bf16[1,2048,2,704]{1,3,2,0:T(8,128)(2,1)}, bf16[1,2048,2,704]{1,3,2,0:T(8,128)(2,1)}, u32[]{:S(2)}, u32[]{:S(2)}) collective-permute-start(bf16[1,2048,2,704]{1,3,2,0:T(8,128)(2,1)} %param.25), channel_id=1, source_target_pairs={{0,32},{32,0},{1,33},{33,1},{2,34},{34,2},{3,35},{35,3},{4,36},{36... | collective-permute-start | bytes 17301512 | tf_op jit(solution)/shard_map/ppermute | solution.py:120
  78.5 41.4 %all-to-all-start = ((bf16[4,64,1152]{2,1,0:T(8,128)(2,1)}), bf16[4,64,1152]{2,1,0:T(8,128)(2,1)S(1)}, u32[]{:S(2)}, u32[]{:S(2)}) async-start(bf16[4,64,1152]{2,1,0:T(8,128)(2,1)} %bitcast.48), calls=%async_computation.1 | async-start | bytes 1179648 | tf_op jit(solution)/shard_map/all_to_all | solution.py:66
  82.8 89.9 %all-gather.2.cloned.1.call-start = ((), (), s32[]{:S(2)}) async-start(), calls=%async_computation.9 | async-start | bytes 2621440 | tf_op jit(solution)/shard_map/all_gather | solution.py:118
  142.8 81.8 %reduce-scatter.8.cloned.1.call-start = ((), (), s32[]{:S(2)}) async-start(), calls=%async_computation.10 | async-start | bytes 2621440 | tf_op jit(solution)/shard_map/reduce_scatter | solution.py:134
  142.9 44.2 %collective-permute-start.1 = (bf16[1,704,2048]{2,1,0:T(8,128)(2,1)}, bf16[1,704,2048]{2,1,0:T(8,128)(2,1)}, u32[]{:S(2)}, u32[]{:S(2)}) collective-permute-start(bf16[1,704,2048]{2,1,0:T(8,128)(2,1)} %param.26), channel_id=1, source_target_pairs={{0,32},{32,0},{1,33},{33,1},{2,34},{34,2},{3,35},{35,3},{4,36},{36... | collective-permute-start | bytes 8650760 | tf_op jit(solution)/shard_map/ppermute | solution.py:121
  172.6 6.6 %copy-start.9 = (bf16[1,704,2048]{2,1,0:T(8,128)(2,1)S(1)}, bf16[1,704,2048]{2,1,0:T(8,128)(2,1)}, u32[]{:S(2)}) copy-start(bf16[1,704,2048]{2,1,0:T(8,128)(2,1)} %param.26) | copy-start | bytes 8650756
  179.2 1.9 copy-start.11
  187.0 5.4 %copy-start.6 = (bf16[2048]{0:T(1024)(128)(2,1)S(1)}, bf16[2048]{0:T(1024)(128)(2,1)}, u32[]{:S(2)}) copy-start(bf16[2048]{0:T(1024)(128)(2,1)} %param.27) | copy-start | bytes 12292
  192.2 44.6 %copy-start.12 = (bf16[2048,8]{0,1:T(8,128)(2,1)S(1)}, bf16[2048,8]{0,1:T(8,128)(2,1)}, u32[]{:S(2)}) copy-start(bf16[2048,8]{0,1:T(8,128)(2,1)} %param.20) | copy-start | bytes 98308
  226.6 27.4 %all-to-all-start.3 = ((bf16[32,4,2048]{2,1,0:T(4,128)(2,1)}), bf16[32,4,2048]{2,1,0:T(4,128)(2,1)S(1)}, u32[]{:S(2)}, u32[]{:S(2)}) async-start(bf16[32,4,2048]{2,1,0:T(4,128)(2,1)} %all_to_all.35), calls=%async_computation.6 | async-start | bytes 1048576 | tf_op jit(solution)/shard_map/all_to_all | solution.py:135
Sparse Core Ops, SparseCore 0:
  17.4 61.0 reduce-scatter.3
  81.0 37.8 reduce-scatter.5
  143.0 29.6 all-gather.1
  192.3 32.2 reduce-scatter.7

commit v10 on v9

--- a/solution.py
+++ b/solution.py
@@ -1,4 +1,6 @@
 import jax
+import ml_dtypes
+import numpy as np
 import jax.numpy as jnp
 from jax import lax
 from jax.sharding import Mesh, PartitionSpec as P
@@ -48,13 +50,15 @@
     top_count = att_routes.shape[1]
     gate_att = pair_gates(att_scores)
     width = att_experts * slice_ctx
-    column = jnp.arange(width, dtype=jnp.int32)
-    source = jnp.arange(slice_ctx * top_count, dtype=jnp.int32)[:, None]
+    column = np.arange(width)
+    source = np.arange(slice_ctx * top_count)[:, None]
+    owner = jnp.asarray((column // slice_ctx)[None, :].astype(np.int32))
     mixed = jnp.zeros((group_rows, width), jnp.float32)
     for choice in range(top_count):
-        spread = (source == (column % slice_ctx)[None, :] * top_count + choice).astype(jnp.bfloat16)
+        spread = source == (column % slice_ctx)[None, :] * top_count + choice
+        spread = jnp.asarray(spread.astype(ml_dtypes.bfloat16))
         picked = jnp.dot(contexts, spread, preferred_element_type=jnp.float32)
-        chosen = att_routes[:, choice : choice + 1] == (column // slice_ctx)[None, :]
+        chosen = att_routes[:, choice : choice + 1] == owner
         mixed = mixed + jnp.where(chosen, picked * gate_att[:, choice : choice + 1], 0.0)
     row_block = mixed.astype(jnp.bfloat16)
     weight_flat = att_out_w.reshape(width, model_width)

time: 263 us -> 263 us (level)
  no operation moved by 1% of the time
where the time goes in v10:
time: 263 us
  waiting for transfers between devices  114 us (43%)
  blocking collectives  68.8 us (26%)
  matrix products  32 us (12%)
  starting transfers between devices  14.9 us (6%)
  between operations  14.1 us (5%)
  local copies, waits for them, and re-layouts  10.6 us (4%)
  other arithmetic  7.92 us (3%)
    all_to_all x1, blocking collectives, per_device(): lax.all_to_all(y_first.astype(jnp.bfloat16), 'ty', split_axis=0, concat_a...  47.6 us
    reduce_scatter x1, waiting for transfers between devices, per_device(): lax.psum_scatter(y_first.astype(jnp.bfloat16), 'tz', scatter_dimension=0,...  36 us
    reduce_scatter x1, waiting for transfers between devices, per_device(): lax.psum_scatter(down.astype(jnp.bfloat16), 'ex', scatter_dimension=0, ti...  32.2 us
    all_gather x1, waiting for transfers between devices, per_device(): arrived = lax.all_gather(exchanged, 'ex', axis=0, tiled=True)  29 us
    all_to_all x1, blocking collectives, per_device(): lax.all_to_all(send_rows, TENSOR, split_axis=0, concat_axis=0, tiled=True)  21.3 us
    all_to_all x1, waiting for transfers between devices, per_device(): lax.all_to_all(summed, TENSOR, split_axis=0, concat_axis=0, tiled=True)  15.6 us
    dot_general x2, matrix products, expert_part(): jnp.dot(arrived, gate_up.reshape(model_width, 2 * hidden_units), preferre...  12.4 us
    all_to_all x1, starting transfers between devices, per_device(): lax.all_to_all(summed, TENSOR, split_axis=0, concat_axis=0, tiled=True)  10.1 us
  transfers between devices with their start and end apart: 8, of which 5 were waited for; matrix products, arithmetic and copies ran while one was open for 11% of the time, Pallas kernels for 0%

profile of v10, /device:TPU:32, one launch (start us, length us, event | category | flops | bytes accessed | tf_op | source)
XLA Modules:
  0.0 262.6 jit_solution(15316673456897120611)
XLA Ops:
  7.3 0.8 fusion.27
  8.1 0.8 broadcast_subtract_fusion
  8.9 1.6 fusion.28
  10.6 1.5 fusion.1
  12.1 1.3 copy-done.1
  13.5 4.7 %convolution_convert_fusion = bf16[2048,1152]{1,0:T(8,128)(2,1)} fusion(bf16[2048,512]{0,1:T(8,128)(2,1)S(1)} %fusion.1, bf16[512,2048]{1,0:T(8,128)(2,1)S(1)} %bitcast.57), kind=kOutput, calls=%fused_computation.1 | convolution fusion | flops 2418278400 | bytes 7995392 | tf_op jit(solution)/shard_map/dot_general | solution.py:68
  18.2 2.9 %copy.59 = bf16[2048,512]{1,0:T(8,128)(2,1)S(1)} copy(bf16[2048,512]{0,1:T(8,128)(2,1)} %copy-done.1) | data formatting | bytes 4194304 | tf_op jit(solution)/shard_map/convert_element_type | solution.py:63
  21.1 0.1 copy.60
  21.2 3.6 %convolution_convert_fusion.1 = bf16[2048,896]{1,0:T(8,128)(2,1)S(1)} fusion(bf16[2048,512]{1,0:T(8,128)(2,1)S(1)} %bitcast.49, bf16[512,2048]{1,0:T(8,128)(2,1)} %bitcast.56), kind=kOutput, calls=%fused_computation.7 | convolution fusion | flops 1880883200 | bytes 6684672 | tf_op jit(solution)/shard_map/dot_general | solution.py:73
  24.8 47.6 %all_to_all.42 = bf16[4,512,896]{2,1,0:T(8,128)(2,1)} all-to-all(bf16[4,512,896]{2,1,0:T(8,128)(2,1)S(1)} %bitcast.48), channel_id=1, replica_groups=mesh['ex'=4,'ec'=2,'tz'=8,'ty'=4] {'ty'}, dimensions={0} | all-to-all | bytes 7340032 | tf_op jit(solution)/shard_map/all_to_all | solution.py:74
  72.4 3.7 %reduce_sum.115 = bf16[512,896]{1,0:T(8,128)(2,1)} reduce(bf16[4,512,896]{2,1,0:T(8,128)(2,1)} %all_to_all.42, bf16[]{:T(256)} %constant.75.clone.1), dimensions={0}, to_apply=%region_2.3 | reduce | flops 1376256 | bytes 4587522 | tf_op jit(solution)/shard_map/reduce_sum | solution.py:75
  76.3 0.1 copy.61
  76.4 0.1 convert_reduce_fusion.2
  76.6 0.1 and_select_fusion.1
  76.9 0.1 eq.168
  77.0 0.1 eq.154
  77.1 0.2 convert_reduce_fusion.1
  77.3 0.1 fusion.21
  77.4 0.2 reduce_window_sum.11
  77.6 0.2 select_reduce_fusion.1
  77.8 0.1 reshape.138
  78.0 1.4 reduce-scatter.4.cloned.1.call-done
  79.4 4.3 %all-to-all-start = ((bf16[4,64,1152]{2,1,0:T(8,128)(2,1)}), bf16[4,64,1152]{2,1,0:T(8,128)(2,1)S(1)}, u32[]{:S(2)}, u32[]{:S(2)}) async-start(bf16[4,64,1152]{2,1,0:T(8,128)(2,1)} %bitcast.50), calls=%async_computation.1 | async-start | bytes 1179648 | tf_op jit(solution)/shard_map/all_to_all | solution.py:70
  83.9 36.0 %reduce-scatter.6.cloned.1.call-done = bf16[64,896]{1,0:T(8,128)(2,1)} async-done(((bf16[512,896]{1,0:T(8,128)(2,1)}), bf16[64,896]{1,0:T(8,128)(2,1)}) %reduce-scatter.6.cloned.1.call-update) | async-done | bytes 114704 | tf_op jit(solution)/shard_map/reduce_scatter | solution.py:76
  119.8 0.9 convert_element_type.77
  120.9 0.2 fusion.13
  121.0 0.4 convolution_convert_fusion.2
  121.4 0.2 all_to_all.32
  121.6 21.3 %all_to_all.43 = bf16[32,4,2048]{2,1,0:T(4,128)(2,1)S(1)} all-to-all(bf16[32,4,2048]{2,1,0:T(4,128)(2,1)S(1)} %all_to_all.32), channel_id=1, replica_groups=mesh['ex'=4,'ec'=2,'tz'=8,'ty'=4] {'tz','ty'}, dimensions={0} | all-to-all | bytes 1048576 | tf_op jit(solution)/shard_map/all_to_all | solution.py:121
  142.9 0.9 all_to_all.34
  143.9 0.3 collective-permute-start.1
  144.2 29.0 %all-gather.2.cloned.1.call-done = bf16[512,2048]{1,0:T(8,128)(2,1)} async-done(((bf16[128,2048]{1,0:T(8,128)(2,1)}), bf16[512,2048]{1,0:T(8,128)(2,1)}) %all-gather.2.cloned.1.call-update) | async-done | bytes 2097168 | tf_op jit(solution)/shard_map/all_gather | solution.py:122
  173.2 6.6 %fusion.29 = f32[512,1408]{1,0:T(8,128)S(1)} fusion(bf16[512,2048]{1,0:T(8,128)(2,1)} %all-gather.2.cloned.1.call-done, bf16[2048,1408]{0,1:T(8,128)(2,1)} %bitcast.55), kind=kOutput, calls=%fused_computation.70 | convolution fusion | flops 2952790016 | bytes 10747904 | tf_op jit(solution)/shard_map/dot_general | solution.py:129
  179.8 1.9 fusion.3
  181.8 5.8 %fusion.30 = f32[512,1408]{1,0:T(8,128)S(1)} fusion(bf16[512,2048]{1,0:T(8,128)(2,1)S(1)} %copy-done.11, bf16[2048,1408]{0,1:T(8,128)(2,1)} %bitcast.15), kind=kOutput, calls=%fused_computation.71 | convolution fusion | flops 2952790016 | bytes 10747904 | tf_op jit(solution)/shard_map/dot_general | solution.py:129
  187.6 5.1 %add_convert_fusion = bf16[512,2048]{1,0:T(8,128)(2,1)} fusion(f32[512,2048]{1,0:T(8,128)S(1)} %fusion.3, bf16[1,704,2048]{2,1,0:T(8,128)(2,1)} %collective-permute-done.1, f32[512,1408]{1,0:T(8,128)S(1)} %fusion.30), kind=kOutput, calls=%fused_computation.6 | convolution fusion | flops 1480654848 | bytes 12320768 | tf_op jit(solution)/shard_map/dot_general | solution.py:133
  192.9 0.1 reshape.144
  193.0 32.2 %reduce-scatter.8.cloned.1.call-done = bf16[128,2048]{1,0:T(8,128)(2,1)} async-done(((bf16[512,2048]{1,0:T(8,128)(2,1)}), bf16[128,2048]{1,0:T(8,128)(2,1)}) %reduce-scatter.8.cloned.1.call-update) | async-done | bytes 524304 | tf_op jit(solution)/shard_map/reduce_scatter | solution.py:138
  225.2 2.0 all_to_all.35
  227.2 10.1 %all-to-all-start.3 = ((bf16[32,4,2048]{2,1,0:T(4,128)(2,1)}), bf16[32,4,2048]{2,1,0:T(4,128)(2,1)S(1)}, u32[]{:S(2)}, u32[]{:S(2)}) async-start(bf16[32,4,2048]{2,1,0:T(4,128)(2,1)} %all_to_all.35), calls=%async_computation.6 | async-start | bytes 1048576 | tf_op jit(solution)/shard_map/all_to_all | solution.py:139
  237.3 0.2 fusion.18
  237.6 1.0 gather_fusion
  238.6 0.1 reshape.147
  238.9 0.1 select_reduce_fusion
  239.0 15.6 %all-to-all-done.3 = bf16[32,4,2048]{2,1,0:T(4,128)(2,1)S(1)} async-done(((bf16[32,4,2048]{2,1,0:T(4,128)(2,1)}), bf16[32,4,2048]{2,1,0:T(4,128)(2,1)S(1)}, u32[]{:S(2)}, u32[]{:S(2)}) %all-to-all-start.3) | async-done | bytes 524320 | tf_op jit(solution)/shard_map/all_to_all | solution.py:139
  254.6 0.1 all_to_all.37
  254.7 0.5 multiply_reduce_fusion
  255.2 0.8 multiply_convert_fusion
  (58 shorter events, 1.1 us)
Async XLA Ops:
  7.2 1.7 copy-start
  7.2 3.4 %copy-start.13 = (bf16[128,512]{1,0:T(8,128)(2,1)S(1)}, bf16[128,512]{1,0:T(8,128)(2,1)}, u32[]{:S(2)}) copy-start(bf16[128,512]{1,0:T(8,128)(2,1)} %constant.88.clone) | copy-start | bytes 393220
  7.2 3.4 %copy-start.14 = (s32[512]{0:T(512)S(1)}, s32[512]{0:T(512)}, u32[]{:S(2)}) copy-start(s32[512]{0:T(512)} %constant.94) | copy-start | bytes 6148
  7.2 72.2 %reduce-scatter.4.cloned.1.call-start = ((), (), s32[]{:S(2)}) async-start(), calls=%async_computation.7 | async-start | bytes 5308416 | tf_op jit(solution)/shard_map/reduce_scatter | solution.py:69
  10.6 2.9 %copy-start.10 = (bf16[8,64,2048]{2,1,0:T(8,128)(2,1)S(1)}, bf16[8,64,2048]{2,1,0:T(8,128)(2,1)}, u32[]{:S(2)}) copy-start(bf16[8,64,2048]{2,1,0:T(8,128)(2,1)} %param.21) | copy-start | bytes 6291460
  12.1 1.4 copy-start.1
  18.1 101.7 %reduce-scatter.6.cloned.1.call-start = ((), (), s32[]{:S(2)}) async-start(), calls=%async_computation.8 | async-start | bytes 1032192 | tf_op jit(solution)/shard_map/reduce_scatter | solution.py:76
  72.4 3.9 %copy-start.3 = (s32[64,2]{0,1:T(2,128)S(1)}, s32[64,2]{0,1:T(2,128)}, u32[]{:S(2)}) copy-start(s32[64,2]{0,1:T(2,128)} %param.24) | copy-start | bytes 1540
  72.4 4.0 %copy-start.4 = (s32[32]{0:T(128)S(1)}, s32[32]{0:T(128)}, u32[]{:S(2)}) copy-start(s32[32]{0:T(128)} %param.26) | copy-start | bytes 388
  72.4 4.2 %copy-start.7 = (s32[64,2]{0,1:T(2,128)S(1)}, s32[64,2]{0,1:T(2,128)}, u32[]{:S(2)}) copy-start(s32[64,2]{0,1:T(2,128)} %param.25) | copy-start | bytes 1540
  72.4 5.6 %copy-start.5 = (bf16[2048]{0:T(1024)(128)(2,1)S(1)}, bf16[2048]{0:T(1024)(128)(2,1)}, u32[]{:S(2)}) copy-start(bf16[2048]{0:T(1024)(128)(2,1)} %param.22) | copy-start | bytes 12292
  72.4 11.2 %copy-start.8 = (s32[32]{0:T(128)S(1)}, s32[32]{0:T(128)}, u32[]{:S(2)}) copy-start(s32[32]{0:T(128)} %param.27) | copy-start | bytes 388
  76.2 44.7 %copy-start.2 = (bf16[64,2048]{1,0:T(8,128)(2,1)S(1)}, bf16[64,2048]{1,0:T(8,128)(2,1)}, u32[]{:S(2)}) copy-start(bf16[64,2048]{1,0:T(8,128)(2,1)} %param.17) | copy-start | bytes 786436
  76.2 105.5 %collective-permute-start = (bf16[1,2048,2,704]{1,3,2,0:T(8,128)(2,1)}, bf16[1,2048,2,704]{1,3,2,0:T(8,128)(2,1)}, u32[]{:S(2)}, u32[]{:S(2)}) collective-permute-start(bf16[1,2048,2,704]{1,3,2,0:T(8,128)(2,1)} %param.28), channel_id=1, source_target_pairs={{0,32},{32,0},{1,33},{33,1},{2,34},{34,2},{3,35},{35,3},{4,36},{36... | collective-permute-start | bytes 17301512 | tf_op jit(solution)/shard_map/ppermute | solution.py:124
  79.4 41.4 %all-to-all-start = ((bf16[4,64,1152]{2,1,0:T(8,128)(2,1)}), bf16[4,64,1152]{2,1,0:T(8,128)(2,1)S(1)}, u32[]{:S(2)}, u32[]{:S(2)}) async-start(bf16[4,64,1152]{2,1,0:T(8,128)(2,1)} %bitcast.50), calls=%async_computation.1 | async-start | bytes 1179648 | tf_op jit(solution)/shard_map/all_to_all | solution.py:70
  83.7 89.5 %all-gather.2.cloned.1.call-start = ((), (), s32[]{:S(2)}) async-start(), calls=%async_computation.9 | async-start | bytes 2621440 | tf_op jit(solution)/shard_map/all_gather | solution.py:122
  143.8 81.4 %reduce-scatter.8.cloned.1.call-start = ((), (), s32[]{:S(2)}) async-start(), calls=%async_computation.10 | async-start | bytes 2621440 | tf_op jit(solution)/shard_map/reduce_scatter | solution.py:138
  143.9 43.7 %collective-permute-start.1 = (bf16[1,704,2048]{2,1,0:T(8,128)(2,1)}, bf16[1,704,2048]{2,1,0:T(8,128)(2,1)}, u32[]{:S(2)}, u32[]{:S(2)}) collective-permute-start(bf16[1,704,2048]{2,1,0:T(8,128)(2,1)} %param.29), channel_id=1, source_target_pairs={{0,32},{32,0},{1,33},{33,1},{2,34},{34,2},{3,35},{35,3},{4,36},{36... | collective-permute-start | bytes 8650760 | tf_op jit(solution)/shard_map/ppermute | solution.py:125
  173.2 6.6 %copy-start.9 = (bf16[1,704,2048]{2,1,0:T(8,128)(2,1)S(1)}, bf16[1,704,2048]{2,1,0:T(8,128)(2,1)}, u32[]{:S(2)}) copy-start(bf16[1,704,2048]{2,1,0:T(8,128)(2,1)} %param.29) | copy-start | bytes 8650756
  179.8 1.9 copy-start.11
  187.6 5.4 %copy-start.6 = (bf16[2048]{0:T(1024)(128)(2,1)S(1)}, bf16[2048]{0:T(1024)(128)(2,1)}, u32[]{:S(2)}) copy-start(bf16[2048]{0:T(1024)(128)(2,1)} %param.30) | copy-start | bytes 12292
  192.7 44.6 %copy-start.12 = (bf16[2048,8]{0,1:T(8,128)(2,1)S(1)}, bf16[2048,8]{0,1:T(8,128)(2,1)}, u32[]{:S(2)}) copy-start(bf16[2048,8]{0,1:T(8,128)(2,1)} %param.23) | copy-start | bytes 98308
  227.2 27.3 %all-to-all-start.3 = ((bf16[32,4,2048]{2,1,0:T(4,128)(2,1)}), bf16[32,4,2048]{2,1,0:T(4,128)(2,1)S(1)}, u32[]{:S(2)}, u32[]{:S(2)}) async-start(bf16[32,4,2048]{2,1,0:T(4,128)(2,1)} %all_to_all.35), calls=%async_computation.6 | async-start | bytes 1048576 | tf_op jit(solution)/shard_map/all_to_all | solution.py:139
Sparse Core Ops, SparseCore 0:
  18.3 61.0 reduce-scatter.3
  81.9 37.8 reduce-scatter.5
  144.0 29.2 all-gather.1
  192.9 32.2 reduce-scatter.7

commit v11 on v9

--- a/solution.py
+++ b/solution.py
@@ -63,14 +63,14 @@
     split = model_width * Z_SHARE // 16
     z_first = jnp.dot(row_block, weight_flat[:, :split], preferred_element_type=jnp.float32)
     z_first = lax.psum_scatter(z_first.astype(jnp.bfloat16), "tz", scatter_dimension=0, tiled=True)
-    z_first = lax.all_to_all(z_first, "ty", split_axis=0, concat_axis=0, tiled=True)
-    z_first = jnp.sum(z_first.reshape(n_y, -1, split).astype(jnp.float32), axis=0)
+    z_first = lax.psum_scatter(z_first, "ty", scatter_dimension=0, tiled=True).astype(jnp.float32)
     by_y = row_block.reshape(n_z, n_y, -1, width).transpose(1, 0, 2, 3).reshape(group_rows, width)
     y_first = jnp.dot(by_y, weight_flat[:, split:], preferred_element_type=jnp.float32)
     y_first = lax.all_to_all(y_first.astype(jnp.bfloat16), "ty", split_axis=0, concat_axis=0, tiled=True)
     y_first = jnp.sum(y_first.reshape(n_y, -1, model_width - split).astype(jnp.float32), axis=0)
-    y_first = lax.psum_scatter(y_first.astype(jnp.bfloat16), "tz", scatter_dimension=0, tiled=True)
-    attention = jnp.concatenate([z_first, y_first.astype(jnp.float32)], axis=1)
+    y_first = lax.all_to_all(y_first.astype(jnp.bfloat16), "tz", split_axis=0, concat_axis=0, tiled=True)
+    y_first = jnp.sum(y_first.reshape(n_z, -1, model_width - split).astype(jnp.float32), axis=0)
+    attention = jnp.concatenate([z_first, y_first], axis=1)
     stream = (resid.astype(jnp.float32) + attention).astype(jnp.bfloat16)
     normed = rms_norm(stream.astype(jnp.float32), norm_gain).astype(jnp.bfloat16)
     logits = jnp.dot(normed, router_w, preferred_element_type=jnp.float32)

time: 263 us -> 257 us (0.977)
  waiting for transfers between devices: 115 us -> 102 us
  starting transfers between devices: 14.9 us -> 19.2 us
  blocking collectives: 68.8 us -> 71.5 us
    reduce_scatter x1, waiting for transfers between devices: 35.9 us -> 3.46 us  [per_device(): lax.psum_scatter(z_first, 'ty', scatter_dimension=0, tiled=True)]
    all_to_all x1, waiting for transfers between devices: 0.01 us -> 20.8 us  [per_device(): lax.all_to_all(y_first.astype(jnp.bfloat16), 'tz', split_axis=0, concat_a...]
    all_to_all x1, starting transfers between devices: 4.29 us -> 8.72 us  [per_device(): lax.all_to_all(y_first.astype(jnp.bfloat16), 'tz', split_axis=0, concat_a...]
    all_to_all x1, blocking collectives: 21.2 us -> 24 us  [per_device(): lax.all_to_all(send_rows, TENSOR, split_axis=0, concat_axis=0, tiled=True)]
  transfers between devices with their start and end apart: 8 -> 8, of which waited for: 5 -> 5; matrix products, arithmetic and copies ran while one was open for 11% -> 12% of each run, Pallas kernels for 0% -> 0%
where the time goes in v11:
time: 257 us
  waiting for transfers between devices  102 us (40%)
  blocking collectives  71.5 us (28%)
  matrix products  31.1 us (12%)
  starting transfers between devices  19.2 us (7%)
  between operations  14.1 us (5%)
  local copies, waits for them, and re-layouts  10.6 us (4%)
  other arithmetic  7.99 us (3%)
    all_to_all x1, blocking collectives, per_device(): lax.all_to_all(y_first.astype(jnp.bfloat16), 'ty', split_axis=0, concat_a...  47.6 us
    reduce_scatter x1, waiting for transfers between devices, per_device(): lax.psum_scatter(down.astype(jnp.bfloat16), 'ex', scatter_dimension=0, ti...  32.1 us
    all_gather x1, waiting for transfers between devices, per_device(): arrived = lax.all_gather(exchanged, 'ex', axis=0, tiled=True)  29.6 us
    all_to_all x1, blocking collectives, per_device(): lax.all_to_all(send_rows, TENSOR, split_axis=0, concat_axis=0, tiled=True)  24 us
    all_to_all x1, waiting for transfers between devices, per_device(): lax.all_to_all(y_first.astype(jnp.bfloat16), 'tz', split_axis=0, concat_a...  20.8 us
    all_to_all x1, waiting for transfers between devices, per_device(): lax.all_to_all(summed, TENSOR, split_axis=0, concat_axis=0, tiled=True)  15.6 us
    dot_general x2, matrix products, expert_part(): jnp.dot(arrived, gate_up.reshape(model_width, 2 * hidden_units), preferre...  12.4 us
    all_to_all x1, starting transfers between devices, per_device(): lax.all_to_all(summed, TENSOR, split_axis=0, concat_axis=0, tiled=True)  10.1 us
  transfers between devices with their start and end apart: 8, of which 5 were waited for; matrix products, arithmetic and copies ran while one was open for 12% of the time, Pallas kernels for 0%

profile of v11, /device:TPU:32, one launch (start us, length us, event | category | flops | bytes accessed | tf_op | source)
XLA Modules:
  0.0 256.7 jit_solution(539719650118904905)
XLA Ops:
  7.2 0.8 fusion.42
  8.1 0.8 broadcast_subtract_fusion
  8.9 0.7 fusion.20
  9.7 1.5 fusion.1
  11.2 1.3 copy-done.1
  12.5 4.7 %convolution_convert_fusion = bf16[2048,1152]{1,0:T(8,128)(2,1)} fusion(bf16[2048,512]{0,1:T(8,128)(2,1)S(1)} %fusion.1, bf16[512,2048]{1,0:T(8,128)(2,1)S(1)} %bitcast.54), kind=kOutput, calls=%fused_computation.1 | convolution fusion | flops 2418278400 | bytes 7995392 | tf_op jit(solution)/shard_map/dot_general | solution.py:64
  17.2 2.9 %copy.56 = bf16[2048,512]{1,0:T(8,128)(2,1)S(1)} copy(bf16[2048,512]{0,1:T(8,128)(2,1)} %copy-done.1) | data formatting | bytes 4194304 | tf_op jit(solution)/shard_map/convert_element_type | solution.py:59
  20.1 0.1 copy.57
  20.3 3.6 %convolution_convert_fusion.1 = bf16[2048,896]{1,0:T(8,128)(2,1)S(1)} fusion(bf16[2048,512]{1,0:T(8,128)(2,1)S(1)} %bitcast.47, bf16[512,2048]{1,0:T(8,128)(2,1)} %bitcast.53), kind=kOutput, calls=%fused_computation.7 | convolution fusion | flops 1880883200 | bytes 6684672 | tf_op jit(solution)/shard_map/dot_general | solution.py:68
  23.9 47.6 %all_to_all.42 = bf16[4,512,896]{2,1,0:T(8,128)(2,1)} all-to-all(bf16[4,512,896]{2,1,0:T(8,128)(2,1)S(1)} %bitcast.46), channel_id=1, replica_groups=mesh['ex'=4,'ec'=2,'tz'=8,'ty'=4] {'ty'}, dimensions={0} | all-to-all | bytes 7340032 | tf_op jit(solution)/shard_map/all_to_all | solution.py:69
  71.5 3.7 %reduce_sum.114 = bf16[512,896]{1,0:T(8,128)(2,1)} reduce(bf16[4,512,896]{2,1,0:T(8,128)(2,1)} %all_to_all.42, bf16[]{:T(256)} %constant.108.clone.1), dimensions={0}, to_apply=%region_2.3 | reduce | flops 1376256 | bytes 4587522 | tf_op jit(solution)/shard_map/reduce_sum | solution.py:70
  75.2 8.7 %all-to-all-start.1 = ((bf16[8,64,896]{2,1,0:T(8,128)(2,1)}), bf16[8,64,896]{2,1,0:T(8,128)(2,1)S(1)}, u32[]{:S(2)}, u32[]{:S(2)}) async-start(bf16[8,64,896]{2,1,0:T(8,128)(2,1)} %bitcast.11), calls=%async_computation.3 | async-start | bytes 1835008 | tf_op jit(solution)/shard_map/all_to_all | solution.py:71
  84.0 0.1 convert_reduce_fusion.2
  84.2 0.5 reduce-scatter.6.cloned.1.call-update
  84.7 0.1 and_select_fusion.1
  85.1 0.1 eq.202
  85.2 0.1 eq.188
  85.3 0.2 convert_reduce_fusion.1
  85.5 0.1 fusion.28
  85.6 0.2 reduce_window_sum.11
  85.8 0.2 select_reduce_fusion.1
  86.0 0.1 reshape.166
  86.4 20.8 %all-to-all-done.1 = bf16[8,64,896]{2,1,0:T(8,128)(2,1)S(1)} async-done(((bf16[8,64,896]{2,1,0:T(8,128)(2,1)}), bf16[8,64,896]{2,1,0:T(8,128)(2,1)S(1)}, u32[]{:S(2)}, u32[]{:S(2)}) %all-to-all-start.1) | async-done | bytes 917536 | tf_op jit(solution)/shard_map/all_to_all | solution.py:71
  107.2 0.1 convert_reduce_fusion
  107.3 3.5 %reduce-scatter.6.cloned.1.call-done = bf16[64,1152]{1,0:T(8,128)(2,1)} async-done(((bf16[256,1152]{1,0:T(8,128)(2,1)}), bf16[64,1152]{1,0:T(8,128)(2,1)}) %reduce-scatter.6.cloned.1.call-update) | async-done | bytes 147472 | tf_op jit(solution)/shard_map/reduce_scatter | solution.py:66
  110.8 0.9 convert_element_type.77
  111.8 0.2 fusion.13
  111.9 0.4 convolution_convert_fusion.2
  112.3 0.2 all_to_all.32
  112.5 24.0 %all_to_all.43 = bf16[32,4,2048]{2,1,0:T(4,128)(2,1)S(1)} all-to-all(bf16[32,4,2048]{2,1,0:T(4,128)(2,1)S(1)} %all_to_all.32), channel_id=1, replica_groups=mesh['ex'=4,'ec'=2,'tz'=8,'ty'=4] {'tz','ty'}, dimensions={0} | all-to-all | bytes 1048576 | tf_op jit(solution)/shard_map/all_to_all | solution.py:117
  136.5 0.9 all_to_all.34
  137.5 0.3 collective-permute-start.1
  137.8 29.6 %all-gather.2.cloned.1.call-done = bf16[512,2048]{1,0:T(8,128)(2,1)} async-done(((bf16[128,2048]{1,0:T(8,128)(2,1)}), bf16[512,2048]{1,0:T(8,128)(2,1)}) %all-gather.2.cloned.1.call-update) | async-done | bytes 2097168 | tf_op jit(solution)/shard_map/all_gather | solution.py:118
  167.3 6.6 %fusion.43 = f32[512,1408]{1,0:T(8,128)S(1)} fusion(bf16[512,2048]{1,0:T(8,128)(2,1)} %all-gather.2.cloned.1.call-done, bf16[2048,1408]{0,1:T(8,128)(2,1)} %bitcast.52), kind=kOutput, calls=%fused_computation.89 | convolution fusion | flops 2952790016 | bytes 10747904 | tf_op jit(solution)/shard_map/dot_general | solution.py:125
  174.0 1.9 fusion.3
  175.9 5.8 %fusion.44 = f32[512,1408]{1,0:T(8,128)S(1)} fusion(bf16[512,2048]{1,0:T(8,128)(2,1)S(1)} %copy-done.11, bf16[2048,1408]{0,1:T(8,128)(2,1)} %bitcast.15), kind=kOutput, calls=%fused_computation.90 | convolution fusion | flops 2952790016 | bytes 10747904 | tf_op jit(solution)/shard_map/dot_general | solution.py:125
  181.8 5.1 %add_convert_fusion = bf16[512,2048]{1,0:T(8,128)(2,1)} fusion(f32[512,2048]{1,0:T(8,128)S(1)} %fusion.3, bf16[1,704,2048]{2,1,0:T(8,128)(2,1)} %collective-permute-done.1, f32[512,1408]{1,0:T(8,128)S(1)} %fusion.44), kind=kOutput, calls=%fused_computation.6 | convolution fusion | flops 1480654848 | bytes 12320768 | tf_op jit(solution)/shard_map/dot_general | solution.py:129
  187.0 0.1 reshape.172
  187.2 32.1 %reduce-scatter.8.cloned.1.call-done = bf16[128,2048]{1,0:T(8,128)(2,1)} async-done(((bf16[512,2048]{1,0:T(8,128)(2,1)}), bf16[128,2048]{1,0:T(8,128)(2,1)}) %reduce-scatter.8.cloned.1.call-update) | async-done | bytes 524304 | tf_op jit(solution)/shard_map/reduce_scatter | solution.py:134
  219.3 2.0 all_to_all.35
  221.4 10.1 %all-to-all-start.3 = ((bf16[32,4,2048]{2,1,0:T(4,128)(2,1)}), bf16[32,4,2048]{2,1,0:T(4,128)(2,1)S(1)}, u32[]{:S(2)}, u32[]{:S(2)}) async-start(bf16[32,4,2048]{2,1,0:T(4,128)(2,1)} %all_to_all.35), calls=%async_computation.6 | async-start | bytes 1048576 | tf_op jit(solution)/shard_map/all_to_all | solution.py:135
  231.5 0.2 fusion.25
  231.7 1.0 gather_fusion
  232.7 0.1 reshape.175
  233.1 15.6 %all-to-all-done.3 = bf16[32,4,2048]{2,1,0:T(4,128)(2,1)S(1)} async-done(((bf16[32,4,2048]{2,1,0:T(4,128)(2,1)}), bf16[32,4,2048]{2,1,0:T(4,128)(2,1)S(1)}, u32[]{:S(2)}, u32[]{:S(2)}) %all-to-all-start.3) | async-done | bytes 524320 | tf_op jit(solution)/shard_map/all_to_all | solution.py:135
  248.7 0.1 all_to_all.37
  248.8 0.5 multiply_reduce_fusion
  249.4 0.8 multiply_convert_fusion
  (56 shorter events, 1.1 us)
Async XLA Ops:
  7.2 1.7 copy-start
  7.2 77.0 %reduce-scatter.4.cloned.1.call-start = ((), (), s32[]{:S(2)}) async-start(), calls=%async_computation.7 | async-start | bytes 5308416 | tf_op jit(solution)/shard_map/reduce_scatter | solution.py:65
  9.6 2.9 %copy-start.10 = (bf16[8,64,2048]{2,1,0:T(8,128)(2,1)S(1)}, bf16[8,64,2048]{2,1,0:T(8,128)(2,1)}, u32[]{:S(2)}) copy-start(bf16[8,64,2048]{2,1,0:T(8,128)(2,1)} %param.18) | copy-start | bytes 6291460
  11.2 1.4 copy-start.1
  71.4 12.5 %copy-start.4 = (s32[32]{0:T(128)S(1)}, s32[32]{0:T(128)}, u32[]{:S(2)}) copy-start(s32[32]{0:T(128)} %param.23) | copy-start | bytes 388
  71.4 12.6 %copy-start.3 = (s32[64,2]{0,1:T(2,128)S(1)}, s32[64,2]{0,1:T(2,128)}, u32[]{:S(2)}) copy-start(s32[64,2]{0,1:T(2,128)} %param.21) | copy-start | bytes 1540
  71.4 13.3 %copy-start.7 = (s32[64,2]{0,1:T(2,128)S(1)}, s32[64,2]{0,1:T(2,128)}, u32[]{:S(2)}) copy-start(s32[64,2]{0,1:T(2,128)} %param.22) | copy-start | bytes 1540
  71.5 14.8 %copy-start.5 = (bf16[2048]{0:T(1024)(128)(2,1)S(1)}, bf16[2048]{0:T(1024)(128)(2,1)}, u32[]{:S(2)}) copy-start(bf16[2048]{0:T(1024)(128)(2,1)} %param.19) | copy-start | bytes 12292
  71.5 14.8 %copy-start.8 = (s32[32]{0:T(128)S(1)}, s32[32]{0:T(128)}, u32[]{:S(2)}) copy-start(s32[32]{0:T(128)} %param.24) | copy-start | bytes 388
  75.2 36.5 %copy-start.2 = (bf16[64,2048]{1,0:T(8,128)(2,1)S(1)}, bf16[64,2048]{1,0:T(8,128)(2,1)}, u32[]{:S(2)}) copy-start(bf16[64,2048]{1,0:T(8,128)(2,1)} %param.14) | copy-start | bytes 786436
  75.2 32.0 %all-to-all-start.1 = ((bf16[8,64,896]{2,1,0:T(8,128)(2,1)}), bf16[8,64,896]{2,1,0:T(8,128)(2,1)S(1)}, u32[]{:S(2)}, u32[]{:S(2)}) async-start(bf16[8,64,896]{2,1,0:T(8,128)(2,1)} %bitcast.11), calls=%async_computation.3 | async-start | bytes 1835008 | tf_op jit(solution)/shard_map/all_to_all | solution.py:71
  83.9 26.9 %reduce-scatter.6.cloned.1.call-start = ((), (), s32[]{:S(2)}) async-start(), calls=%async_computation.8 | async-start | bytes 737280 | tf_op jit(solution)/shard_map/reduce_scatter | solution.py:66
  83.9 91.9 %collective-permute-start = (bf16[1,2048,2,704]{1,3,2,0:T(8,128)(2,1)}, bf16[1,2048,2,704]{1,3,2,0:T(8,128)(2,1)}, u32[]{:S(2)}, u32[]{:S(2)}) collective-permute-start(bf16[1,2048,2,704]{1,3,2,0:T(8,128)(2,1)} %param.25), channel_id=1, source_target_pairs={{0,32},{32,0},{1,33},{33,1},{2,34},{34,2},{3,35},{35,3},{4,36},{36... | collective-permute-start | bytes 17301512 | tf_op jit(solution)/shard_map/ppermute | solution.py:120
  84.7 82.7 %all-gather.2.cloned.1.call-start = ((), (), s32[]{:S(2)}) async-start(), calls=%async_computation.9 | async-start | bytes 2621440 | tf_op jit(solution)/shard_map/all_gather | solution.py:118
  137.5 81.9 %reduce-scatter.8.cloned.1.call-start = ((), (), s32[]{:S(2)}) async-start(), calls=%async_computation.10 | async-start | bytes 2621440 | tf_op jit(solution)/shard_map/reduce_scatter | solution.py:134
  137.5 44.3 %collective-permute-start.1 = (bf16[1,704,2048]{2,1,0:T(8,128)(2,1)}, bf16[1,704,2048]{2,1,0:T(8,128)(2,1)}, u32[]{:S(2)}, u32[]{:S(2)}) collective-permute-start(bf16[1,704,2048]{2,1,0:T(8,128)(2,1)} %param.26), channel_id=1, source_target_pairs={{0,32},{32,0},{1,33},{33,1},{2,34},{34,2},{3,35},{35,3},{4,36},{36... | collective-permute-start | bytes 8650760 | tf_op jit(solution)/shard_map/ppermute | solution.py:121
  167.3 6.6 %copy-start.9 = (bf16[1,704,2048]{2,1,0:T(8,128)(2,1)S(1)}, bf16[1,704,2048]{2,1,0:T(8,128)(2,1)}, u32[]{:S(2)}) copy-start(bf16[1,704,2048]{2,1,0:T(8,128)(2,1)} %param.26) | copy-start | bytes 8650756
  174.0 1.9 copy-start.11
  181.7 5.4 %copy-start.6 = (bf16[2048]{0:T(1024)(128)(2,1)S(1)}, bf16[2048]{0:T(1024)(128)(2,1)}, u32[]{:S(2)}) copy-start(bf16[2048]{0:T(1024)(128)(2,1)} %param.27) | copy-start | bytes 12292
  186.9 44.6 %copy-start.12 = (bf16[2048,8]{0,1:T(8,128)(2,1)S(1)}, bf16[2048,8]{0,1:T(8,128)(2,1)}, u32[]{:S(2)}) copy-start(bf16[2048,8]{0,1:T(8,128)(2,1)} %param.20) | copy-start | bytes 98308
  221.4 27.4 %all-to-all-start.3 = ((bf16[32,4,2048]{2,1,0:T(4,128)(2,1)}), bf16[32,4,2048]{2,1,0:T(4,128)(2,1)S(1)}, u32[]{:S(2)}, u32[]{:S(2)}) async-start(bf16[32,4,2048]{2,1,0:T(4,128)(2,1)} %all_to_all.35), calls=%async_computation.6 | async-start | bytes 1048576 | tf_op jit(solution)/shard_map/all_to_all | solution.py:135
Sparse Core Ops, SparseCore 0:
  17.4 61.0 reduce-scatter.3
  87.3 23.4 reduce-scatter.5
  137.6 29.7 all-gather.1
  187.0 32.2 reduce-scatter.7

commit v12 on v11

--- a/solution.py
+++ b/solution.py
@@ -7,7 +7,7 @@
 TENSOR = ("tz", "ty")
 EXPERT = ("ex", "ec")
 ALL = ("ex", "ec", "tz", "ty")
-Z_SHARE = 9
+Z_SHARE = 10
 
 
 norm_eps = 1e-06

time: 257 us -> 271 us (1.054)
  waiting for transfers between devices: 102 us -> 122 us
  blocking collectives: 71.5 us -> 66.4 us
    reduce_scatter x1, waiting for transfers between devices: 3.46 us -> 21.4 us  [per_device(): lax.psum_scatter(z_first, 'ty', scatter_dimension=0, tiled=True)]
    reduce_scatter x1, waiting for transfers between devices: 0.01 us -> 13.8 us  [per_device(): lax.psum_scatter(z_first.astype(jnp.bfloat16), 'tz', scatter_dimension=0,...]
    all_to_all x1, waiting for transfers between devices: 20.8 us -> 9.2 us  [per_device(): lax.all_to_all(y_first.astype(jnp.bfloat16), 'tz', split_axis=0, concat_a...]
    all_to_all x1, blocking collectives: 47.6 us -> 41.9 us  [per_device(): lax.all_to_all(y_first.astype(jnp.bfloat16), 'ty', split_axis=0, concat_a...]
  transfers between devices with their start and end apart: 8 -> 8, of which waited for: 5 -> 6; matrix products, arithmetic and copies ran while one was open for 12% -> 11% of each run, Pallas kernels for 0% -> 0%
where the time goes in v12:
time: 271 us; the launch traced here: 270 us
  waiting for transfers between devices  122 us (45%)
  blocking collectives  66.4 us (25%)
  matrix products  30.5 us (11%)
  starting transfers between devices  19.2 us (7%)
  between operations  14.1 us (5%)
  local copies, waits for them, and re-layouts  10.6 us (4%)
  other arithmetic  7.76 us (3%)
    all_to_all x1, blocking collectives, per_device(): lax.all_to_all(y_first.astype(jnp.bfloat16), 'ty', split_axis=0, concat_a...  41.9 us
    reduce_scatter x1, waiting for transfers between devices, per_device(): lax.psum_scatter(down.astype(jnp.bfloat16), 'ex', scatter_dimension=0, ti...  32.1 us
    all_gather x1, waiting for transfers between devices, per_device(): arrived = lax.all_gather(exchanged, 'ex', axis=0, tiled=True)  29.5 us
    all_to_all x1, blocking collectives, per_device(): lax.all_to_all(send_rows, TENSOR, split_axis=0, concat_axis=0, tiled=True)  24.4 us
    reduce_scatter x1, waiting for transfers between devices, per_device(): lax.psum_scatter(z_first, 'ty', scatter_dimension=0, tiled=True)  21.4 us
    all_to_all x1, waiting for transfers between devices, per_device(): lax.all_to_all(summed, TENSOR, split_axis=0, concat_axis=0, tiled=True)  15.6 us
    reduce_scatter x1, waiting for transfers between devices, per_device(): lax.psum_scatter(z_first.astype(jnp.bfloat16), 'tz', scatter_dimension=0,...  13.8 us
    dot_general x2, matrix products, expert_part(): jnp.dot(arrived, gate_up.reshape(model_width, 2 * hidden_units), preferre...  12.4 us
  transfers between devices with their start and end apart: 8, of which 6 were waited for; matrix products, arithmetic and copies ran while one was open for 11% of the time, Pallas kernels for 0%

profile of v12, /device:TPU:32, one launch (start us, length us, event | category | flops | bytes accessed | tf_op | source)
XLA Modules:
  0.0 270.3 jit_solution(10257468709735269902)
XLA Ops:
  7.2 0.8 fusion.42
  8.1 0.8 broadcast_subtract_fusion
  8.9 0.7 fusion.20
  9.7 1.5 fusion.1
  11.2 1.3 copy-done.1
  12.5 4.8 %convolution_convert_fusion = bf16[2048,1280]{1,0:T(8,128)(2,1)} fusion(bf16[2048,512]{0,1:T(8,128)(2,1)S(1)} %fusion.1, bf16[512,2048]{1,0:T(8,128)(2,1)S(1)} %bitcast.54), kind=kOutput, calls=%fused_computation.1 | convolution fusion | flops 2686976000 | bytes 8650752 | tf_op jit(solution)/shard_map/dot_general | solution.py:64
  17.3 2.9 %copy.56 = bf16[2048,512]{1,0:T(8,128)(2,1)S(1)} copy(bf16[2048,512]{0,1:T(8,128)(2,1)} %copy-done.1) | data formatting | bytes 4194304 | tf_op jit(solution)/shard_map/convert_element_type | solution.py:59
  20.2 0.1 copy.57
  20.4 2.9 %convolution_convert_fusion.1 = bf16[2048,768]{1,0:T(8,128)(2,1)S(1)} fusion(bf16[2048,512]{1,0:T(8,128)(2,1)S(1)} %bitcast.47, bf16[512,2048]{1,0:T(8,128)(2,1)} %bitcast.53), kind=kOutput, calls=%fused_computation.7 | convolution fusion | flops 1612185600 | bytes 6029312 | tf_op jit(solution)/shard_map/dot_general | solution.py:68
  23.3 41.9 %all_to_all.42 = bf16[4,512,768]{2,1,0:T(8,128)(2,1)} all-to-all(bf16[4,512,768]{2,1,0:T(8,128)(2,1)S(1)} %bitcast.46), channel_id=1, replica_groups=mesh['ex'=4,'ec'=2,'tz'=8,'ty'=4] {'ty'}, dimensions={0} | all-to-all | bytes 6291456 | tf_op jit(solution)/shard_map/all_to_all | solution.py:69
  65.3 3.5 %reduce_sum.114 = bf16[512,768]{1,0:T(8,128)(2,1)} reduce(bf16[4,512,768]{2,1,0:T(8,128)(2,1)} %all_to_all.42, bf16[]{:T(256)} %constant.108.clone.1), dimensions={0}, to_apply=%region_2.3 | reduce | flops 1179648 | bytes 3932162 | tf_op jit(solution)/shard_map/reduce_sum | solution.py:70
  68.8 8.7 %all-to-all-start.1 = ((bf16[8,64,768]{2,1,0:T(8,128)(2,1)}), bf16[8,64,768]{2,1,0:T(8,128)(2,1)S(1)}, u32[]{:S(2)}, u32[]{:S(2)}) async-start(bf16[8,64,768]{2,1,0:T(8,128)(2,1)} %bitcast.11), calls=%async_computation.3 | async-start | bytes 1572864 | tf_op jit(solution)/shard_map/all_to_all | solution.py:71
  77.5 0.1 convert_reduce_fusion.2
  77.6 13.8 %reduce-scatter.4.cloned.1.call-done = bf16[256,1280]{1,0:T(8,128)(2,1)} async-done(((bf16[2048,1280]{1,0:T(8,128)(2,1)}), bf16[256,1280]{1,0:T(8,128)(2,1)}) %reduce-scatter.4.cloned.1.call-update) | async-done | bytes 655376 | tf_op jit(solution)/shard_map/reduce_scatter | solution.py:65
  91.7 0.1 and_select_fusion.1
  91.9 0.1 eq.202
  92.1 0.1 eq.188
  92.2 0.2 convert_reduce_fusion.1
  92.4 0.1 fusion.28
  92.5 0.2 reduce_window_sum.11
  92.7 0.2 select_reduce_fusion.1
  92.9 0.1 reshape.166
  93.3 9.2 %all-to-all-done.1 = bf16[8,64,768]{2,1,0:T(8,128)(2,1)S(1)} async-done(((bf16[8,64,768]{2,1,0:T(8,128)(2,1)}), bf16[8,64,768]{2,1,0:T(8,128)(2,1)S(1)}, u32[]{:S(2)}, u32[]{:S(2)}) %all-to-all-start.1) | async-done | bytes 786464 | tf_op jit(solution)/shard_map/all_to_all | solution.py:71
  102.5 0.1 convert_reduce_fusion
  102.6 21.4 %reduce-scatter.6.cloned.1.call-done = bf16[64,1280]{1,0:T(8,128)(2,1)} async-done(((bf16[256,1280]{1,0:T(8,128)(2,1)}), bf16[64,1280]{1,0:T(8,128)(2,1)}) %reduce-scatter.6.cloned.1.call-update) | async-done | bytes 163856 | tf_op jit(solution)/shard_map/reduce_scatter | solution.py:66
  124.0 0.9 convert_element_type.77
  124.9 0.2 fusion.13
  125.1 0.4 convolution_convert_fusion.2
  125.5 0.2 all_to_all.32
  125.7 24.4 %all_to_all.43 = bf16[32,4,2048]{2,1,0:T(4,128)(2,1)S(1)} all-to-all(bf16[32,4,2048]{2,1,0:T(4,128)(2,1)S(1)} %all_to_all.32), channel_id=1, replica_groups=mesh['ex'=4,'ec'=2,'tz'=8,'ty'=4] {'tz','ty'}, dimensions={0} | all-to-all | bytes 1048576 | tf_op jit(solution)/shard_map/all_to_all | solution.py:117
  150.1 0.9 all_to_all.34
  151.1 0.3 collective-permute-start.1
  151.4 29.5 %all-gather.2.cloned.1.call-done = bf16[512,2048]{1,0:T(8,128)(2,1)} async-done(((bf16[128,2048]{1,0:T(8,128)(2,1)}), bf16[512,2048]{1,0:T(8,128)(2,1)}) %all-gather.2.cloned.1.call-update) | async-done | bytes 2097168 | tf_op jit(solution)/shard_map/all_gather | solution.py:118
  180.9 6.6 %fusion.43 = f32[512,1408]{1,0:T(8,128)S(1)} fusion(bf16[512,2048]{1,0:T(8,128)(2,1)} %all-gather.2.cloned.1.call-done, bf16[2048,1408]{0,1:T(8,128)(2,1)} %bitcast.52), kind=kOutput, calls=%fused_computation.89 | convolution fusion | flops 2952790016 | bytes 10747904 | tf_op jit(solution)/shard_map/dot_general | solution.py:125
  187.6 1.9 fusion.3
  189.5 5.8 %fusion.44 = f32[512,1408]{1,0:T(8,128)S(1)} fusion(bf16[512,2048]{1,0:T(8,128)(2,1)S(1)} %copy-done.11, bf16[2048,1408]{0,1:T(8,128)(2,1)} %bitcast.15), kind=kOutput, calls=%fused_computation.90 | convolution fusion | flops 2952790016 | bytes 10747904 | tf_op jit(solution)/shard_map/dot_general | solution.py:125
  195.4 5.1 %add_convert_fusion = bf16[512,2048]{1,0:T(8,128)(2,1)} fusion(f32[512,2048]{1,0:T(8,128)S(1)} %fusion.3, bf16[1,704,2048]{2,1,0:T(8,128)(2,1)} %collective-permute-done.1, f32[512,1408]{1,0:T(8,128)S(1)} %fusion.44), kind=kOutput, calls=%fused_computation.6 | convolution fusion | flops 1480654848 | bytes 12320768 | tf_op jit(solution)/shard_map/dot_general | solution.py:129
  200.6 0.1 reshape.172
  200.8 32.1 %reduce-scatter.8.cloned.1.call-done = bf16[128,2048]{1,0:T(8,128)(2,1)} async-done(((bf16[512,2048]{1,0:T(8,128)(2,1)}), bf16[128,2048]{1,0:T(8,128)(2,1)}) %reduce-scatter.8.cloned.1.call-update) | async-done | bytes 524304 | tf_op jit(solution)/shard_map/reduce_scatter | solution.py:134
  232.9 2.0 all_to_all.35
  235.0 10.1 %all-to-all-start.3 = ((bf16[32,4,2048]{2,1,0:T(4,128)(2,1)}), bf16[32,4,2048]{2,1,0:T(4,128)(2,1)S(1)}, u32[]{:S(2)}, u32[]{:S(2)}) async-start(bf16[32,4,2048]{2,1,0:T(4,128)(2,1)} %all_to_all.35), calls=%async_computation.6 | async-start | bytes 1048576 | tf_op jit(solution)/shard_map/all_to_all | solution.py:135
  245.1 0.2 fusion.25
  245.3 1.0 gather_fusion
  246.3 0.1 reshape.175
  246.7 15.6 %all-to-all-done.3 = bf16[32,4,2048]{2,1,0:T(4,128)(2,1)S(1)} async-done(((bf16[32,4,2048]{2,1,0:T(4,128)(2,1)}), bf16[32,4,2048]{2,1,0:T(4,128)(2,1)S(1)}, u32[]{:S(2)}, u32[]{:S(2)}) %all-to-all-start.3) | async-done | bytes 524320 | tf_op jit(solution)/shard_map/all_to_all | solution.py:135
  262.3 0.1 all_to_all.37
  262.4 0.5 multiply_reduce_fusion
  262.9 0.8 multiply_convert_fusion
  (56 shorter events, 1.1 us)
Async XLA Ops:
  7.2 1.7 copy-start
  7.2 84.3 %reduce-scatter.4.cloned.1.call-start = ((), (), s32[]{:S(2)}) async-start(), calls=%async_computation.7 | async-start | bytes 5898240 | tf_op jit(solution)/shard_map/reduce_scatter | solution.py:65
  9.6 2.9 %copy-start.10 = (bf16[8,64,2048]{2,1,0:T(8,128)(2,1)S(1)}, bf16[8,64,2048]{2,1,0:T(8,128)(2,1)}, u32[]{:S(2)}) copy-start(bf16[8,64,2048]{2,1,0:T(8,128)(2,1)} %param.18) | copy-start | bytes 6291460
  11.2 1.4 copy-start.1
  65.2 12.3 %copy-start.4 = (s32[32]{0:T(128)S(1)}, s32[32]{0:T(128)}, u32[]{:S(2)}) copy-start(s32[32]{0:T(128)} %param.23) | copy-start | bytes 388
  65.2 26.3 %copy-start.3 = (s32[64,2]{0,1:T(2,128)S(1)}, s32[64,2]{0,1:T(2,128)}, u32[]{:S(2)}) copy-start(s32[64,2]{0,1:T(2,128)} %param.21) | copy-start | bytes 1540
  65.2 26.5 %copy-start.7 = (s32[64,2]{0,1:T(2,128)S(1)}, s32[64,2]{0,1:T(2,128)}, u32[]{:S(2)}) copy-start(s32[64,2]{0,1:T(2,128)} %param.22) | copy-start | bytes 1540
  65.2 27.8 %copy-start.5 = (bf16[2048]{0:T(1024)(128)(2,1)S(1)}, bf16[2048]{0:T(1024)(128)(2,1)}, u32[]{:S(2)}) copy-start(bf16[2048]{0:T(1024)(128)(2,1)} %param.19) | copy-start | bytes 12292
  65.2 27.8 %copy-start.8 = (s32[32]{0:T(128)S(1)}, s32[32]{0:T(128)}, u32[]{:S(2)}) copy-start(s32[32]{0:T(128)} %param.24) | copy-start | bytes 388
  68.8 56.1 %copy-start.2 = (bf16[64,2048]{1,0:T(8,128)(2,1)S(1)}, bf16[64,2048]{1,0:T(8,128)(2,1)}, u32[]{:S(2)}) copy-start(bf16[64,2048]{1,0:T(8,128)(2,1)} %param.14) | copy-start | bytes 786436
  68.8 33.7 %all-to-all-start.1 = ((bf16[8,64,768]{2,1,0:T(8,128)(2,1)}), bf16[8,64,768]{2,1,0:T(8,128)(2,1)S(1)}, u32[]{:S(2)}, u32[]{:S(2)}) async-start(bf16[8,64,768]{2,1,0:T(8,128)(2,1)} %bitcast.11), calls=%async_computation.3 | async-start | bytes 1572864 | tf_op jit(solution)/shard_map/all_to_all | solution.py:71
  77.5 46.5 %reduce-scatter.6.cloned.1.call-start = ((), (), s32[]{:S(2)}) async-start(), calls=%async_computation.8 | async-start | bytes 819200 | tf_op jit(solution)/shard_map/reduce_scatter | solution.py:66
  77.5 112.0 %collective-permute-start = (bf16[1,2048,2,704]{1,3,2,0:T(8,128)(2,1)}, bf16[1,2048,2,704]{1,3,2,0:T(8,128)(2,1)}, u32[]{:S(2)}, u32[]{:S(2)}) collective-permute-start(bf16[1,2048,2,704]{1,3,2,0:T(8,128)(2,1)} %param.25), channel_id=1, source_target_pairs={{0,32},{32,0},{1,33},{33,1},{2,34},{34,2},{3,35},{35,3},{4,36},{36... | collective-permute-start | bytes 17301512 | tf_op jit(solution)/shard_map/ppermute | solution.py:120
  91.5 89.5 %all-gather.2.cloned.1.call-start = ((), (), s32[]{:S(2)}) async-start(), calls=%async_computation.9 | async-start | bytes 2621440 | tf_op jit(solution)/shard_map/all_gather | solution.py:118
  151.1 81.8 %reduce-scatter.8.cloned.1.call-start = ((), (), s32[]{:S(2)}) async-start(), calls=%async_computation.10 | async-start | bytes 2621440 | tf_op jit(solution)/shard_map/reduce_scatter | solution.py:134
  151.1 44.2 %collective-permute-start.1 = (bf16[1,704,2048]{2,1,0:T(8,128)(2,1)}, bf16[1,704,2048]{2,1,0:T(8,128)(2,1)}, u32[]{:S(2)}, u32[]{:S(2)}) collective-permute-start(bf16[1,704,2048]{2,1,0:T(8,128)(2,1)} %param.26), channel_id=1, source_target_pairs={{0,32},{32,0},{1,33},{33,1},{2,34},{34,2},{3,35},{35,3},{4,36},{36... | collective-permute-start | bytes 8650760 | tf_op jit(solution)/shard_map/ppermute | solution.py:121
  180.9 6.6 %copy-start.9 = (bf16[1,704,2048]{2,1,0:T(8,128)(2,1)S(1)}, bf16[1,704,2048]{2,1,0:T(8,128)(2,1)}, u32[]{:S(2)}) copy-start(bf16[1,704,2048]{2,1,0:T(8,128)(2,1)} %param.26) | copy-start | bytes 8650756
  187.6 1.9 copy-start.11
  195.3 5.4 %copy-start.6 = (bf16[2048]{0:T(1024)(128)(2,1)S(1)}, bf16[2048]{0:T(1024)(128)(2,1)}, u32[]{:S(2)}) copy-start(bf16[2048]{0:T(1024)(128)(2,1)} %param.27) | copy-start | bytes 12292
  200.5 44.6 %copy-start.12 = (bf16[2048,8]{0,1:T(8,128)(2,1)S(1)}, bf16[2048,8]{0,1:T(8,128)(2,1)}, u32[]{:S(2)}) copy-start(bf16[2048,8]{0,1:T(8,128)(2,1)} %param.20) | copy-start | bytes 98308
  235.0 27.3 %all-to-all-start.3 = ((bf16[32,4,2048]{2,1,0:T(4,128)(2,1)}), bf16[32,4,2048]{2,1,0:T(4,128)(2,1)S(1)}, u32[]{:S(2)}, u32[]{:S(2)}) async-start(bf16[32,4,2048]{2,1,0:T(4,128)(2,1)} %all_to_all.35), calls=%async_computation.6 | async-start | bytes 1048576 | tf_op jit(solution)/shard_map/all_to_all | solution.py:135
Sparse Core Ops, SparseCore 0:
  17.5 73.9 reduce-scatter.3
  94.0 29.9 reduce-scatter.5
  151.2 29.6 all-gather.1
  200.6 32.2 reduce-scatter.7
